TPU v7x, 32 devices: a whole 2x2x4 slice. The times are simulated.
32 devices in a mesh: led: 4 (over y, x), row: 8 (over z, core).
Axes of the slice: x: 2, y: 2, z: 4, core: 2. Of those that a mesh axis runs over, the one named last changes fastest.
Arguments:
- spectrum: float32 [2, 4096, 4096], P(None, 'led', 'row'), may hold values from -6 to 6
- amplitudes: float32 [4, 2048, 2048], P('led', 'row'), may hold values from 0.2 to 3
- offsets: int32 [4, 2], replicated, may hold values from 0 to 2048
- coeffs: float32 [6], replicated, may hold values from -2.5 to 2.5
Outputs:
- updated: float32 [2, 4096, 4096], P(None, 'led', 'row')
All inputs are finite; a program needn't handle non-finite values.
Results may differ from a plain program's by a relative error of at most 0.0001.
Values sent between devices are 32-bit elements; how exact they have to be, the bound alone decides.
No kernel may reach another device: no remote copies, remote signals or barrier semaphores. Data moves between devices by JAX's collectives and lax.ppermute only.
A program may use at most 128 MiB of HBM per device.

v0:
```python
import math

import jax
import jax.numpy as jnp
from jax import lax
from jax.sharding import PartitionSpec as P

SOFTENING = 0.1
HIGHEST_PRECISION = lax.Precision.HIGHEST


def pupil_at(down_index, across_index, coeffs, centre):
    offset_down = down_index - centre
    offset_across = across_index - centre
    inside = offset_down * offset_down + offset_across * offset_across < centre * centre
    upper_norm = offset_down.astype(jnp.float32) * (1.0 / centre)
    lateral = offset_across.astype(jnp.float32) * (1.0 / centre)
    radial = upper_norm * upper_norm + lateral * lateral
    phases = (
        coeffs[0] * (2.0 * radial - 1.0)
        + coeffs[1] * (upper_norm * upper_norm - lateral * lateral)
        + coeffs[2] * (2.0 * upper_norm * lateral)
        + (3.0 * radial - 2.0) * (coeffs[3] * upper_norm + coeffs[4] * lateral)
        + coeffs[5] * (6.0 * radial * radial - 6.0 * radial + 1.0)
    )
    weight = jnp.where(inside, 1.0, 0.0).astype(jnp.float32)
    return (weight * jnp.cos(phases), weight * jnp.sin(phases))


def tables(outer_size, inner_size, direction):
    length = outer_size * inner_size
    angle_step = direction * 2.0 * math.pi / length
    first_index = jnp.arange(outer_size, dtype=jnp.int32)
    grid_first = first_index[:, None] * first_index[None, :] * inner_size % length
    angles_first = grid_first.astype(jnp.float32) * angle_step
    index_k = jnp.arange(outer_size, dtype=jnp.int32)[:, None, None]
    index_r = jnp.arange(inner_size, dtype=jnp.int32)[None, :, None]
    index_j = jnp.arange(inner_size, dtype=jnp.int32)[None, None, :]
    grid_second = index_r * (index_k + outer_size * index_j) % length
    angles_second = grid_second.astype(jnp.float32) * angle_step
    return (
        jnp.cos(angles_first),
        jnp.sin(angles_first),
        jnp.cos(angles_second),
        jnp.sin(angles_second),
    )


def transform(paired, inputs, middle, output, outer_size, inner_size, direction):
    first_re, first_im, second_re, second_im = tables(outer_size, inner_size, direction)
    scaling = 1.0 / math.sqrt(outer_size * inner_size)
    first_table = jnp.stack([jnp.stack([first_re, first_im]), jnp.stack([-first_im, first_re])])
    second_table = (
        jnp.stack([jnp.stack([second_re, second_im]), jnp.stack([-second_im, second_re])]) * scaling
    )
    middle_pair = jnp.einsum(
        "p" + inputs + ",pqtk->q" + middle, paired, first_table, precision=HIGHEST_PRECISION
    )
    return jnp.einsum(
        "p" + middle + ",pqkrj->q" + output, middle_pair, second_table, precision=HIGHEST_PRECISION
    )


def correct(field_re, field_im, measured):
    magnitude = jnp.sqrt(field_re * field_re + field_im * field_im + SOFTENING)
    factor = measured / magnitude
    return (field_re * factor - field_re, field_im * factor - field_im)


def on_device(spectrum, amplitudes, offsets, coeffs):
    led_count = lax.axis_size("led")
    row_count = lax.axis_size("row")
    led_index = lax.axis_index("led")
    row_index = lax.axis_index("row")
    size_rows = spectrum.shape[1]
    size_cols = spectrum.shape[2]
    window = amplitudes.shape[2]
    centre = window // 2
    block_rows = window // row_count
    outer_rows = window // led_count
    outer_cols = window // row_count
    row_shift = offsets[led_index, 0]
    col_shift = offsets[led_index, 1]
    measured = amplitudes[0]
    shape_cols = (2, block_rows, outer_cols, row_count)
    region = lax.all_gather(spectrum, "led", axis=1, tiled=True)
    band_rows = lax.dynamic_slice_in_dim(region, row_shift, window, 1)
    row_ids = jnp.arange(window, dtype=jnp.int32)[:, None]
    col_ids = (row_index * size_cols + jnp.arange(size_cols, dtype=jnp.int32))[None, :] - col_shift
    pupil_re, pupil_im = pupil_at(row_ids, col_ids, coeffs, centre)
    lit_re = pupil_re * band_rows[0] - pupil_im * band_rows[1]
    lit_im = pupil_re * band_rows[1] + pupil_im * band_rows[0]
    shape_rows = (2, outer_rows, led_count, size_cols)
    half = transform(
        jnp.stack([lit_re, lit_im]).reshape(shape_rows),
        "trc",
        "krc",
        "jkc",
        outer_rows,
        led_count,
        1.0,
    )
    stacked = half.reshape(2, window, size_cols)
    spread = lax.all_to_all(stacked, "row", split_axis=1, concat_axis=2, tiled=True)
    window_part = lax.dynamic_slice_in_dim(spread, col_shift, window, 2)
    field = transform(
        window_part.reshape(shape_cols), "ytr", "ykr", "yjk", outer_cols, row_count, 1.0
    )
    field = field.reshape(2, block_rows, window)
    diff_re, diff_im = correct(field[0], field[1], measured)
    back = transform(
        jnp.stack([diff_re, diff_im]).reshape(shape_cols),
        "ytr",
        "ykr",
        "yjk",
        outer_cols,
        row_count,
        -1.0,
    )
    padded = jnp.zeros((2, block_rows, row_count * size_cols), jnp.float32)
    padded = lax.dynamic_update_slice_in_dim(
        padded, back.reshape(2, block_rows, window), col_shift, 2
    )
    gathered_cols = lax.all_to_all(padded, "row", split_axis=2, concat_axis=1, tiled=True)
    spec = transform(
        gathered_cols.reshape(shape_rows), "trc", "krc", "jkc", outer_rows, led_count, -1.0
    ).reshape(2, window, size_cols)
    upd_re = pupil_re * spec[0] + pupil_im * spec[1]
    upd_im = pupil_re * spec[1] - pupil_im * spec[0]
    embedded = jnp.zeros((2, size_rows * led_count, size_cols), jnp.float32)
    embedded = lax.dynamic_update_slice_in_dim(embedded, jnp.stack([upd_re, upd_im]), row_shift, 1)
    summed = lax.psum_scatter(embedded, "led", scatter_dimension=1, tiled=True)
    return spectrum + summed


def solution(mesh):
    return jax.shard_map(
        on_device,
        mesh=mesh,
        in_specs=(P(None, "led", "row"), P("led", "row", None), P(), P()),
        out_specs=P(None, "led", "row"),
        check_vma=False,
    )
```

profile of v0, /device:TPU:0, one launch (start us, length us, event | category | flops | bytes accessed | tf_op | source)
XLA Modules:
  0.0 1087.2 jit_solution(2746678404710610124)
XLA Ops:
  27.8 141.4 %all-gather.2.cloned.1.call-done = f32[2,4096,512]{2,1,0:T(8,128)} async-done(((f32[2,1024,512]{2,1,0:T(8,128)}), f32[2,4096,512]{2,1,0:T(8,128)}) %all-gather.2.cloned.1.call-update) | async-done | bytes 16777232 | tf_op jit(solution)/shard_map/all_gather | solution.py:86
  169.3 26.9 %multiply_subtract_fusion = (f32[1,2048,512]{2,1,0:T(8,128)}, f32[1,2048,512]{2,1,0:T(8,128)}) fusion(f32[2,4096,512]{2,1,0:T(8,128)} %all-gather.2.cloned.1.call-done, s32[]{:T(128)S(6)} %select_n.238, s32[]{:T(128)S(6)} %add.718, f32[]{:T(128)} %bitcast.6, f32[512]{0:T(512)S(1)} %get-tuple-element.53, f32[2048]{0:T(1024)S(1)} %get-tuple-element.58, ...), kind=kLoop, calls=%fused_computation.55 | loop fusion | flops 33554432 | bytes 16818200 | tf_op jit(solution)/shard_map/sub | solution.py:91
  196.1 7.9 stack.215
  209.6 7.7 stack.216
  221.4 28.3 %fusion.46 = f32[2,512,4,512,1]{3,1,2,0,4:T(8,128)} fusion(f32[1,512,4,512]{3,1,0,2:T(8,128)S(1)} %copy.144, f32[1,512,4,512]{3,1,0,2:T(8,128)S(1)} %copy-done.3, f32[1,2,512,512]{2,3,0,1:T(8,128)S(1)} %copy-done.4, f32[1,2,512,512]{2,3,0,1:T(8,128)S(1)} %get-tuple-element.17), kind=kOutput, calls=%fused_computation.58 | convolution fusion | flops 25772949504 | bytes 20971520 | tf_op jit(solution)/shard_map/ptrc,pqtk->qkrc/dot_general | solution.py:56
  249.7 32.7 %fusion.11 = f32[2,4,512,512]{3,1,0,2:T(4,128)S(1)} fusion(f32[2,2,512,4,4]{3,4,0,1,2:T(4,128)} %copy.145, f32[2,512,4,512,1]{3,1,2,0,4:T(8,128)} %fusion.46), kind=kOutput, calls=%fused_computation.19 | convolution fusion | flops 201326592 | bytes 16908288 | tf_op jit(solution)/shard_map/pkrc,pqkrj->qjkc/dot_general | solution.py:59
  287.2 16.5 %copy.148 = f32[2,2048,512]{2,0,1:T(2,128)} copy(f32[2,2048,512]{2,1,0:T(8,128)S(1)} %bitcast.186) | data formatting | bytes 16777216 | tf_op jit(solution)/shard_map/reshape | solution.py:103
  327.6 165.1 %all-to-all-done = f32[2,2048,512]{2,0,1:T(2,128)} async-done(((f32[2,2048,512]{2,0,1:T(2,128)}), f32[2,2048,512]{2,0,1:T(2,128)}, u32[]{:S(2)}, u32[]{:S(2)}) %all-to-all-start) | async-done | bytes 8388640 | tf_op jit(solution)/shard_map/all_to_all | solution.py:104
  492.7 8.2 copy.149
  501.0 8.8 copy.150
  519.5 9.7 fusion.54
  529.3 7.0 fusion.47
  545.6 9.1 fusion.53
  554.8 7.0 fusion.50
  569.6 12.4 %copy_dynamic-update-slice_fusion = f32[2,256,4096]{1,0,2:T(2,128)} fusion(f32[2,256,4096]{1,0,2:T(2,128)} %broadcast_in_dim.15, s32[]{:T(128)S(6)} %select_n.239, f32[2,256,2048]{1,2,0:T(8,128)S(1)} %bitcast.190), kind=kLoop, calls=%fused_computation.52 | loop fusion | bytes 8388612 | tf_op jit(solution)/shard_map/dynamic_update_slice | solution.py:121
  600.4 170.5 %all-to-all-done.1 = f32[2,256,4096]{1,0,2:T(2,128)} async-done(((f32[2,256,4096]{1,0,2:T(2,128)}), f32[2,256,4096]{1,0,2:T(2,128)}, u32[]{:S(2)}, u32[]{:S(2)}) %all-to-all-start.1) | async-done | bytes 8388640 | tf_op jit(solution)/shard_map/all_to_all | solution.py:124
  770.9 7.3 copy.164
  778.2 13.3 %copy.165 = f32[2,8,256,512]{3,0,2,1:T(2,128)} copy(f32[2,8,256,512]{2,3,1,0:T(8,128)} %bitcast.188) | data formatting | bytes 16777216 | tf_op jit(solution)/shard_map/all_to_all | solution.py:124
  791.5 31.6 %fusion.41 = f32[2,512,4,512,1]{3,1,2,0,4:T(8,128)} fusion(f32[2,512,4,512]{3,0,2,1:T(2,128)} %bitcast.191, f32[1,2,512,512]{2,3,1,0:T(8,128)} %get-tuple-element.16, f32[1,2,512,512]{2,3,1,0:T(8,128)S(1)} %get-tuple-element.15), kind=kOutput, calls=%fused_computation.57 | convolution fusion | flops 25770852352 | bytes 20971520 | tf_op jit(solution)/shard_map/ptrc,pqtk->qkrc/dot_general | solution.py:56
  823.2 32.4 %fusion.14 = f32[2,4,512,512]{3,1,0,2:T(4,128)S(1)} fusion(f32[2,2,512,4,4]{3,4,0,1,2:T(4,128)} %copy.168, f32[2,512,4,512,1]{3,1,2,0,4:T(8,128)} %fusion.41), kind=kOutput, calls=%fused_computation.20 | convolution fusion | flops 201326592 | bytes 16908288 | tf_op jit(solution)/shard_map/pkrc,pqkrj->qjkc/dot_general | solution.py:59
  863.9 23.1 %fusion.32 = (f32[1,2048,512]{2,1,0:T(8,128)S(1)}, f32[1,2048,512]{2,1,0:T(8,128)S(1)}) fusion(f32[1,4,512,512]{3,2,1,0:T(8,128)S(1)} %copy.171, f32[1,4,512,512]{3,2,1,0:T(8,128)S(1)} %copy.170, f32[]{:T(128)} %bitcast.6, f32[512]{0:T(512)S(1)} %get-tuple-element.53, f32[2048]{0:T(1024)S(1)} %get-tuple-element.58, f32[512]{0:T(512)S(1)} %get-tuple-element.54, ...), kind=kLoop, calls=%fused_computation.41 | loop fusion | flops 33554432 | bytes 16818192 | tf_op jit(solution)/shard_map/add | solution.py:128
  891.3 7.9 broadcast_in_dim.12
  899.2 22.6 %dynamic_update_slice.7 = f32[2,4096,512]{2,1,0:T(8,128)} dynamic-update-slice(f32[2,4096,512]{2,1,0:T(8,128)} %broadcast_in_dim.12, f32[2,2048,512]{2,1,0:T(8,128)} %pad_maximum_fusion, s32[]{:T(128)} %constant.100.clone.1, s32[]{:T(128)S(6)} %select_n.238, s32[]{:T(128)} %constant.100.clone.1) | dynamic-update-slice | bytes 16777220 | tf_op jit(solution)/shard_map/dynamic_update_slice | solution.py:131
  921.8 151.8 %reduce-scatter.2.cloned.1.call-done = f32[2,1024,512]{2,1,0:T(8,128)} async-done(((f32[2,4096,512]{2,1,0:T(8,128)}), f32[2,1024,512]{2,1,0:T(8,128)}) %reduce-scatter.2.cloned.1.call-update) | async-done | bytes 4194320 | tf_op jit(solution)/shard_map/reduce_scatter | solution.py:132
  (75 shorter events, 118.4 us)
Async XLA Ops:
  6.5 0.7 copy-start.6
  6.5 2.8 copy-start.5
  6.5 162.7 %all-gather.2.cloned.1.call-start = ((), (), s32[]{:S(2)}) async-start(), calls=%async_computation.3 | async-start | bytes 20971520 | tf_op jit(solution)/shard_map/all_gather | solution.py:86
  217.3 3.7 copy-start.3
  217.3 4.1 copy-start.4
  303.7 189.0 %all-to-all-start = ((f32[2,2048,512]{2,0,1:T(2,128)}), f32[2,2048,512]{2,0,1:T(2,128)}, u32[]{:S(2)}, u32[]{:S(2)}) async-start(f32[2,2048,512]{2,0,1:T(2,128)} %copy.148), calls=%async_computation | async-start | bytes 16777216 | tf_op jit(solution)/shard_map/all_to_all | solution.py:104
  519.5 9.7 copy-start.1
  540.8 3.1 copy-start.2
  545.6 9.1 copy-start
  582.1 188.8 %all-to-all-start.1 = ((f32[2,256,4096]{1,0,2:T(2,128)}), f32[2,256,4096]{1,0,2:T(2,128)}, u32[]{:S(2)}, u32[]{:S(2)}) async-start(f32[2,256,4096]{1,0,2:T(2,128)} %copy_dynamic-update-slice_fusion), calls=%async_computation.1 | async-start | bytes 16777216 | tf_op jit(solution)/shard_map/all_to_all | solution.py:124
  587.0 486.6 %reduce-scatter.2.cloned.1.call-start = ((), (), s32[]{:S(2)}) async-start(), calls=%async_computation.4 | async-start | bytes 20971520 | tf_op jit(solution)/shard_map/reduce_scatter | solution.py:132
Sparse Core Ops, SparseCore 0:
  9.2 160.0 all-gather.1
  921.9 151.6 reduce-scatter.1
where the time goes:
time: 1100 us; the launch traced here: 1090 us
  waiting for transfers between devices  630 us (57%)
  local copies, waits for them, and re-layouts  178 us (16%)
  matrix products  158 us (14%)
  other arithmetic  91.9 us (8%)
  between operations  19.3 us (2%)
    all_to_all x1, waiting for transfers between devices, on_device(): lax.all_to_all(padded, 'row', split_axis=2, concat_axis=1, tiled=True)  171 us
    all_to_all x1, waiting for transfers between devices, on_device(): lax.all_to_all(stacked, 'row', split_axis=1, concat_axis=2, tiled=True)  165 us
    reduce_scatter x1, waiting for transfers between devices, on_device(): summed = lax.psum_scatter(embedded, 'led', scatter_dimension=1, tiled=True)  152 us
    all_gather x1, waiting for transfers between devices, on_device(): region = lax.all_gather(spectrum, 'led', axis=1, tiled=True)  141 us
    dot_general x4, matrix products, transform(): jnp.einsum('p' + middle + ',pqkrj->q' + output, middle_pair, second_table...  79.1 us
    dot_general x4, matrix products, transform(): jnp.einsum('p' + inputs + ',pqtk->q' + middle, paired, first_table, preci...  78.8 us
    sub x1, other arithmetic, on_device(): lit_re = pupil_re * band_rows[0] - pupil_im * band_rows[1]  26.9 us
    another operation x4, local copies, waits for them, and re-layouts, on_device(): jnp.stack([lit_re, lit_im]).reshape(shape_rows)  24.8 us
  transfers between devices with their start and end apart: 4, of which 4 were waited for; matrix products, arithmetic and copies ran while one was open for 4% of the time, Pallas kernels for 0%

commit v1 on v0

--- a/solution.py
+++ b/solution.py
@@ -7,6 +7,7 @@
 
 SOFTENING = 0.1
 HIGHEST_PRECISION = lax.Precision.HIGHEST
+CHUNKS = 2
 
 
 def pupil_at(down_index, across_index, coeffs, centre):
@@ -61,6 +62,65 @@
     )
 
 
+def unit_times(value_re, value_im, turn):
+    eighths = round(turn * 8) % 8
+    if eighths == 0:
+        return value_re, value_im
+    if eighths == 2:
+        return -value_im, value_re
+    if eighths == 4:
+        return -value_re, -value_im
+    if eighths == 6:
+        return value_im, -value_re
+    c = math.cos(2.0 * math.pi * turn)
+    s = math.sin(2.0 * math.pi * turn)
+    return value_re * c - value_im * s, value_re * s + value_im * c
+
+
+def row_transform(pair_re, pair_im, direction, inner=4):
+    length, width = pair_re.shape
+    outer = length // inner
+    angle_step = direction * 2.0 * math.pi / outer
+    index = jnp.arange(outer, dtype=jnp.int32)
+    grid = (index[:, None] * index[None, :]) % outer
+    angles = grid.astype(jnp.float32) * angle_step
+    cos_t = jnp.cos(angles)
+    sin_t = jnp.sin(angles)
+    table = jnp.concatenate(
+        [jnp.concatenate([cos_t, -sin_t], axis=1), jnp.concatenate([sin_t, cos_t], axis=1)], axis=0
+    )
+    stacked = jnp.concatenate(
+        [pair_re.reshape(outer, inner * width), pair_im.reshape(outer, inner * width)], axis=0
+    )
+    middle = jnp.dot(table, stacked, precision=HIGHEST_PRECISION)
+    mid_re = middle[:outer]
+    mid_im = middle[outer:]
+    scaling = 1.0 / math.sqrt(length)
+    twiddled = []
+    for r in range(inner):
+        part_re = mid_re[:, r * width:(r + 1) * width]
+        part_im = mid_im[:, r * width:(r + 1) * width]
+        if r == 0:
+            twiddled.append((part_re * scaling, part_im * scaling))
+            continue
+        tw_angle = (r * index % length).astype(jnp.float32) * (direction * 2.0 * math.pi / length)
+        tw_re = (jnp.cos(tw_angle) * scaling)[:, None]
+        tw_im = (jnp.sin(tw_angle) * scaling)[:, None]
+        twiddled.append((part_re * tw_re - part_im * tw_im, part_re * tw_im + part_im * tw_re))
+    out_re = []
+    out_im = []
+    for j in range(inner):
+        acc_re = None
+        acc_im = None
+        for r in range(inner):
+            t_re, t_im = unit_times(twiddled[r][0], twiddled[r][1], direction * r * j / inner)
+            acc_re = t_re if acc_re is None else acc_re + t_re
+            acc_im = t_im if acc_im is None else acc_im + t_im
+        out_re.append(acc_re)
+        out_im.append(acc_im)
+    return jnp.concatenate(out_re, axis=0), jnp.concatenate(out_im, axis=0)
+
+
 def correct(field_re, field_im, measured):
     magnitude = jnp.sqrt(field_re * field_re + field_im * field_im + SOFTENING)
     factor = measured / magnitude
@@ -77,32 +137,34 @@
     window = amplitudes.shape[2]
     centre = window // 2
     block_rows = window // row_count
-    outer_rows = window // led_count
     outer_cols = window // row_count
+    chunks = max(1, min(CHUNKS, size_cols // 128))
+    width = size_cols // chunks
     row_shift = offsets[led_index, 0]
     col_shift = offsets[led_index, 1]
     measured = amplitudes[0]
     shape_cols = (2, block_rows, outer_cols, row_count)
-    region = lax.all_gather(spectrum, "led", axis=1, tiled=True)
-    band_rows = lax.dynamic_slice_in_dim(region, row_shift, window, 1)
     row_ids = jnp.arange(window, dtype=jnp.int32)[:, None]
-    col_ids = (row_index * size_cols + jnp.arange(size_cols, dtype=jnp.int32))[None, :] - col_shift
-    pupil_re, pupil_im = pupil_at(row_ids, col_ids, coeffs, centre)
-    lit_re = pupil_re * band_rows[0] - pupil_im * band_rows[1]
-    lit_im = pupil_re * band_rows[1] + pupil_im * band_rows[0]
-    shape_rows = (2, outer_rows, led_count, size_cols)
-    half = transform(
-        jnp.stack([lit_re, lit_im]).reshape(shape_rows),
-        "trc",
-        "krc",
-        "jkc",
-        outer_rows,
-        led_count,
-        1.0,
-    )
-    stacked = half.reshape(2, window, size_cols)
-    spread = lax.all_to_all(stacked, "row", split_axis=1, concat_axis=2, tiled=True)
-    window_part = lax.dynamic_slice_in_dim(spread, col_shift, window, 2)
+
+    pupils = []
+    spreads = []
+    for chunk in range(chunks):
+        part = spectrum[:, :, chunk * width:(chunk + 1) * width]
+        region = lax.all_gather(part, "led", axis=1, tiled=True)
+        band = lax.dynamic_slice_in_dim(region, row_shift, window, 1)
+        col_ids = (
+            row_index * size_cols + chunk * width + jnp.arange(width, dtype=jnp.int32)
+        )[None, :] - col_shift
+        pupil_re, pupil_im = pupil_at(row_ids, col_ids, coeffs, centre)
+        pupils.append((pupil_re, pupil_im))
+        lit_re = pupil_re * band[0] - pupil_im * band[1]
+        lit_im = pupil_re * band[1] + pupil_im * band[0]
+        half_re, half_im = row_transform(lit_re, lit_im, 1.0)
+        stacked = jnp.stack([half_re, half_im])
+        spread = lax.all_to_all(stacked, "row", split_axis=1, concat_axis=2, tiled=True)
+        spreads.append(spread.reshape(2, block_rows, row_count, width))
+    spread_all = jnp.stack(spreads, axis=3).reshape(2, block_rows, row_count * size_cols)
+    window_part = lax.dynamic_slice_in_dim(spread_all, col_shift, window, 2)
     field = transform(
         window_part.reshape(shape_cols), "ytr", "ykr", "yjk", outer_cols, row_count, 1.0
     )
@@ -121,15 +183,21 @@
     padded = lax.dynamic_update_slice_in_dim(
         padded, back.reshape(2, block_rows, window), col_shift, 2
     )
-    gathered_cols = lax.all_to_all(padded, "row", split_axis=2, concat_axis=1, tiled=True)
-    spec = transform(
-        gathered_cols.reshape(shape_rows), "trc", "krc", "jkc", outer_rows, led_count, -1.0
-    ).reshape(2, window, size_cols)
-    upd_re = pupil_re * spec[0] + pupil_im * spec[1]
-    upd_im = pupil_re * spec[1] - pupil_im * spec[0]
-    embedded = jnp.zeros((2, size_rows * led_count, size_cols), jnp.float32)
-    embedded = lax.dynamic_update_slice_in_dim(embedded, jnp.stack([upd_re, upd_im]), row_shift, 1)
-    summed = lax.psum_scatter(embedded, "led", scatter_dimension=1, tiled=True)
+    padded = padded.reshape(2, block_rows, row_count, chunks, width)
+    results = []
+    for chunk in range(chunks):
+        piece = padded[:, :, :, chunk, :].reshape(2, block_rows, row_count * width)
+        gathered = lax.all_to_all(piece, "row", split_axis=2, concat_axis=1, tiled=True)
+        spec_re, spec_im = row_transform(gathered[0], gathered[1], -1.0)
+        pupil_re, pupil_im = pupils[chunk]
+        upd_re = pupil_re * spec_re + pupil_im * spec_im
+        upd_im = pupil_re * spec_im - pupil_im * spec_re
+        embedded = jnp.zeros((2, size_rows * led_count, width), jnp.float32)
+        embedded = lax.dynamic_update_slice_in_dim(
+            embedded, jnp.stack([upd_re, upd_im]), row_shift, 1
+        )
+        results.append(lax.psum_scatter(embedded, "led", scatter_dimension=1, tiled=True))
+    summed = jnp.concatenate(results, axis=2)
     return spectrum + summed
 
 

time: 1100 us -> 1100 us (level)
  other arithmetic: 91.9 us -> 168 us
  matrix products: 158 us -> 92 us
  waiting for transfers between devices: 630 us -> 578 us
  local copies, waits for them, and re-layouts: 178 us -> 208 us
    dot_general x4 -> x2, matrix products: 79.1 us -> 14 us  [transform(): jnp.einsum('p' + middle + ',pqkrj->q' + output, middle_pair, second_table...]
    dot_general x4 -> x2, matrix products: 78.8 us -> 18.8 us  [transform(): jnp.einsum('p' + inputs + ',pqtk->q' + middle, paired, first_table, preci...]
    dot_general x0 -> x4, matrix products: none -> 59.2 us  [row_transform(): middle = jnp.dot(table, stacked, precision=HIGHEST_PRECISION)]
    another operation x4 -> x11, local copies, waits for them, and re-layouts: 24.8 us -> 68.8 us  [the longest x2 24.5 us: on_device(): stacked = jnp.stack([half_re, half_im])]
    add x1 -> x10, other arithmetic: 23.1 us -> 56.5 us  [the longest x2 33.4 us: on_device(): upd_re = pupil_re * spec_re + pupil_im * spec_im]
    sub x1 -> x4, other arithmetic: 26.9 us -> 59.8 us  [the longest x2 33.2 us: on_device(): upd_im = pupil_re * spec_im - pupil_im * spec_re]
    reduce_scatter x1 -> x2, waiting for transfers between devices: 152 us -> 119 us  [on_device(): lax.psum_scatter(embedded, 'led', scatter_dimension=1, tiled=True)]
    slice x3 -> x9, local copies, waits for them, and re-layouts: 8.34 us -> 29.8 us  [the longest x6 12.7 us: on_device(): spec_re, spec_im = row_transform(gathered[0], gathered[1], -1.0)]
  transfers between devices with their start and end apart: 4 -> 8, of which waited for: 4 -> 8; matrix products, arithmetic and copies ran while one was open for 4% -> 13% of each run, Pallas kernels for 0% -> 0%
where the time goes in v1:
time: 1100 us; the launch traced here: 1080 us
  waiting for transfers between devices  578 us (53%)
  local copies, waits for them, and re-layouts  208 us (19%)
  other arithmetic  168 us (15%)
  matrix products  92 us (8%)
  between operations  19.8 us (2%)
  starting transfers between devices  18.8 us (2%)
    all_to_all x2, waiting for transfers between devices, on_device(): lax.all_to_all(piece, 'row', split_axis=2, concat_axis=1, tiled=True)  158 us
    all_gather x2, waiting for transfers between devices, on_device(): region = lax.all_gather(part, 'led', axis=1, tiled=True)  151 us
    all_to_all x2, waiting for transfers between devices, on_device(): lax.all_to_all(stacked, 'row', split_axis=1, concat_axis=2, tiled=True)  150 us
    reduce_scatter x2, waiting for transfers between devices, on_device(): lax.psum_scatter(embedded, 'led', scatter_dimension=1, tiled=True)  119 us
    dot_general x4, matrix products, row_transform(): middle = jnp.dot(table, stacked, precision=HIGHEST_PRECISION)  59.2 us
    add x2, other arithmetic, on_device(): upd_re = pupil_re * spec_re + pupil_im * spec_im  33.4 us
    sub x2, other arithmetic, on_device(): upd_im = pupil_re * spec_im - pupil_im * spec_re  33.2 us
    sub x2, other arithmetic, on_device(): lit_re = pupil_re * band[0] - pupil_im * band[1]  26.6 us
  transfers between devices with their start and end apart: 8, of which 8 were waited for; matrix products, arithmetic and copies ran while one was open for 13% of the time, Pallas kernels for 0%

profile of v1, /device:TPU:0, one launch (start us, length us, event | category | flops | bytes accessed | tf_op | source)
XLA Modules:
  0.0 1084.8 jit_solution(2999352237423477570)
XLA Ops:
  39.5 62.0 %all-gather.3.cloned.1.call-done = f32[2,4096,256]{2,1,0:T(8,128)} async-done(((f32[2,1024,256]{2,1,0:T(8,128)}), f32[2,4096,256]{2,1,0:T(8,128)}) %all-gather.3.cloned.1.call-update) | async-done | bytes 8388624 | tf_op jit(solution)/shard_map/all_gather | solution.py:153
  101.5 89.4 %all-gather.5.cloned.1.call-done = f32[2,4096,256]{2,1,0:T(8,128)} async-done(((f32[2,1024,256]{2,1,0:T(8,128)}), f32[2,4096,256]{2,1,0:T(8,128)}) %all-gather.5.cloned.1.call-update) | async-done | bytes 8388624 | tf_op jit(solution)/shard_map/all_gather | solution.py:153
  206.5 14.6 %multiply_subtract_fusion.6 = (f32[512,1024]{1,0:T(8,128)S(1)}, pred[512,1024]{1,0:T(8,128)(4,1)S(1)}, f32[512,1024]{1,0:T(8,128)S(1)}) fusion(f32[512,1024]{1,0:T(8,128)} %squeeze.58, f32[512,1024]{1,0:T(8,128)} %squeeze.57, s32[512,1024]{1,0:T(8,128)} %bitcast.206, s32[1024]{0:T(1024)S(1)} %bitcast.225, f32[]{:T(128)} %bitcast.6, ...), kind=kLoop, calls=%fused_computation.109 | loop fusion | flops 15204352 | bytes 17317904 | tf_op jit(solution)/shard_map/sub | solution.py:160
  229.4 12.1 %multiply_subtract_fusion.7 = (f32[512,1024]{1,0:T(8,128)S(1)}, pred[512,1024]{1,0:T(8,128)(4,1)S(1)}, f32[512,1024]{1,0:T(8,128)S(1)}) fusion(f32[512,1024]{1,0:T(8,128)S(1)} %copy-done.2, f32[512,1024]{1,0:T(8,128)S(1)} %squeeze.55, s32[512,1024]{1,0:T(8,128)S(1)} %bitcast.207, s32[1024]{0:T(1024)S(1)} %bitcast.229, f32[]{:T(128)} %bitcast.6, ...), kind=kLoop, calls=%fused_computation.112 | loop fusion | flops 15204352 | bytes 17317904 | tf_op jit(solution)/shard_map/sub | solution.py:160
  249.5 13.8 %fusion.4 = f32[1024,1024]{1,0:T(8,128)S(1)} fusion(f32[512,1024]{1,0:T(8,128)S(1)} %multiply_add_fusion.2, f32[512,1024]{1,0:T(8,128)S(1)} %get-tuple-element.44, f32[512,512]{1,0:T(8,128)S(1)} %copy-done.21, f32[512,512]{1,0:T(8,128)S(1)} %copy-done.20, f32[512,512]{1,0:T(8,128)S(1)} %fusion.78), kind=kOutput, calls=%fused_computation.16 | convolution fusion | flops 12889096192 | bytes 11534336 | tf_op jit(solution)/shard_map/dot_general | solution.py:95
  263.2 13.9 %fusion = f32[1024,1024]{1,0:T(8,128)S(1)} fusion(f32[512,1024]{1,0:T(8,128)S(1)} %multiply_add_fusion.3, f32[512,1024]{1,0:T(8,128)S(1)} %get-tuple-element.32, f32[512,512]{1,0:T(8,128)S(1)} %copy-done.21, f32[512,512]{1,0:T(8,128)S(1)} %copy-done.20, f32[512,512]{1,0:T(8,128)S(1)} %fusion.78), kind=kOutput, calls=%fused_computation.11 | convolution fusion | flops 12889096192 | bytes 11534336 | tf_op jit(solution)/shard_map/dot_general | solution.py:95
  283.1 12.2 %copy.111 = f32[2,2048,256]{2,0,1:T(2,128)} copy(f32[2,2048,256]{2,1,0:T(8,128)S(1)} %pad_maximum_fusion.1) | data formatting | bytes 8388608 | tf_op jit(solution)/shard_map/stack | solution.py:163
  303.1 12.3 %copy.113 = f32[2,2048,256]{2,0,1:T(2,128)} copy(f32[2,2048,256]{2,1,0:T(8,128)S(1)} %pad_maximum_fusion.2) | data formatting | bytes 8388608 | tf_op jit(solution)/shard_map/stack | solution.py:163
  315.4 78.6 %all-to-all-done = f32[2,2048,256]{2,0,1:T(2,128)} async-done(((f32[2,2048,256]{2,0,1:T(2,128)}), f32[2,2048,256]{2,0,1:T(2,128)}, u32[]{:S(2)}, u32[]{:S(2)}) %all-to-all-start) | async-done | bytes 4194336 | tf_op jit(solution)/shard_map/all_to_all | solution.py:164
  422.0 70.9 %all-to-all-done.1 = f32[2,2048,256]{2,0,1:T(2,128)} async-done(((f32[2,2048,256]{2,0,1:T(2,128)}), f32[2,2048,256]{2,0,1:T(2,128)}, u32[]{:S(2)}, u32[]{:S(2)}) %all-to-all-start.1) | async-done | bytes 4194336 | tf_op jit(solution)/shard_map/all_to_all | solution.py:164
  569.5 12.5 %dynamic_update_slice.9 = f32[2,256,4096]{1,2,0:T(8,128)} dynamic-update-slice(f32[2,256,4096]{1,2,0:T(8,128)} %broadcast_in_dim.18, f32[2,256,2048]{1,2,0:T(8,128)} %bitcast.212, s32[]{:T(128)} %constant.153.clone.1, s32[]{:T(128)} %constant.153.clone.1, s32[]{:T(128)S(6)} %select_n.348) | dynamic-update-slice | bytes 8388612 | tf_op jit(solution)/shard_map/dynamic_update_slice | solution.py:183
  588.2 12.4 %copy.132 = f32[2,256,2048]{1,0,2:T(2,128)} copy(f32[2,256,2048]{1,2,0:T(8,128)S(1)} %bitcast.217) | data formatting | bytes 8388608 | tf_op jit(solution)/shard_map/reshape;squeeze | solution.py:189
  614.0 85.2 %all-to-all-done.3 = f32[2,256,2048]{1,0,2:T(2,128)} async-done(((f32[2,256,2048]{1,0,2:T(2,128)}), f32[2,256,2048]{1,0,2:T(2,128)}, u32[]{:S(2)}, u32[]{:S(2)}) %all-to-all-start.3) | async-done | bytes 4194336 | tf_op jit(solution)/shard_map/all_to_all | solution.py:190
  725.2 72.4 %all-to-all-done.2 = f32[2,256,2048]{1,0,2:T(2,128)} async-done(((f32[2,256,2048]{1,0,2:T(2,128)}), f32[2,256,2048]{1,0,2:T(2,128)}, u32[]{:S(2)}, u32[]{:S(2)}) %all-to-all-start.2) | async-done | bytes 4194336 | tf_op jit(solution)/shard_map/all_to_all | solution.py:190
  809.8 17.7 %fusion.15 = f32[1024,1024]{1,0:T(8,128)S(1)} fusion(f32[512,1024]{1,0:T(8,128)} %reshape_squeeze.23, f32[512,1024]{1,0:T(8,128)} %reshape_squeeze.22, f32[512,512]{1,0:T(8,128)} %get-tuple-element.150, f32[512,512]{1,0:T(8,128)} %get-tuple-element.149, f32[512,512]{1,0:T(8,128)S(1)} %fusion.77), kind=kOutput, calls=%fused_computation.30 | convolution fusion | flops 12889096192 | bytes 11534336 | tf_op jit(solution)/shard_map/dot_general | solution.py:95
  827.5 13.8 %fusion.11 = f32[1024,1024]{1,0:T(8,128)S(1)} fusion(f32[512,1024]{1,0:T(8,128)S(1)} %copy-done.15, f32[512,1024]{1,0:T(8,128)S(1)} %copy-done.14, f32[512,512]{1,0:T(8,128)S(1)} %copy-done.23, f32[512,512]{1,0:T(8,128)S(1)} %copy-done.22, f32[512,512]{1,0:T(8,128)S(1)} %fusion.77), kind=kOutput, calls=%fused_computation.25 | convolution fusion | flops 12889096192 | bytes 11534336 | tf_op jit(solution)/shard_map/dot_general | solution.py:95
  846.0 16.6 %multiply_add_fusion.1 = f32[1,2048,256]{2,1,0:T(8,128)S(1)} fusion(f32[1,512,256]{2,1,0:T(8,128)S(1)} %get-tuple-element.56, f32[1,512,256]{2,1,0:T(8,128)S(1)} %get-tuple-element.74, f32[1,512,256]{2,1,0:T(8,128)S(1)} %get-tuple-element.55, f32[1,512,256]{2,1,0:T(8,128)S(1)} %get-tuple-element.109, f32[1,512,256]{2,1,0:T(8,128)S(1)} %get-tuple-element.108, ...), kind=kLoop, calls=%fused_computation.107 | loop fusion | flops 18350080 | bytes 6328336 | tf_op jit(solution)/shard_map/add | solution.py:193
  862.6 16.6 %multiply_subtract_fusion.5 = f32[1,2048,256]{2,1,0:T(8,128)S(1)} fusion(f32[1,512,256]{2,1,0:T(8,128)S(1)} %get-tuple-element.56, f32[1,512,256]{2,1,0:T(8,128)S(1)} %get-tuple-element.74, f32[1,512,256]{2,1,0:T(8,128)S(1)} %get-tuple-element.55, f32[1,512,256]{2,1,0:T(8,128)S(1)} %get-tuple-element.109, f32[1,512,256]{2,1,0:T(8,128)S(1)} %get-tuple-element.108, ...), kind=kLoop, calls=%fused_computation.106 | loop fusion | flops 18350080 | bytes 6328336 | tf_op jit(solution)/shard_map/sub | solution.py:194
  885.5 12.5 %dynamic_update_slice.10 = f32[2,4096,256]{2,1,0:T(8,128)} dynamic-update-slice(f32[2,4096,256]{2,1,0:T(8,128)} %broadcast.2090.clone.1, f32[2,2048,256]{2,1,0:T(8,128)} %pad_maximum_fusion.3, s32[]{:T(128)} %constant.153.clone.1, s32[]{:T(128)S(6)} %select_n.343, s32[]{:T(128)} %constant.153.clone.1) | dynamic-update-slice | bytes 8388612 | tf_op jit(solution)/shard_map/dynamic_update_slice | solution.py:196
  900.3 16.8 %multiply_add_fusion = f32[1,2048,256]{2,1,0:T(8,128)S(1)} fusion(f32[1,512,256]{2,1,0:T(8,128)S(1)} %get-tuple-element.58, f32[1,512,256]{2,1,0:T(8,128)S(1)} %get-tuple-element.73, f32[1,512,256]{2,1,0:T(8,128)S(1)} %get-tuple-element.57, f32[1,512,256]{2,1,0:T(8,128)S(1)} %get-tuple-element.21, f32[1,512,256]{2,1,0:T(8,128)S(1)} %get-tuple-element.66, ...), kind=kLoop, calls=%fused_computation.104 | loop fusion | flops 18350080 | bytes 6328336 | tf_op jit(solution)/shard_map/add | solution.py:193
  917.1 16.6 %multiply_subtract_fusion.4 = f32[1,2048,256]{2,1,0:T(8,128)S(1)} fusion(f32[1,512,256]{2,1,0:T(8,128)S(1)} %get-tuple-element.58, f32[1,512,256]{2,1,0:T(8,128)S(1)} %get-tuple-element.73, f32[1,512,256]{2,1,0:T(8,128)S(1)} %get-tuple-element.57, f32[1,512,256]{2,1,0:T(8,128)S(1)} %get-tuple-element.21, f32[1,512,256]{2,1,0:T(8,128)S(1)} %get-tuple-element.66, ...), kind=kLoop, calls=%fused_computation.103 | loop fusion | flops 18350080 | bytes 6328336 | tf_op jit(solution)/shard_map/sub | solution.py:194
  939.8 12.6 %dynamic_update_slice.11 = f32[2,4096,256]{2,1,0:T(8,128)} dynamic-update-slice(f32[2,4096,256]{2,1,0:T(8,128)} %broadcast.2090.clone, f32[2,2048,256]{2,1,0:T(8,128)} %pad_maximum_fusion.4, s32[]{:T(128)} %constant.153.clone.1, s32[]{:T(128)S(6)} %select_n.343, s32[]{:T(128)} %constant.153.clone.1) | dynamic-update-slice | bytes 8388612 | tf_op jit(solution)/shard_map/dynamic_update_slice | solution.py:196
  952.5 29.9 %reduce-scatter.3.cloned.1.call-done = f32[2,1024,256]{2,1,0:T(8,128)} async-done(((f32[2,4096,256]{2,1,0:T(8,128)}), f32[2,1024,256]{2,1,0:T(8,128)}) %reduce-scatter.3.cloned.1.call-update) | async-done | bytes 2097168 | tf_op jit(solution)/shard_map/reduce_scatter | solution.py:199
  982.4 89.3 %reduce-scatter.5.cloned.1.call-done = f32[2,1024,256]{2,1,0:T(8,128)} async-done(((f32[2,4096,256]{2,1,0:T(8,128)}), f32[2,1024,256]{2,1,0:T(8,128)}) %reduce-scatter.5.cloned.1.call-update) | async-done | bytes 2097168 | tf_op jit(solution)/shard_map/reduce_scatter | solution.py:199
  (225 shorter events, 260.3 us)
Async XLA Ops:
  6.5 95.0 %all-gather.3.cloned.1.call-start = ((), (), s32[]{:S(2)}) async-start(), calls=%async_computation.6 | async-start | bytes 10485760 | tf_op jit(solution)/shard_map/all_gather | solution.py:153
  11.2 179.7 %all-gather.5.cloned.1.call-start = ((), (), s32[]{:S(2)}) async-start(), calls=%async_computation.7 | async-start | bytes 10485760 | tf_op jit(solution)/shard_map/all_gather | solution.py:153
  16.7 12.6 %copy-start.33 = (s32[256]{0:T(256)}, s32[256]{0:T(256)S(1)}, u32[]{:S(2)}) copy-start(s32[256]{0:T(256)S(1)} %get-tuple-element.139) | copy-start | bytes 3076
  17.4 12.0 %copy-start.35 = (f32[256]{0:T(256)}, f32[256]{0:T(256)S(1)}, u32[]{:S(2)}) copy-start(f32[256]{0:T(256)S(1)} %get-tuple-element.141) | copy-start | bytes 3076
  206.5 14.6 %copy-start.3 = (f32[512,1024]{1,0:T(8,128)S(1)}, f32[512,1024]{1,0:T(8,128)}, u32[]{:S(2)}) copy-start(f32[512,1024]{1,0:T(8,128)} %squeeze.57) | copy-start | bytes 6291460
  206.5 14.6 %copy-start.4 = (f32[512,1024]{1,0:T(8,128)S(1)}, f32[512,1024]{1,0:T(8,128)}, u32[]{:S(2)}) copy-start(f32[512,1024]{1,0:T(8,128)} %squeeze.58) | copy-start | bytes 6291460
  206.5 22.9 %copy-start.8 = (f32[64,8,4,256]{3,1,2,0:T(8,128)S(1)}, f32[64,8,4,256]{3,1,2,0:T(8,128)}, u32[]{:S(2)}) copy-start(f32[64,8,4,256]{3,1,2,0:T(8,128)} %copy.154) | copy-start | bytes 6291460
  221.1 8.3 copy-start.2
  221.1 8.3 copy-start.5
  221.1 8.3 copy-start.6
  263.2 17.4 %copy-start.1 = (f32[1024,1024]{1,0:T(8,128)}, f32[1024,1024]{1,0:T(8,128)S(1)}, u32[]{:S(2)}) copy-start(f32[1024,1024]{1,0:T(8,128)S(1)} %fusion.4) | copy-start | bytes 12582916
  295.3 98.7 %all-to-all-start = ((f32[2,2048,256]{2,0,1:T(2,128)}), f32[2,2048,256]{2,0,1:T(2,128)}, u32[]{:S(2)}, u32[]{:S(2)}) async-start(f32[2,2048,256]{2,0,1:T(2,128)} %copy.111), calls=%async_computation | async-start | bytes 8388608 | tf_op jit(solution)/shard_map/all_to_all | solution.py:164
  394.0 98.9 %all-to-all-start.1 = ((f32[2,2048,256]{2,0,1:T(2,128)}), f32[2,2048,256]{2,0,1:T(2,128)}, u32[]{:S(2)}, u32[]{:S(2)}) async-start(f32[2,2048,256]{2,0,1:T(2,128)} %copy.113), calls=%async_computation.1 | async-start | bytes 8388608 | tf_op jit(solution)/shard_map/all_to_all | solution.py:164
  518.9 9.5 copy-start.10
  544.8 9.4 copy-start.9
  600.6 98.5 %all-to-all-start.3 = ((f32[2,256,2048]{1,0,2:T(2,128)}), f32[2,256,2048]{1,0,2:T(2,128)}, u32[]{:S(2)}, u32[]{:S(2)}) async-start(f32[2,256,2048]{1,0,2:T(2,128)} %copy.132), calls=%async_computation.4 | async-start | bytes 8388608 | tf_op jit(solution)/shard_map/all_to_all | solution.py:190
  699.2 98.5 %all-to-all-start.2 = ((f32[2,256,2048]{1,0,2:T(2,128)}), f32[2,256,2048]{1,0,2:T(2,128)}, u32[]{:S(2)}, u32[]{:S(2)}) async-start(f32[2,256,2048]{1,0,2:T(2,128)} %copy.128), calls=%async_computation.2 | async-start | bytes 8388608 | tf_op jit(solution)/shard_map/all_to_all | solution.py:190
  703.7 278.7 %reduce-scatter.3.cloned.1.call-start = ((), (), s32[]{:S(2)}) async-start(), calls=%async_computation.8 | async-start | bytes 10485760 | tf_op jit(solution)/shard_map/reduce_scatter | solution.py:199
  809.8 17.7 %copy-start.14 = (f32[512,1024]{1,0:T(8,128)S(1)}, f32[512,1024]{1,0:T(8,128)}, u32[]{:S(2)}) copy-start(f32[512,1024]{1,0:T(8,128)} %reshape_squeeze.19) | copy-start | bytes 6291460
  809.8 17.7 %copy-start.15 = (f32[512,1024]{1,0:T(8,128)S(1)}, f32[512,1024]{1,0:T(8,128)}, u32[]{:S(2)}) copy-start(f32[512,1024]{1,0:T(8,128)} %reshape_squeeze.20) | copy-start | bytes 6291460
  809.8 17.7 %copy-start.22 = (f32[512,512]{1,0:T(8,128)S(1)}, f32[512,512]{1,0:T(8,128)}, u32[]{:S(2)}) copy-start(f32[512,512]{1,0:T(8,128)} %get-tuple-element.149) | copy-start | bytes 3145732
  809.8 17.7 %copy-start.23 = (f32[512,512]{1,0:T(8,128)S(1)}, f32[512,512]{1,0:T(8,128)}, u32[]{:S(2)}) copy-start(f32[512,512]{1,0:T(8,128)} %get-tuple-element.150) | copy-start | bytes 3145732
  827.5 16.4 %copy-start = (f32[1024,1024]{1,0:T(8,128)}, f32[1024,1024]{1,0:T(8,128)S(1)}, u32[]{:S(2)}) copy-start(f32[1024,1024]{1,0:T(8,128)S(1)} %fusion.15) | copy-start | bytes 12582916
  898.0 173.6 %reduce-scatter.5.cloned.1.call-start = ((), (), s32[]{:S(2)}) async-start(), calls=%async_computation.9 | async-start | bytes 10485760 | tf_op jit(solution)/shard_map/reduce_scatter | solution.py:199
  (26 other events, 60.8 us)
Sparse Core Ops, SparseCore 0:
  11.3 90.1 all-gather.2
  103.4 87.4 all-gather.4
  898.1 84.2 reduce-scatter.2
  985.3 86.3 reduce-scatter.4

commit v2 on v1

--- a/solution.py
+++ b/solution.py
@@ -5,9 +5,10 @@
 from jax import lax
 from jax.sharding import PartitionSpec as P
 
+
 SOFTENING = 0.1
-HIGHEST_PRECISION = lax.Precision.HIGHEST
-CHUNKS = 2
+HIGHEST_PRECISION = lax.Precision.HIGH
+CHUNKS = 4
 
 
 def pupil_at(down_index, across_index, coeffs, centre):
@@ -146,17 +147,24 @@
     shape_cols = (2, block_rows, outer_cols, row_count)
     row_ids = jnp.arange(window, dtype=jnp.int32)[:, None]
 
-    pupils = []
+    col_ids = (row_index * size_cols + jnp.arange(size_cols, dtype=jnp.int32))[None, :]
+    pupil_full = pupil_at(row_ids, col_ids - col_shift, coeffs, centre)
+    pupil_full = lax.optimization_barrier(pupil_full)
+    pupils = [
+        (pupil_full[0][:, c * width:(c + 1) * width], pupil_full[1][:, c * width:(c + 1) * width])
+        for c in range(chunks)
+    ]
+    regions = []
+    for chunk in range(chunks):
+        part = spectrum[:, :, chunk * width:(chunk + 1) * width]
+        regions.append(lax.all_gather(part, "led", axis=1, tiled=True))
     spreads = []
     for chunk in range(chunks):
-        part = spectrum[:, :, chunk * width:(chunk + 1) * width]
-        region = lax.all_gather(part, "led", axis=1, tiled=True)
+        region = regions[chunk]
+        if spreads:
+            region, _ = lax.optimization_barrier((region, stacked))
         band = lax.dynamic_slice_in_dim(region, row_shift, window, 1)
-        col_ids = (
-            row_index * size_cols + chunk * width + jnp.arange(width, dtype=jnp.int32)
-        )[None, :] - col_shift
-        pupil_re, pupil_im = pupil_at(row_ids, col_ids, coeffs, centre)
-        pupils.append((pupil_re, pupil_im))
+        pupil_re, pupil_im = pupils[chunk]
         lit_re = pupil_re * band[0] - pupil_im * band[1]
         lit_im = pupil_re * band[1] + pupil_im * band[0]
         half_re, half_im = row_transform(lit_re, lit_im, 1.0)
@@ -184,10 +192,15 @@
         padded, back.reshape(2, block_rows, window), col_shift, 2
     )
     padded = padded.reshape(2, block_rows, row_count, chunks, width)
+    gathered_all = []
+    for chunk in range(chunks):
+        piece = padded[:, :, :, chunk, :].reshape(2, block_rows, row_count * width)
+        gathered_all.append(lax.all_to_all(piece, "row", split_axis=2, concat_axis=1, tiled=True))
     results = []
     for chunk in range(chunks):
-        piece = padded[:, :, :, chunk, :].reshape(2, block_rows, row_count * width)
-        gathered = lax.all_to_all(piece, "row", split_axis=2, concat_axis=1, tiled=True)
+        gathered = gathered_all[chunk]
+        if results:
+            gathered, _ = lax.optimization_barrier((gathered, embedded))
         spec_re, spec_im = row_transform(gathered[0], gathered[1], -1.0)
         pupil_re, pupil_im = pupils[chunk]
         upd_re = pupil_re * spec_re + pupil_im * spec_im

time: 1100 us -> 1040 us (0.945); the launches traced: 1080 us -> 1040 us
  other arithmetic: 168 us -> 102 us
  matrix products: 92 us -> 70.5 us
  waiting for transfers between devices: 578 us -> 595 us
  starting transfers between devices: 18.8 us -> 35.1 us
    reduce_scatter x2 -> x4, waiting for transfers between devices: 119 us -> 215 us  [on_device(): lax.psum_scatter(embedded, 'led', scatter_dimension=1, tiled=True)]
    all_to_all x2 -> x4, waiting for transfers between devices: 158 us -> 96.2 us  [on_device(): lax.all_to_all(piece, 'row', split_axis=2, concat_axis=1, tiled=True)]
    add x4 -> x0, other arithmetic: 49.5 us -> none  [the longest x2 33.4 us: on_device(): upd_re = pupil_re * spec_re + pupil_im * spec_im]
    sub x2 -> x0, other arithmetic: 33.2 us -> none  [on_device(): upd_im = pupil_re * spec_im - pupil_im * spec_re]
    mul x1, other arithmetic: 0.01 us -> 24.6 us  [pupil_at(): return (weight * jnp.cos(phases), weight * jnp.sin(phases))]
    all_gather x2 -> x4, waiting for transfers between devices: 151 us -> 131 us  [on_device(): regions.append(lax.all_gather(part, 'led', axis=1, tiled=True))]
    sub x2 -> x4, other arithmetic: 26.6 us -> 13.3 us  [on_device(): lit_re = pupil_re * band[0] - pupil_im * band[1]]
    reshape x0 -> x8, local copies, waits for them, and re-layouts: none -> 11.9 us  [the longest x4 8.26 us: row_transform(): pair_re.reshape(outer, inner * width)]
  transfers between devices with their start and end apart: 8 -> 16, of which waited for: 8 -> 16; matrix products, arithmetic and copies ran while one was open for 13% -> 21% of each run, Pallas kernels for 0% -> 0%
where the time goes in v2:
time: 1040 us
  waiting for transfers between devices  595 us (57%)
  local copies, waits for them, and re-layouts  214 us (21%)
  other arithmetic  102 us (10%)
  matrix products  70.5 us (7%)
  starting transfers between devices  35.1 us (3%)
  between operations  19.5 us (2%)
    reduce_scatter x4, waiting for transfers between devices, on_device(): lax.psum_scatter(embedded, 'led', scatter_dimension=1, tiled=True)  215 us
    all_to_all x4, waiting for transfers between devices, on_device(): lax.all_to_all(stacked, 'row', split_axis=1, concat_axis=2, tiled=True)  149 us
    all_gather x4, waiting for transfers between devices, on_device(): regions.append(lax.all_gather(part, 'led', axis=1, tiled=True))  131 us
    all_to_all x4, waiting for transfers between devices, on_device(): lax.all_to_all(piece, 'row', split_axis=2, concat_axis=1, tiled=True)  96.2 us
    dot_general x8, matrix products, row_transform(): middle = jnp.dot(table, stacked, precision=HIGHEST_PRECISION)  49.3 us
    dynamic_update_slice x4, local copies, waits for them, and re-layouts, on_device(): lax.dynamic_update_slice_in_dim(embedded, jnp.stack([upd_re, upd_im]), ro...  28.2 us
    another operation x4, local copies, waits for them, and re-layouts, on_device(): stacked = jnp.stack([half_re, half_im])  28 us
    mul x1, other arithmetic, pupil_at(): return (weight * jnp.cos(phases), weight * jnp.sin(phases))  24.6 us
  transfers between devices with their start and end apart: 16, of which 16 were waited for; matrix products, arithmetic and copies ran while one was open for 21% of the time, Pallas kernels for 0%

profile of v2, /device:TPU:0, one launch (start us, length us, event | category | flops | bytes accessed | tf_op | source)
XLA Modules:
  0.0 1036.1 jit_solution(13660951631757972791)
XLA Ops:
  27.6 24.6 %select_multiply_fusion = (f32[2048,512]{1,0:T(8,128)}, f32[2048,512]{1,0:T(8,128)}) fusion(f32[]{:T(128)} %bitcast.6, f32[512]{0:T(512)S(1)} %get-tuple-element.199, f32[2048]{0:T(1024)S(1)} %get-tuple-element.202, f32[512]{0:T(512)S(1)} %get-tuple-element.200, f32[2048]{0:T(1024)S(1)} %convert_multiply_fusion.1, f32[]{:T(128)} %bitcast.3, f32[]{:T(128)} %bitcast.2, ...), kind=kLoop, calls=%fused_computation.6 | loop fusion | flops 27262976 | bytes 8429584 | tf_op jit(solution)/shard_map/mul | solution.py:29
  54.1 12.4 %all-gather.5.cloned.1.call-done = f32[2,4096,128]{2,1,0:T(8,128)} async-done(((f32[2,1024,128]{2,1,0:T(8,128)}), f32[2,4096,128]{2,1,0:T(8,128)}) %all-gather.5.cloned.1.call-update) | async-done | bytes 4194320 | tf_op jit(solution)/shard_map/all_gather | solution.py:160
  77.5 43.4 %all-gather.7.cloned.1.call-done = f32[2,4096,128]{2,1,0:T(8,128)} async-done(((f32[2,1024,128]{2,1,0:T(8,128)}), f32[2,4096,128]{2,1,0:T(8,128)}) %all-gather.7.cloned.1.call-update) | async-done | bytes 4194320 | tf_op jit(solution)/shard_map/all_gather | solution.py:160
  137.7 37.6 %all-gather.9.cloned.1.call-done = f32[2,4096,128]{2,1,0:T(8,128)} async-done(((f32[2,1024,128]{2,1,0:T(8,128)}), f32[2,4096,128]{2,1,0:T(8,128)}) %all-gather.9.cloned.1.call-update) | async-done | bytes 4194320 | tf_op jit(solution)/shard_map/all_gather | solution.py:160
  182.5 7.2 fusion.40
  192.5 37.1 %all-gather.11.cloned.1.call-done = f32[2,4096,128]{2,1,0:T(8,128)} async-done(((f32[2,1024,128]{2,1,0:T(8,128)}), f32[2,4096,128]{2,1,0:T(8,128)}) %all-gather.11.cloned.1.call-update) | async-done | bytes 4194320 | tf_op jit(solution)/shard_map/all_gather | solution.py:160
  244.6 8.5 copy.137
  263.4 43.7 %all-to-all-done.3 = f32[2,2048,128]{2,0,1:T(2,128)} async-done(((f32[2,2048,128]{2,0,1:T(2,128)}), f32[2,2048,128]{2,0,1:T(2,128)}, u32[]{:S(2)}, u32[]{:S(2)}) %all-to-all-start.3) | async-done | bytes 2097184 | tf_op jit(solution)/shard_map/all_to_all | solution.py:172
  317.0 43.5 %all-to-all-done.2 = f32[2,2048,128]{2,0,1:T(2,128)} async-done(((f32[2,2048,128]{2,0,1:T(2,128)}), f32[2,2048,128]{2,0,1:T(2,128)}, u32[]{:S(2)}, u32[]{:S(2)}) %all-to-all-start.2) | async-done | bytes 2097184 | tf_op jit(solution)/shard_map/all_to_all | solution.py:172
  364.9 8.5 copy.131
  373.5 40.5 %all-to-all-done.1 = f32[2,2048,128]{2,0,1:T(2,128)} async-done(((f32[2,2048,128]{2,0,1:T(2,128)}), f32[2,2048,128]{2,0,1:T(2,128)}, u32[]{:S(2)}, u32[]{:S(2)}) %all-to-all-start.1) | async-done | bytes 2097184 | tf_op jit(solution)/shard_map/all_to_all | solution.py:172
  446.6 21.2 %all-to-all-done = f32[2,2048,128]{2,0,1:T(2,128)} async-done(((f32[2,2048,128]{2,0,1:T(2,128)}), f32[2,2048,128]{2,0,1:T(2,128)}, u32[]{:S(2)}, u32[]{:S(2)}) %all-to-all-start) | async-done | bytes 2097184 | tf_op jit(solution)/shard_map/all_to_all | solution.py:172
  475.5 8.7 copy.139
  533.0 12.5 %dynamic_update_slice.15 = f32[2,256,4096]{1,2,0:T(8,128)} dynamic-update-slice(f32[2,256,4096]{1,2,0:T(8,128)} %broadcast_in_dim.12, f32[2,256,2048]{1,2,0:T(8,128)} %bitcast.229, s32[]{:T(128)} %constant.193.clone.1, s32[]{:T(128)} %constant.193.clone.1, s32[]{:T(128)S(6)} %select_n.445) | dynamic-update-slice | bytes 8388612 | tf_op jit(solution)/shard_map/dynamic_update_slice | solution.py:191
  563.2 44.4 %all-to-all-done.4 = f32[2,256,1024]{1,0,2:T(2,128)S(1)} async-done(((f32[2,256,1024]{1,0,2:T(2,128)}), f32[2,256,1024]{1,0,2:T(2,128)S(1)}, u32[]{:S(2)}, u32[]{:S(2)}) %all-to-all-start.4) | async-done | bytes 2097184 | tf_op jit(solution)/shard_map/all_to_all | solution.py:198
  637.0 24.5 %all-to-all-done.5 = f32[2,256,1024]{1,0,2:T(2,128)S(1)} async-done(((f32[2,256,1024]{1,0,2:T(2,128)}), f32[2,256,1024]{1,0,2:T(2,128)S(1)}, u32[]{:S(2)}, u32[]{:S(2)}) %all-to-all-start.5) | async-done | bytes 2097184 | tf_op jit(solution)/shard_map/all_to_all | solution.py:198
  682.4 7.1 dynamic_update_slice.16
  701.4 13.7 %all-to-all-done.6 = f32[2,256,1024]{1,0,2:T(2,128)} async-done(((f32[2,256,1024]{1,0,2:T(2,128)}), f32[2,256,1024]{1,0,2:T(2,128)}, u32[]{:S(2)}, u32[]{:S(2)}) %all-to-all-start.6) | async-done | bytes 2097184 | tf_op jit(solution)/shard_map/all_to_all | solution.py:198
  754.9 13.6 %all-to-all-done.7 = f32[2,256,1024]{1,0,2:T(2,128)} async-done(((f32[2,256,1024]{1,0,2:T(2,128)}), f32[2,256,1024]{1,0,2:T(2,128)}, u32[]{:S(2)}, u32[]{:S(2)}) %all-to-all-start.7) | async-done | bytes 2097184 | tf_op jit(solution)/shard_map/all_to_all | solution.py:198
  775.8 7.1 dynamic_update_slice.18
  807.8 48.6 %reduce-scatter.11.cloned.1.call-done = f32[2,1024,128]{2,1,0:T(8,128)} async-done(((f32[2,4096,128]{2,1,0:T(8,128)}), f32[2,1024,128]{2,1,0:T(8,128)}) %reduce-scatter.11.cloned.1.call-update) | async-done | bytes 1048592 | tf_op jit(solution)/shard_map/reduce_scatter | solution.py:212
  856.4 55.4 %reduce-scatter.9.cloned.1.call-done = f32[2,1024,128]{2,1,0:T(8,128)} async-done(((f32[2,4096,128]{2,1,0:T(8,128)}), f32[2,1024,128]{2,1,0:T(8,128)}) %reduce-scatter.9.cloned.1.call-update) | async-done | bytes 1048592 | tf_op jit(solution)/shard_map/reduce_scatter | solution.py:212
  911.8 55.6 %reduce-scatter.7.cloned.1.call-done = f32[2,1024,128]{2,1,0:T(8,128)} async-done(((f32[2,4096,128]{2,1,0:T(8,128)}), f32[2,1024,128]{2,1,0:T(8,128)}) %reduce-scatter.7.cloned.1.call-update) | async-done | bytes 1048592 | tf_op jit(solution)/shard_map/reduce_scatter | solution.py:212
  967.4 55.6 %reduce-scatter.5.cloned.1.call-done = f32[2,1024,128]{2,1,0:T(8,128)} async-done(((f32[2,4096,128]{2,1,0:T(8,128)}), f32[2,1024,128]{2,1,0:T(8,128)}) %reduce-scatter.5.cloned.1.call-update) | async-done | bytes 1048592 | tf_op jit(solution)/shard_map/reduce_scatter | solution.py:212
  (233 shorter events, 341.6 us)
Async XLA Ops:
  6.5 59.9 %all-gather.5.cloned.1.call-start = ((), (), s32[]{:S(2)}) async-start(), calls=%async_computation.12 | async-start | bytes 5242880 | tf_op jit(solution)/shard_map/all_gather | solution.py:160
  10.9 14.1 %copy-start.21 = (f32[6]{0:T(128)S(1)}, f32[6]{0:T(128)}, u32[]{:S(2)}) copy-start(f32[6]{0:T(128)} %param.7) | copy-start | bytes 76
  10.9 110.0 %all-gather.7.cloned.1.call-start = ((), (), s32[]{:S(2)}) async-start(), calls=%async_computation.13 | async-start | bytes 5242880 | tf_op jit(solution)/shard_map/all_gather | solution.py:160
  11.7 163.7 %all-gather.9.cloned.1.call-start = ((), (), s32[]{:S(2)}) async-start(), calls=%async_computation.14 | async-start | bytes 5242880 | tf_op jit(solution)/shard_map/all_gather | solution.py:160
  12.4 217.2 %all-gather.11.cloned.1.call-start = ((), (), s32[]{:S(2)}) async-start(), calls=%async_computation.15 | async-start | bytes 5242880 | tf_op jit(solution)/shard_map/all_gather | solution.py:160
  20.2 50.1 %copy-start.15 = (f32[512,512]{1,0:T(8,128)}, f32[512,512]{1,0:T(8,128)S(1)}, u32[]{:S(2)}) copy-start(f32[512,512]{1,0:T(8,128)S(1)} %get-tuple-element.203) | copy-start | bytes 3145732
  253.2 54.0 %all-to-all-start.3 = ((f32[2,2048,128]{2,0,1:T(2,128)}), f32[2,2048,128]{2,0,1:T(2,128)}, u32[]{:S(2)}, u32[]{:S(2)}) async-start(f32[2,2048,128]{2,0,1:T(2,128)} %copy.137), calls=%async_computation.3 | async-start | bytes 4194304 | tf_op jit(solution)/shard_map/all_to_all | solution.py:172
  307.1 53.4 %all-to-all-start.2 = ((f32[2,2048,128]{2,0,1:T(2,128)}), f32[2,2048,128]{2,0,1:T(2,128)}, u32[]{:S(2)}, u32[]{:S(2)}) async-start(f32[2,2048,128]{2,0,1:T(2,128)} %copy.135), calls=%async_computation.2 | async-start | bytes 4194304 | tf_op jit(solution)/shard_map/all_to_all | solution.py:172
  360.5 53.4 %all-to-all-start.1 = ((f32[2,2048,128]{2,0,1:T(2,128)}), f32[2,2048,128]{2,0,1:T(2,128)}, u32[]{:S(2)}, u32[]{:S(2)}) async-start(f32[2,2048,128]{2,0,1:T(2,128)} %copy.133), calls=%async_computation.1 | async-start | bytes 4194304 | tf_op jit(solution)/shard_map/all_to_all | solution.py:172
  413.9 53.8 %all-to-all-start = ((f32[2,2048,128]{2,0,1:T(2,128)}), f32[2,2048,128]{2,0,1:T(2,128)}, u32[]{:S(2)}, u32[]{:S(2)}) async-start(f32[2,2048,128]{2,0,1:T(2,128)} %copy.131), calls=%async_computation | async-start | bytes 4194304 | tf_op jit(solution)/shard_map/all_to_all | solution.py:172
  494.0 6.0 copy-start.8
  514.1 5.7 copy-start.7
  554.6 53.0 %all-to-all-start.4 = ((f32[2,256,1024]{1,0,2:T(2,128)}), f32[2,256,1024]{1,0,2:T(2,128)S(1)}, u32[]{:S(2)}, u32[]{:S(2)}) async-start(f32[2,256,1024]{1,0,2:T(2,128)} %copy.152), calls=%async_computation.4 | async-start | bytes 4194304 | tf_op jit(solution)/shard_map/all_to_all | solution.py:198
  608.9 52.6 %all-to-all-start.5 = ((f32[2,256,1024]{1,0,2:T(2,128)}), f32[2,256,1024]{1,0,2:T(2,128)S(1)}, u32[]{:S(2)}, u32[]{:S(2)}) async-start(f32[2,256,1024]{1,0,2:T(2,128)} %copy.156), calls=%async_computation.6 | async-start | bytes 4194304 | tf_op jit(solution)/shard_map/all_to_all | solution.py:198
  612.6 14.5 %copy-start.12 = (f32[2,256,8,1,128]{1,4,3,2,0:T(8,128)S(1)}, f32[2,256,8,1,128]{1,4,3,2,0:T(8,128)}, u32[]{:S(2)}) copy-start(f32[2,256,8,1,128]{1,4,3,2,0:T(8,128)} %get-tuple-element.102) | copy-start | bytes 6291460
  622.3 7.6 copy-start.11
  661.5 53.6 %all-to-all-start.6 = ((f32[2,256,1024]{1,0,2:T(2,128)}), f32[2,256,1024]{1,0,2:T(2,128)}, u32[]{:S(2)}, u32[]{:S(2)}) async-start(f32[2,256,1024]{1,0,2:T(2,128)} %copy.159), calls=%async_computation.8 | async-start | bytes 4194304 | tf_op jit(solution)/shard_map/all_to_all | solution.py:198
  666.1 4.6 copy-start.16
  676.1 3.1 copy-start
  715.1 53.4 %all-to-all-start.7 = ((f32[2,256,1024]{1,0,2:T(2,128)}), f32[2,256,1024]{1,0,2:T(2,128)}, u32[]{:S(2)}, u32[]{:S(2)}) async-start(f32[2,256,1024]{1,0,2:T(2,128)} %copy.162), calls=%async_computation.10 | async-start | bytes 4194304 | tf_op jit(solution)/shard_map/all_to_all | solution.py:198
  719.5 136.9 %reduce-scatter.11.cloned.1.call-start = ((), (), s32[]{:S(2)}) async-start(), calls=%async_computation.19 | async-start | bytes 5242880 | tf_op jit(solution)/shard_map/reduce_scatter | solution.py:212
  805.7 106.1 %reduce-scatter.9.cloned.1.call-start = ((), (), s32[]{:S(2)}) async-start(), calls=%async_computation.18 | async-start | bytes 5242880 | tf_op jit(solution)/shard_map/reduce_scatter | solution.py:212
  806.3 161.1 %reduce-scatter.7.cloned.1.call-start = ((), (), s32[]{:S(2)}) async-start(), calls=%async_computation.17 | async-start | bytes 5242880 | tf_op jit(solution)/shard_map/reduce_scatter | solution.py:212
  807.1 215.9 %reduce-scatter.5.cloned.1.call-start = ((), (), s32[]{:S(2)}) async-start(), calls=%async_computation.16 | async-start | bytes 5242880 | tf_op jit(solution)/shard_map/reduce_scatter | solution.py:212
  (15 other events, 39.0 us)
Sparse Core Ops, SparseCore 0:
  11.0 55.3 all-gather.4
  68.3 52.5 all-gather.6
  122.7 52.5 all-gather.8
  177.0 52.5 all-gather.10
  805.8 50.4 reduce-scatter.10
  859.2 52.5 reduce-scatter.8
  914.8 52.5 reduce-scatter.6
  970.4 52.5 reduce-scatter.4

commit v3 on v2

--- a/solution.py
+++ b/solution.py
@@ -7,7 +7,7 @@
 
 
 SOFTENING = 0.1
-HIGHEST_PRECISION = lax.Precision.HIGH
+HIGHEST_PRECISION = lax.Precision.HIGHEST
 CHUNKS = 4
 
 
@@ -144,7 +144,6 @@
     row_shift = offsets[led_index, 0]
     col_shift = offsets[led_index, 1]
     measured = amplitudes[0]
-    shape_cols = (2, block_rows, outer_cols, row_count)
     row_ids = jnp.arange(window, dtype=jnp.int32)[:, None]
 
     col_ids = (row_index * size_cols + jnp.arange(size_cols, dtype=jnp.int32))[None, :]
@@ -172,30 +171,48 @@
         spread = lax.all_to_all(stacked, "row", split_axis=1, concat_axis=2, tiled=True)
         spreads.append(spread.reshape(2, block_rows, row_count, width))
     spread_all = jnp.stack(spreads, axis=3).reshape(2, block_rows, row_count * size_cols)
-    window_part = lax.dynamic_slice_in_dim(spread_all, col_shift, window, 2)
-    field = transform(
-        window_part.reshape(shape_cols), "ytr", "ykr", "yjk", outer_cols, row_count, 1.0
-    )
-    field = field.reshape(2, block_rows, window)
-    diff_re, diff_im = correct(field[0], field[1], measured)
-    back = transform(
-        jnp.stack([diff_re, diff_im]).reshape(shape_cols),
-        "ytr",
-        "ykr",
-        "yjk",
-        outer_cols,
-        row_count,
-        -1.0,
-    )
-    padded = jnp.zeros((2, block_rows, row_count * size_cols), jnp.float32)
-    padded = lax.dynamic_update_slice_in_dim(
-        padded, back.reshape(2, block_rows, window), col_shift, 2
-    )
-    padded = padded.reshape(2, block_rows, row_count, chunks, width)
-    gathered_all = []
-    for chunk in range(chunks):
-        piece = padded[:, :, :, chunk, :].reshape(2, block_rows, row_count * width)
-        gathered_all.append(lax.all_to_all(piece, "row", split_axis=2, concat_axis=1, tiled=True))
+    halves = 2 if block_rows % 16 == 0 else 1
+    half_rows = block_rows // halves
+    shape_half = (2, half_rows, outer_cols, row_count)
+    returned = []
+    previous = None
+    for half in range(halves):
+        rows_part = spread_all[:, half * half_rows:(half + 1) * half_rows]
+        if previous is not None:
+            rows_part, _ = lax.optimization_barrier((rows_part, previous))
+        window_part = lax.dynamic_slice_in_dim(rows_part, col_shift, window, 2)
+        field = transform(
+            window_part.reshape(shape_half), "ytr", "ykr", "yjk", outer_cols, row_count, 1.0
+        )
+        field = field.reshape(2, half_rows, window)
+        diff_re, diff_im = correct(
+            field[0], field[1], measured[half * half_rows:(half + 1) * half_rows]
+        )
+        back = transform(
+            jnp.stack([diff_re, diff_im]).reshape(shape_half),
+            "ytr",
+            "ykr",
+            "yjk",
+            outer_cols,
+            row_count,
+            -1.0,
+        )
+        padded = jnp.zeros((2, half_rows, row_count * size_cols), jnp.float32)
+        padded = lax.dynamic_update_slice_in_dim(
+            padded, back.reshape(2, half_rows, window), col_shift, 2
+        )
+        previous = padded
+        padded = padded.reshape(2, half_rows, row_count, chunks, width)
+        pieces = []
+        for chunk in range(chunks):
+            piece = padded[:, :, :, chunk, :].reshape(2, half_rows, row_count * width)
+            got = lax.all_to_all(piece, "row", split_axis=2, concat_axis=1, tiled=True)
+            pieces.append(got.reshape(2, row_count, half_rows, width))
+        returned.append(pieces)
+    gathered_all = [
+        jnp.stack([returned[h][c] for h in range(halves)], axis=2).reshape(2, window, width)
+        for c in range(chunks)
+    ]
     results = []
     for chunk in range(chunks):
         gathered = gathered_all[chunk]

time: 1040 us -> 1130 us (1.087)
  matrix products: 70.5 us -> 121 us
  other arithmetic: 102 us -> 120 us
  starting transfers between devices: 35.1 us -> 51.8 us
  waiting for transfers between devices: 595 us -> 582 us
    dot_general x8, matrix products: 49.3 us -> 81.7 us  [row_transform(): middle = jnp.dot(table, stacked, precision=HIGHEST_PRECISION)]
    another operation x10 -> x23, local copies, waits for them, and re-layouts: 29.3 us -> 52 us  [the longest x8 16.9 us: on_device(): piece = padded[:, :, :, chunk, :].reshape(2, half_rows, row_count * width)]
    all_to_all x4 -> x8, starting transfers between devices: 16.5 us -> 33.8 us  [on_device(): got = lax.all_to_all(piece, 'row', split_axis=2, concat_axis=1, tiled=True)]
    all_gather x4, waiting for transfers between devices: 131 us -> 119 us  [on_device(): regions.append(lax.all_gather(part, 'led', axis=1, tiled=True))]
    all_to_all x4 -> x8, waiting for transfers between devices: 96.2 us -> 102 us  [on_device(): got = lax.all_to_all(piece, 'row', split_axis=2, concat_axis=1, tiled=True)]
  transfers between devices with their start and end apart: 16 -> 20, of which waited for: 16 -> 18; matrix products, arithmetic and copies ran while one was open for 21% -> 24% of each run, Pallas kernels for 0% -> 0%
where the time goes in v3:
time: 1130 us; the launch traced here: 1120 us
  waiting for transfers between devices  582 us (52%)
  local copies, waits for them, and re-layouts  222 us (20%)
  matrix products  121 us (11%)
  other arithmetic  120 us (11%)
  starting transfers between devices  51.8 us (5%)
  between operations  19.9 us (2%)
    reduce_scatter x4, waiting for transfers between devices, on_device(): lax.psum_scatter(embedded, 'led', scatter_dimension=1, tiled=True)  215 us
    all_to_all x4, waiting for transfers between devices, on_device(): lax.all_to_all(stacked, 'row', split_axis=1, concat_axis=2, tiled=True)  143 us
    all_gather x4, waiting for transfers between devices, on_device(): regions.append(lax.all_gather(part, 'led', axis=1, tiled=True))  119 us
    all_to_all x8, waiting for transfers between devices, on_device(): got = lax.all_to_all(piece, 'row', split_axis=2, concat_axis=1, tiled=True)  102 us
    dot_general x8, matrix products, row_transform(): middle = jnp.dot(table, stacked, precision=HIGHEST_PRECISION)  81.7 us
    all_to_all x8, starting transfers between devices, on_device(): got = lax.all_to_all(piece, 'row', split_axis=2, concat_axis=1, tiled=True)  33.8 us
    dynamic_update_slice x4, local copies, waits for them, and re-layouts, on_device(): lax.dynamic_update_slice_in_dim(embedded, jnp.stack([upd_re, upd_im]), ro...  28.2 us
    another operation x4, local copies, waits for them, and re-layouts, on_device(): stacked = jnp.stack([half_re, half_im])  28.1 us
  transfers between devices with their start and end apart: 20, of which 18 were waited for; matrix products, arithmetic and copies ran while one was open for 24% of the time, Pallas kernels for 0%

profile of v3, /device:TPU:0, one launch (start us, length us, event | category | flops | bytes accessed | tf_op | source)
XLA Modules:
  0.0 1116.6 jit_solution(15968035960076595922)
XLA Ops:
  27.7 24.3 %select_multiply_fusion = (f32[2048,512]{1,0:T(8,128)}, f32[2048,512]{1,0:T(8,128)}) fusion(f32[]{:T(128)} %bitcast.6, f32[512]{0:T(512)S(1)} %get-tuple-element.211, f32[2048]{0:T(1024)S(1)} %get-tuple-element.214, f32[512]{0:T(512)S(1)} %get-tuple-element.212, f32[2048]{0:T(1024)S(1)} %convert_multiply_fusion.1, f32[]{:T(128)} %bitcast.3, f32[]{:T(128)} %bitcast.2, ...), kind=kLoop, calls=%fused_computation.6 | loop fusion | flops 27262976 | bytes 8429584 | tf_op jit(solution)/shard_map/mul | solution.py:29
  54.0 12.4 %all-gather.5.cloned.1.call-done = f32[2,4096,128]{2,1,0:T(8,128)} async-done(((f32[2,1024,128]{2,1,0:T(8,128)}), f32[2,4096,128]{2,1,0:T(8,128)}) %all-gather.5.cloned.1.call-update) | async-done | bytes 4194320 | tf_op jit(solution)/shard_map/all_gather | solution.py:159
  80.7 40.1 %all-gather.7.cloned.1.call-done = f32[2,4096,128]{2,1,0:T(8,128)} async-done(((f32[2,1024,128]{2,1,0:T(8,128)}), f32[2,4096,128]{2,1,0:T(8,128)}) %all-gather.7.cloned.1.call-update) | async-done | bytes 4194320 | tf_op jit(solution)/shard_map/all_gather | solution.py:159
  127.9 11.2 %fusion.23 = f32[1024,512]{1,0:T(8,128)S(1)} fusion(f32[512,512]{1,0:T(8,128)} %reshape.499, f32[512,512]{1,0:T(8,128)} %reshape.498, f32[512,512]{1,0:T(8,128)} %get-tuple-element.216, f32[512,512]{1,0:T(8,128)} %copy-done.29, f32[512,512]{1,0:T(8,128)} %fusion.118), kind=kOutput, calls=%fused_computation.35 | convolution fusion | flops 6446120960 | bytes 7340032 | tf_op jit(solution)/shard_map/dot_general | solution.py:96
  142.0 33.3 %all-gather.9.cloned.1.call-done = f32[2,4096,128]{2,1,0:T(8,128)} async-done(((f32[2,1024,128]{2,1,0:T(8,128)}), f32[2,4096,128]{2,1,0:T(8,128)}) %all-gather.9.cloned.1.call-update) | async-done | bytes 4194320 | tf_op jit(solution)/shard_map/all_gather | solution.py:159
  182.5 10.9 fusion.27
  196.3 33.3 %all-gather.11.cloned.1.call-done = f32[2,4096,128]{2,1,0:T(8,128)} async-done(((f32[2,1024,128]{2,1,0:T(8,128)}), f32[2,4096,128]{2,1,0:T(8,128)}) %all-gather.11.cloned.1.call-update) | async-done | bytes 4194320 | tf_op jit(solution)/shard_map/all_gather | solution.py:159
  236.8 10.2 fusion.31
  267.6 43.6 %all-to-all-done.3 = f32[2,2048,128]{2,0,1:T(2,128)} async-done(((f32[2,2048,128]{2,0,1:T(2,128)}), f32[2,2048,128]{2,0,1:T(2,128)}, u32[]{:S(2)}, u32[]{:S(2)}) %all-to-all-start.3) | async-done | bytes 2097184 | tf_op jit(solution)/shard_map/all_to_all | solution.py:171
  321.1 43.5 %all-to-all-done.2 = f32[2,2048,128]{2,0,1:T(2,128)} async-done(((f32[2,2048,128]{2,0,1:T(2,128)}), f32[2,2048,128]{2,0,1:T(2,128)}, u32[]{:S(2)}, u32[]{:S(2)}) %all-to-all-start.2) | async-done | bytes 2097184 | tf_op jit(solution)/shard_map/all_to_all | solution.py:171
  377.5 40.5 %all-to-all-done.1 = f32[2,2048,128]{2,0,1:T(2,128)} async-done(((f32[2,2048,128]{2,0,1:T(2,128)}), f32[2,2048,128]{2,0,1:T(2,128)}, u32[]{:S(2)}, u32[]{:S(2)}) %all-to-all-start.1) | async-done | bytes 2097184 | tf_op jit(solution)/shard_map/all_to_all | solution.py:171
  456.0 15.0 %all-to-all-done = f32[2,2048,128]{2,0,1:T(2,128)S(1)} async-done(((f32[2,2048,128]{2,0,1:T(2,128)}), f32[2,2048,128]{2,0,1:T(2,128)S(1)}, u32[]{:S(2)}, u32[]{:S(2)}) %all-to-all-start) | async-done | bytes 2097184 | tf_op jit(solution)/shard_map/all_to_all | solution.py:171
  587.5 20.7 %all-to-all-done.5 = f32[2,128,1024]{1,0,2:T(2,128)S(1)} async-done(((f32[2,128,1024]{1,0,2:T(2,128)}), f32[2,128,1024]{1,0,2:T(2,128)S(1)}, u32[]{:S(2)}, u32[]{:S(2)}) %all-to-all-start.5) | async-done | bytes 1048608 | tf_op jit(solution)/shard_map/all_to_all | solution.py:209
  613.6 24.7 %all-to-all-done.4 = f32[2,128,1024]{1,0,2:T(2,128)S(1)} async-done(((f32[2,128,1024]{1,0,2:T(2,128)}), f32[2,128,1024]{1,0,2:T(2,128)S(1)}, u32[]{:S(2)}, u32[]{:S(2)}) %all-to-all-start.4) | async-done | bytes 1048608 | tf_op jit(solution)/shard_map/all_to_all | solution.py:209
  646.1 23.5 %all-to-all-done.7 = f32[2,128,1024]{1,0,2:T(2,128)S(1)} async-done(((f32[2,128,1024]{1,0,2:T(2,128)}), f32[2,128,1024]{1,0,2:T(2,128)S(1)}, u32[]{:S(2)}, u32[]{:S(2)}) %all-to-all-start.7) | async-done | bytes 1048608 | tf_op jit(solution)/shard_map/all_to_all | solution.py:209
  703.9 10.3 fusion.41
  719.2 11.2 all-to-all-done.9
  756.7 10.2 fusion.45
  801.1 10.2 fusion.49
  823.9 20.6 %all-to-all-done.10 = f32[2,128,1024]{1,0,2:T(2,128)} async-done(((f32[2,128,1024]{1,0,2:T(2,128)}), f32[2,128,1024]{1,0,2:T(2,128)}, u32[]{:S(2)}, u32[]{:S(2)}) %all-to-all-start.10) | async-done | bytes 1048608 | tf_op jit(solution)/shard_map/all_to_all | solution.py:209
  888.3 48.6 %reduce-scatter.11.cloned.1.call-done = f32[2,1024,128]{2,1,0:T(8,128)} async-done(((f32[2,4096,128]{2,1,0:T(8,128)}), f32[2,1024,128]{2,1,0:T(8,128)}) %reduce-scatter.11.cloned.1.call-update) | async-done | bytes 1048592 | tf_op jit(solution)/shard_map/reduce_scatter | solution.py:229
  936.9 55.4 %reduce-scatter.9.cloned.1.call-done = f32[2,1024,128]{2,1,0:T(8,128)} async-done(((f32[2,4096,128]{2,1,0:T(8,128)}), f32[2,1024,128]{2,1,0:T(8,128)}) %reduce-scatter.9.cloned.1.call-update) | async-done | bytes 1048592 | tf_op jit(solution)/shard_map/reduce_scatter | solution.py:229
  992.4 55.6 %reduce-scatter.7.cloned.1.call-done = f32[2,1024,128]{2,1,0:T(8,128)} async-done(((f32[2,4096,128]{2,1,0:T(8,128)}), f32[2,1024,128]{2,1,0:T(8,128)}) %reduce-scatter.7.cloned.1.call-update) | async-done | bytes 1048592 | tf_op jit(solution)/shard_map/reduce_scatter | solution.py:229
  1047.9 55.6 %reduce-scatter.5.cloned.1.call-done = f32[2,1024,128]{2,1,0:T(8,128)} async-done(((f32[2,4096,128]{2,1,0:T(8,128)}), f32[2,1024,128]{2,1,0:T(8,128)}) %reduce-scatter.5.cloned.1.call-update) | async-done | bytes 1048592 | tf_op jit(solution)/shard_map/reduce_scatter | solution.py:229
  (293 shorter events, 431.8 us)
Async XLA Ops:
  6.5 59.9 %all-gather.5.cloned.1.call-start = ((), (), s32[]{:S(2)}) async-start(), calls=%async_computation.16 | async-start | bytes 5242880 | tf_op jit(solution)/shard_map/all_gather | solution.py:159
  10.9 14.2 %copy-start.32 = (f32[6]{0:T(128)S(1)}, f32[6]{0:T(128)}, u32[]{:S(2)}) copy-start(f32[6]{0:T(128)} %param.7) | copy-start | bytes 76
  10.9 109.9 %all-gather.7.cloned.1.call-start = ((), (), s32[]{:S(2)}) async-start(), calls=%async_computation.17 | async-start | bytes 5242880 | tf_op jit(solution)/shard_map/all_gather | solution.py:159
  11.7 163.6 %all-gather.9.cloned.1.call-start = ((), (), s32[]{:S(2)}) async-start(), calls=%async_computation.18 | async-start | bytes 5242880 | tf_op jit(solution)/shard_map/all_gather | solution.py:159
  12.4 217.2 %all-gather.11.cloned.1.call-start = ((), (), s32[]{:S(2)}) async-start(), calls=%async_computation.19 | async-start | bytes 5242880 | tf_op jit(solution)/shard_map/all_gather | solution.py:159
  20.3 50.0 %copy-start.29 = (f32[512,512]{1,0:T(8,128)}, f32[512,512]{1,0:T(8,128)S(1)}, u32[]{:S(2)}) copy-start(f32[512,512]{1,0:T(8,128)S(1)} %get-tuple-element.215) | copy-start | bytes 3145732
  257.2 54.0 %all-to-all-start.3 = ((f32[2,2048,128]{2,0,1:T(2,128)}), f32[2,2048,128]{2,0,1:T(2,128)}, u32[]{:S(2)}, u32[]{:S(2)}) async-start(f32[2,2048,128]{2,0,1:T(2,128)} %copy.142), calls=%async_computation.3 | async-start | bytes 4194304 | tf_op jit(solution)/shard_map/all_to_all | solution.py:171
  311.2 53.4 %all-to-all-start.2 = ((f32[2,2048,128]{2,0,1:T(2,128)}), f32[2,2048,128]{2,0,1:T(2,128)}, u32[]{:S(2)}, u32[]{:S(2)}) async-start(f32[2,2048,128]{2,0,1:T(2,128)} %copy.140), calls=%async_computation.2 | async-start | bytes 4194304 | tf_op jit(solution)/shard_map/all_to_all | solution.py:171
  364.6 53.4 %all-to-all-start.1 = ((f32[2,2048,128]{2,0,1:T(2,128)}), f32[2,2048,128]{2,0,1:T(2,128)}, u32[]{:S(2)}, u32[]{:S(2)}) async-start(f32[2,2048,128]{2,0,1:T(2,128)} %copy.138), calls=%async_computation.1 | async-start | bytes 4194304 | tf_op jit(solution)/shard_map/all_to_all | solution.py:171
  418.0 53.0 %all-to-all-start = ((f32[2,2048,128]{2,0,1:T(2,128)}), f32[2,2048,128]{2,0,1:T(2,128)S(1)}, u32[]{:S(2)}, u32[]{:S(2)}) async-start(f32[2,2048,128]{2,0,1:T(2,128)} %copy.136), calls=%async_computation | async-start | bytes 4194304 | tf_op jit(solution)/shard_map/all_to_all | solution.py:171
  578.2 30.1 %all-to-all-start.5 = ((f32[2,128,1024]{1,0,2:T(2,128)}), f32[2,128,1024]{1,0,2:T(2,128)S(1)}, u32[]{:S(2)}, u32[]{:S(2)}) async-start(f32[2,128,1024]{1,0,2:T(2,128)} %copy.167), calls=%async_computation.5 | async-start | bytes 2097152 | tf_op jit(solution)/shard_map/all_to_all | solution.py:209
  608.2 30.1 %all-to-all-start.4 = ((f32[2,128,1024]{1,0,2:T(2,128)}), f32[2,128,1024]{1,0,2:T(2,128)S(1)}, u32[]{:S(2)}, u32[]{:S(2)}) async-start(f32[2,128,1024]{1,0,2:T(2,128)} %copy.155), calls=%async_computation.4 | async-start | bytes 2097152 | tf_op jit(solution)/shard_map/all_to_all | solution.py:209
  639.3 30.3 %all-to-all-start.7 = ((f32[2,128,1024]{1,0,2:T(2,128)}), f32[2,128,1024]{1,0,2:T(2,128)S(1)}, u32[]{:S(2)}, u32[]{:S(2)}) async-start(f32[2,128,1024]{1,0,2:T(2,128)} %copy.173), calls=%async_computation.8 | async-start | bytes 2097152 | tf_op jit(solution)/shard_map/all_to_all | solution.py:209
  669.6 30.1 %all-to-all-start.6 = ((f32[2,128,1024]{1,0,2:T(2,128)}), f32[2,128,1024]{1,0,2:T(2,128)S(1)}, u32[]{:S(2)}, u32[]{:S(2)}) async-start(f32[2,128,1024]{1,0,2:T(2,128)} %copy.171), calls=%async_computation.7 | async-start | bytes 2097152 | tf_op jit(solution)/shard_map/all_to_all | solution.py:209
  673.1 12.8 %copy-start.17 = (f32[2,128,8,1,128]{1,4,3,2,0:T(8,128)S(1)}, f32[2,128,8,1,128]{1,4,3,2,0:T(8,128)}, u32[]{:S(2)}) copy-start(f32[2,128,8,1,128]{1,4,3,2,0:T(8,128)} %get-tuple-element.107) | copy-start | bytes 3145732
  673.1 14.6 %copy-start.15 = (f32[2,128,8,1,128]{1,4,3,2,0:T(8,128)S(1)}, f32[2,128,8,1,128]{1,4,3,2,0:T(8,128)}, u32[]{:S(2)}) copy-start(f32[2,128,8,1,128]{1,4,3,2,0:T(8,128)} %get-tuple-element.110) | copy-start | bytes 3145732
  699.6 30.8 %all-to-all-start.9 = ((f32[2,128,1024]{1,0,2:T(2,128)}), f32[2,128,1024]{1,0,2:T(2,128)S(1)}, u32[]{:S(2)}, u32[]{:S(2)}) async-start(f32[2,128,1024]{1,0,2:T(2,128)} %copy.178), calls=%async_computation.11 | async-start | bytes 2097152 | tf_op jit(solution)/shard_map/all_to_all | solution.py:209
  730.4 39.2 %all-to-all-start.8 = ((f32[2,128,1024]{1,0,2:T(2,128)}), f32[2,128,1024]{1,0,2:T(2,128)}, u32[]{:S(2)}, u32[]{:S(2)}) async-start(f32[2,128,1024]{1,0,2:T(2,128)} %copy.176), calls=%async_computation.10 | async-start | bytes 2097152 | tf_op jit(solution)/shard_map/all_to_all | solution.py:209
  769.6 43.2 %all-to-all-start.11 = ((f32[2,128,1024]{1,0,2:T(2,128)}), f32[2,128,1024]{1,0,2:T(2,128)S(1)}, u32[]{:S(2)}, u32[]{:S(2)}) async-start(f32[2,128,1024]{1,0,2:T(2,128)} %copy.183), calls=%async_computation.14 | async-start | bytes 2097152 | tf_op jit(solution)/shard_map/all_to_all | solution.py:209
  812.7 31.8 %all-to-all-start.10 = ((f32[2,128,1024]{1,0,2:T(2,128)}), f32[2,128,1024]{1,0,2:T(2,128)}, u32[]{:S(2)}, u32[]{:S(2)}) async-start(f32[2,128,1024]{1,0,2:T(2,128)} %copy.181), calls=%async_computation.13 | async-start | bytes 2097152 | tf_op jit(solution)/shard_map/all_to_all | solution.py:209
  817.8 119.1 %reduce-scatter.11.cloned.1.call-start = ((), (), s32[]{:S(2)}) async-start(), calls=%async_computation.23 | async-start | bytes 5242880 | tf_op jit(solution)/shard_map/reduce_scatter | solution.py:229
  886.3 106.1 %reduce-scatter.9.cloned.1.call-start = ((), (), s32[]{:S(2)}) async-start(), calls=%async_computation.22 | async-start | bytes 5242880 | tf_op jit(solution)/shard_map/reduce_scatter | solution.py:229
  886.8 161.1 %reduce-scatter.7.cloned.1.call-start = ((), (), s32[]{:S(2)}) async-start(), calls=%async_computation.21 | async-start | bytes 5242880 | tf_op jit(solution)/shard_map/reduce_scatter | solution.py:229
  887.6 215.9 %reduce-scatter.5.cloned.1.call-start = ((), (), s32[]{:S(2)}) async-start(), calls=%async_computation.20 | async-start | bytes 5242880 | tf_op jit(solution)/shard_map/reduce_scatter | solution.py:229
  (30 other events, 81.8 us)
Sparse Core Ops, SparseCore 0:
  11.1 55.2 all-gather.4
  68.2 52.5 all-gather.6
  122.7 52.5 all-gather.8
  177.0 52.5 all-gather.10
  886.4 50.4 reduce-scatter.10
  939.8 52.5 reduce-scatter.8
  995.3 52.5 reduce-scatter.6
  1050.9 52.5 reduce-scatter.4

commit v4 on v2

--- a/solution.py
+++ b/solution.py
@@ -7,7 +7,7 @@
 
 
 SOFTENING = 0.1
-HIGHEST_PRECISION = lax.Precision.HIGH
+HIGHEST_PRECISION = lax.Precision.HIGHEST
 CHUNKS = 4
 
 
@@ -27,40 +27,6 @@
     )
     weight = jnp.where(inside, 1.0, 0.0).astype(jnp.float32)
     return (weight * jnp.cos(phases), weight * jnp.sin(phases))
-
-
-def tables(outer_size, inner_size, direction):
-    length = outer_size * inner_size
-    angle_step = direction * 2.0 * math.pi / length
-    first_index = jnp.arange(outer_size, dtype=jnp.int32)
-    grid_first = first_index[:, None] * first_index[None, :] * inner_size % length
-    angles_first = grid_first.astype(jnp.float32) * angle_step
-    index_k = jnp.arange(outer_size, dtype=jnp.int32)[:, None, None]
-    index_r = jnp.arange(inner_size, dtype=jnp.int32)[None, :, None]
-    index_j = jnp.arange(inner_size, dtype=jnp.int32)[None, None, :]
-    grid_second = index_r * (index_k + outer_size * index_j) % length
-    angles_second = grid_second.astype(jnp.float32) * angle_step
-    return (
-        jnp.cos(angles_first),
-        jnp.sin(angles_first),
-        jnp.cos(angles_second),
-        jnp.sin(angles_second),
-    )
-
-
-def transform(paired, inputs, middle, output, outer_size, inner_size, direction):
-    first_re, first_im, second_re, second_im = tables(outer_size, inner_size, direction)
-    scaling = 1.0 / math.sqrt(outer_size * inner_size)
-    first_table = jnp.stack([jnp.stack([first_re, first_im]), jnp.stack([-first_im, first_re])])
-    second_table = (
-        jnp.stack([jnp.stack([second_re, second_im]), jnp.stack([-second_im, second_re])]) * scaling
-    )
-    middle_pair = jnp.einsum(
-        "p" + inputs + ",pqtk->q" + middle, paired, first_table, precision=HIGHEST_PRECISION
-    )
-    return jnp.einsum(
-        "p" + middle + ",pqkrj->q" + output, middle_pair, second_table, precision=HIGHEST_PRECISION
-    )
 
 
 def unit_times(value_re, value_im, turn):
@@ -122,6 +88,81 @@
     return jnp.concatenate(out_re, axis=0), jnp.concatenate(out_im, axis=0)
 
 
+def col_forward(x_re, x_im, direction, inner=8):
+    rows, length = x_re.shape
+    outer = length // inner
+    scaling = 1.0 / math.sqrt(length)
+    parts = [(x_re[:, r * outer:(r + 1) * outer], x_im[:, r * outer:(r + 1) * outer]) for r in range(inner)]
+    t_index = jnp.arange(outer, dtype=jnp.int32)
+    z_re = []
+    z_im = []
+    for j in range(inner):
+        acc_re = None
+        acc_im = None
+        for r in range(inner):
+            t_re, t_im = unit_times(parts[r][0], parts[r][1], direction * r * j / inner)
+            acc_re = t_re if acc_re is None else acc_re + t_re
+            acc_im = t_im if acc_im is None else acc_im + t_im
+        angle = (j * t_index % length).astype(jnp.float32) * (direction * 2.0 * math.pi / length)
+        tw_re = (jnp.cos(angle) * scaling)[None, :]
+        tw_im = (jnp.sin(angle) * scaling)[None, :]
+        z_re.append(acc_re * tw_re - acc_im * tw_im)
+        z_im.append(acc_re * tw_im + acc_im * tw_re)
+    stacked = jnp.concatenate(
+        [jnp.stack(z_re, axis=1).reshape(rows * inner, outer), jnp.stack(z_im, axis=1).reshape(rows * inner, outer)],
+        axis=1,
+    )
+    grid = (t_index[:, None] * t_index[None, :]) % outer
+    angles = grid.astype(jnp.float32) * (direction * 2.0 * math.pi / outer)
+    cos_t = jnp.cos(angles)
+    sin_t = jnp.sin(angles)
+    table = jnp.concatenate(
+        [jnp.concatenate([cos_t, sin_t], axis=1), jnp.concatenate([-sin_t, cos_t], axis=1)], axis=0
+    )
+    out = jnp.dot(stacked, table, precision=HIGHEST_PRECISION)
+    return out[:, :outer].reshape(rows, inner, outer), out[:, outer:].reshape(rows, inner, outer)
+
+
+def col_inverse(x_re, x_im, direction):
+    rows, inner, outer = x_re.shape
+    length = inner * outer
+    scaling = 1.0 / math.sqrt(length)
+    t_index = jnp.arange(outer, dtype=jnp.int32)
+    grid = (t_index[:, None] * t_index[None, :]) % outer
+    angles = grid.astype(jnp.float32) * (direction * 2.0 * math.pi / outer)
+    cos_t = jnp.cos(angles)
+    sin_t = jnp.sin(angles)
+    table = jnp.concatenate(
+        [jnp.concatenate([cos_t, sin_t], axis=1), jnp.concatenate([-sin_t, cos_t], axis=1)], axis=0
+    )
+    stacked = jnp.concatenate(
+        [x_re.reshape(rows * inner, outer), x_im.reshape(rows * inner, outer)], axis=1
+    )
+    mid = jnp.dot(stacked, table, precision=HIGHEST_PRECISION)
+    mid_re = mid[:, :outer].reshape(rows, inner, outer)
+    mid_im = mid[:, outer:].reshape(rows, inner, outer)
+    twiddled = []
+    for j in range(inner):
+        angle = (j * t_index % length).astype(jnp.float32) * (direction * 2.0 * math.pi / length)
+        tw_re = (jnp.cos(angle) * scaling)[None, :]
+        tw_im = (jnp.sin(angle) * scaling)[None, :]
+        m_re = mid_re[:, j]
+        m_im = mid_im[:, j]
+        twiddled.append((m_re * tw_re - m_im * tw_im, m_re * tw_im + m_im * tw_re))
+    out_re = []
+    out_im = []
+    for r in range(inner):
+        acc_re = None
+        acc_im = None
+        for j in range(inner):
+            t_re, t_im = unit_times(twiddled[j][0], twiddled[j][1], direction * r * j / inner)
+            acc_re = t_re if acc_re is None else acc_re + t_re
+            acc_im = t_im if acc_im is None else acc_im + t_im
+        out_re.append(acc_re)
+        out_im.append(acc_im)
+    return jnp.concatenate(out_re, axis=1), jnp.concatenate(out_im, axis=1)
+
+
 def correct(field_re, field_im, measured):
     magnitude = jnp.sqrt(field_re * field_re + field_im * field_im + SOFTENING)
     factor = measured / magnitude
@@ -138,13 +179,11 @@
     window = amplitudes.shape[2]
     centre = window // 2
     block_rows = window // row_count
-    outer_cols = window // row_count
     chunks = max(1, min(CHUNKS, size_cols // 128))
     width = size_cols // chunks
     row_shift = offsets[led_index, 0]
     col_shift = offsets[led_index, 1]
     measured = amplitudes[0]
-    shape_cols = (2, block_rows, outer_cols, row_count)
     row_ids = jnp.arange(window, dtype=jnp.int32)[:, None]
 
     col_ids = (row_index * size_cols + jnp.arange(size_cols, dtype=jnp.int32))[None, :]
@@ -173,20 +212,12 @@
         spreads.append(spread.reshape(2, block_rows, row_count, width))
     spread_all = jnp.stack(spreads, axis=3).reshape(2, block_rows, row_count * size_cols)
     window_part = lax.dynamic_slice_in_dim(spread_all, col_shift, window, 2)
-    field = transform(
-        window_part.reshape(shape_cols), "ytr", "ykr", "yjk", outer_cols, row_count, 1.0
-    )
-    field = field.reshape(2, block_rows, window)
-    diff_re, diff_im = correct(field[0], field[1], measured)
-    back = transform(
-        jnp.stack([diff_re, diff_im]).reshape(shape_cols),
-        "ytr",
-        "ykr",
-        "yjk",
-        outer_cols,
-        row_count,
-        -1.0,
-    )
+    field_re, field_im = col_forward(window_part[0], window_part[1], 1.0)
+    inner_cols = field_re.shape[1]
+    measured_perm = measured.reshape(block_rows, window // inner_cols, inner_cols).transpose(0, 2, 1)
+    diff_re, diff_im = correct(field_re, field_im, measured_perm)
+    back_re, back_im = col_inverse(diff_re, diff_im, -1.0)
+    back = jnp.stack([back_re, back_im])
     padded = jnp.zeros((2, block_rows, row_count * size_cols), jnp.float32)
     padded = lax.dynamic_update_slice_in_dim(
         padded, back.reshape(2, block_rows, window), col_shift, 2

time: 1040 us -> 1090 us (1.048)
  matrix products: 70.5 us -> 94.9 us
  other arithmetic: 102 us -> 119 us
  local copies, waits for them, and re-layouts: 214 us -> 230 us
  waiting for transfers between devices: 595 us -> 582 us
    dot_general x8, matrix products: 49.3 us -> 76.6 us  [row_transform(): middle = jnp.dot(table, stacked, precision=HIGHEST_PRECISION)]
    unnamed x47 -> x83, local copies, waits for them, and re-layouts: 12 us -> 28.8 us
    unnamed x0 -> x26, other arithmetic: none -> 12.2 us
    all_gather x4, waiting for transfers between devices: 131 us -> 119 us  [on_device(): regions.append(lax.all_gather(part, 'led', axis=1, tiled=True))]
where the time goes in v4:
time: 1090 us; the launch traced here: 1080 us
  waiting for transfers between devices  582 us (53%)
  local copies, waits for them, and re-layouts  230 us (21%)
  other arithmetic  119 us (11%)
  matrix products  94.9 us (9%)
  starting transfers between devices  34.7 us (3%)
  between operations  19.7 us (2%)
    reduce_scatter x4, waiting for transfers between devices, on_device(): lax.psum_scatter(embedded, 'led', scatter_dimension=1, tiled=True)  215 us
    all_to_all x4, waiting for transfers between devices, on_device(): lax.all_to_all(stacked, 'row', split_axis=1, concat_axis=2, tiled=True)  158 us
    all_gather x4, waiting for transfers between devices, on_device(): regions.append(lax.all_gather(part, 'led', axis=1, tiled=True))  119 us
    all_to_all x4, waiting for transfers between devices, on_device(): lax.all_to_all(piece, 'row', split_axis=2, concat_axis=1, tiled=True)  86.4 us
    dot_general x8, matrix products, row_transform(): middle = jnp.dot(table, stacked, precision=HIGHEST_PRECISION)  76.6 us
    unnamed x83, local copies, waits for them, and re-layouts  28.8 us
    dynamic_update_slice x4, local copies, waits for them, and re-layouts, on_device(): lax.dynamic_update_slice_in_dim(embedded, jnp.stack([upd_re, upd_im]), ro...  28.3 us
    another operation x4, local copies, waits for them, and re-layouts, on_device(): stacked = jnp.stack([half_re, half_im])  28.1 us
  transfers between devices with their start and end apart: 16, of which 16 were waited for; matrix products, arithmetic and copies ran while one was open for 21% of the time, Pallas kernels for 0%

profile of v4, /device:TPU:0, one launch (start us, length us, event | category | flops | bytes accessed | tf_op | source)
XLA Modules:
  0.0 1080.9 jit_solution(14732510037829152657)
XLA Ops:
  27.5 24.1 %select_multiply_fusion = (f32[2048,512]{1,0:T(8,128)}, f32[2048,512]{1,0:T(8,128)}) fusion(f32[]{:T(128)} %bitcast.6, f32[512]{0:T(512)S(1)} %get-tuple-element.277, f32[2048]{0:T(1024)S(1)} %get-tuple-element.280, f32[512]{0:T(512)S(1)} %get-tuple-element.278, f32[2048]{0:T(1024)S(1)} %convert_multiply_fusion.1, f32[]{:T(128)} %bitcast.3, f32[]{:T(128)} %bitcast.2, ...), kind=kLoop, calls=%fused_computation.6 | loop fusion | flops 27262976 | bytes 8429584 | tf_op jit(solution)/shard_map/mul | solution.py:29
  53.6 12.8 %all-gather.5.cloned.1.call-done = f32[2,4096,128]{2,1,0:T(8,128)} async-done(((f32[2,1024,128]{2,1,0:T(8,128)}), f32[2,4096,128]{2,1,0:T(8,128)}) %all-gather.5.cloned.1.call-update) | async-done | bytes 4194320 | tf_op jit(solution)/shard_map/all_gather | solution.py:199
  81.9 39.0 %all-gather.7.cloned.1.call-done = f32[2,4096,128]{2,1,0:T(8,128)} async-done(((f32[2,1024,128]{2,1,0:T(8,128)}), f32[2,4096,128]{2,1,0:T(8,128)}) %all-gather.7.cloned.1.call-update) | async-done | bytes 4194320 | tf_op jit(solution)/shard_map/all_gather | solution.py:199
  127.9 10.9 %fusion.23 = f32[1024,512]{1,0:T(8,128)S(1)} fusion(f32[512,512]{1,0:T(8,128)} %reshape.431, f32[512,512]{1,0:T(8,128)} %reshape.430, f32[512,512]{1,0:T(8,128)} %get-tuple-element.282, f32[512,512]{1,0:T(8,128)} %copy-done.20, f32[512,512]{1,0:T(8,128)} %fusion.71), kind=kOutput, calls=%fused_computation.44 | convolution fusion | flops 6446120960 | bytes 7340032 | tf_op jit(solution)/shard_map/dot_general | solution.py:62
  141.7 33.6 %all-gather.9.cloned.1.call-done = f32[2,4096,128]{2,1,0:T(8,128)} async-done(((f32[2,1024,128]{2,1,0:T(8,128)}), f32[2,4096,128]{2,1,0:T(8,128)}) %all-gather.9.cloned.1.call-update) | async-done | bytes 4194320 | tf_op jit(solution)/shard_map/all_gather | solution.py:199
  182.5 11.0 %fusion.27 = f32[1024,512]{1,0:T(8,128)S(1)} fusion(f32[512,512]{1,0:T(8,128)} %reshape.433, f32[512,512]{1,0:T(8,128)} %reshape.432, f32[512,512]{1,0:T(8,128)} %get-tuple-element.282, f32[512,512]{1,0:T(8,128)} %copy-done.20, f32[512,512]{1,0:T(8,128)} %fusion.71), kind=kOutput, calls=%fused_computation.49 | convolution fusion | flops 6446120960 | bytes 7340032 | tf_op jit(solution)/shard_map/dot_general | solution.py:62
  196.4 33.3 %all-gather.11.cloned.1.call-done = f32[2,4096,128]{2,1,0:T(8,128)} async-done(((f32[2,1024,128]{2,1,0:T(8,128)}), f32[2,4096,128]{2,1,0:T(8,128)}) %all-gather.11.cloned.1.call-update) | async-done | bytes 4194320 | tf_op jit(solution)/shard_map/all_gather | solution.py:199
  236.8 10.2 fusion.31
  267.7 43.6 %all-to-all-done.3 = f32[2,2048,128]{2,0,1:T(2,128)} async-done(((f32[2,2048,128]{2,0,1:T(2,128)}), f32[2,2048,128]{2,0,1:T(2,128)}, u32[]{:S(2)}, u32[]{:S(2)}) %all-to-all-start.3) | async-done | bytes 2097184 | tf_op jit(solution)/shard_map/all_to_all | solution.py:211
  321.2 43.5 %all-to-all-done.2 = f32[2,2048,128]{2,0,1:T(2,128)} async-done(((f32[2,2048,128]{2,0,1:T(2,128)}), f32[2,2048,128]{2,0,1:T(2,128)}, u32[]{:S(2)}, u32[]{:S(2)}) %all-to-all-start.2) | async-done | bytes 2097184 | tf_op jit(solution)/shard_map/all_to_all | solution.py:211
  377.6 40.5 %all-to-all-done.1 = f32[2,2048,128]{2,0,1:T(2,128)} async-done(((f32[2,2048,128]{2,0,1:T(2,128)}), f32[2,2048,128]{2,0,1:T(2,128)}, u32[]{:S(2)}, u32[]{:S(2)}) %all-to-all-start.1) | async-done | bytes 2097184 | tf_op jit(solution)/shard_map/all_to_all | solution.py:211
  441.0 30.7 %all-to-all-done = f32[2,2048,128]{2,0,1:T(2,128)} async-done(((f32[2,2048,128]{2,0,1:T(2,128)}), f32[2,2048,128]{2,0,1:T(2,128)}, u32[]{:S(2)}, u32[]{:S(2)}) %all-to-all-start) | async-done | bytes 2097184 | tf_op jit(solution)/shard_map/all_to_all | solution.py:211
  506.1 9.4 fusion.11
  573.5 12.6 %dynamic_update_slice.15 = f32[2,256,4096]{1,2,0:T(8,128)} dynamic-update-slice(f32[2,256,4096]{1,2,0:T(8,128)} %broadcast_in_dim.12, f32[2,256,2048]{1,2,0:T(8,128)} %pad_maximum_fusion.1, s32[]{:T(128)} %constant.287.clone.1, s32[]{:T(128)} %constant.287.clone.1, s32[]{:T(128)S(6)} %select_n.612) | dynamic-update-slice | bytes 8388612 | tf_op jit(solution)/shard_map/dynamic_update_slice | solution.py:222
  603.4 44.4 %all-to-all-done.4 = f32[2,256,1024]{1,0,2:T(2,128)S(1)} async-done(((f32[2,256,1024]{1,0,2:T(2,128)}), f32[2,256,1024]{1,0,2:T(2,128)S(1)}, u32[]{:S(2)}, u32[]{:S(2)}) %all-to-all-start.4) | async-done | bytes 2097184 | tf_op jit(solution)/shard_map/all_to_all | solution.py:229
  675.5 26.3 %all-to-all-done.5 = f32[2,256,1024]{1,0,2:T(2,128)S(1)} async-done(((f32[2,256,1024]{1,0,2:T(2,128)}), f32[2,256,1024]{1,0,2:T(2,128)S(1)}, u32[]{:S(2)}, u32[]{:S(2)}) %all-to-all-start.5) | async-done | bytes 2097184 | tf_op jit(solution)/shard_map/all_to_all | solution.py:229
  737.1 10.0 fusion.39
  785.5 8.9 fusion.43
  799.8 9.0 all-to-all-done.7
  827.7 8.9 fusion.47
  852.5 48.7 %reduce-scatter.11.cloned.1.call-done = f32[2,1024,128]{2,1,0:T(8,128)} async-done(((f32[2,4096,128]{2,1,0:T(8,128)}), f32[2,1024,128]{2,1,0:T(8,128)}) %reduce-scatter.11.cloned.1.call-update) | async-done | bytes 1048592 | tf_op jit(solution)/shard_map/reduce_scatter | solution.py:243
  901.2 55.5 %reduce-scatter.9.cloned.1.call-done = f32[2,1024,128]{2,1,0:T(8,128)} async-done(((f32[2,4096,128]{2,1,0:T(8,128)}), f32[2,1024,128]{2,1,0:T(8,128)}) %reduce-scatter.9.cloned.1.call-update) | async-done | bytes 1048592 | tf_op jit(solution)/shard_map/reduce_scatter | solution.py:243
  956.7 55.6 %reduce-scatter.7.cloned.1.call-done = f32[2,1024,128]{2,1,0:T(8,128)} async-done(((f32[2,4096,128]{2,1,0:T(8,128)}), f32[2,1024,128]{2,1,0:T(8,128)}) %reduce-scatter.7.cloned.1.call-update) | async-done | bytes 1048592 | tf_op jit(solution)/shard_map/reduce_scatter | solution.py:243
  1012.3 55.6 %reduce-scatter.5.cloned.1.call-done = f32[2,1024,128]{2,1,0:T(8,128)} async-done(((f32[2,4096,128]{2,1,0:T(8,128)}), f32[2,1024,128]{2,1,0:T(8,128)}) %reduce-scatter.5.cloned.1.call-update) | async-done | bytes 1048592 | tf_op jit(solution)/shard_map/reduce_scatter | solution.py:243
  (305 shorter events, 383.2 us)
Async XLA Ops:
  6.5 59.9 %all-gather.5.cloned.1.call-start = ((), (), s32[]{:S(2)}) async-start(), calls=%async_computation.12 | async-start | bytes 5242880 | tf_op jit(solution)/shard_map/all_gather | solution.py:199
  11.0 109.9 %all-gather.7.cloned.1.call-start = ((), (), s32[]{:S(2)}) async-start(), calls=%async_computation.13 | async-start | bytes 5242880 | tf_op jit(solution)/shard_map/all_gather | solution.py:199
  11.7 163.6 %all-gather.9.cloned.1.call-start = ((), (), s32[]{:S(2)}) async-start(), calls=%async_computation.14 | async-start | bytes 5242880 | tf_op jit(solution)/shard_map/all_gather | solution.py:199
  12.4 217.2 %all-gather.11.cloned.1.call-start = ((), (), s32[]{:S(2)}) async-start(), calls=%async_computation.15 | async-start | bytes 5242880 | tf_op jit(solution)/shard_map/all_gather | solution.py:199
  12.5 12.5 %copy-start.31 = (f32[6]{0:T(128)S(1)}, f32[6]{0:T(128)}, u32[]{:S(2)}) copy-start(f32[6]{0:T(128)} %param.7) | copy-start | bytes 76
  20.2 51.1 %copy-start.20 = (f32[512,512]{1,0:T(8,128)}, f32[512,512]{1,0:T(8,128)S(1)}, u32[]{:S(2)}) copy-start(f32[512,512]{1,0:T(8,128)S(1)} %get-tuple-element.281) | copy-start | bytes 3145732
  257.2 54.1 %all-to-all-start.3 = ((f32[2,2048,128]{2,0,1:T(2,128)}), f32[2,2048,128]{2,0,1:T(2,128)}, u32[]{:S(2)}, u32[]{:S(2)}) async-start(f32[2,2048,128]{2,0,1:T(2,128)} %copy.180), calls=%async_computation.3 | async-start | bytes 4194304 | tf_op jit(solution)/shard_map/all_to_all | solution.py:211
  311.3 53.4 %all-to-all-start.2 = ((f32[2,2048,128]{2,0,1:T(2,128)}), f32[2,2048,128]{2,0,1:T(2,128)}, u32[]{:S(2)}, u32[]{:S(2)}) async-start(f32[2,2048,128]{2,0,1:T(2,128)} %copy.178), calls=%async_computation.2 | async-start | bytes 4194304 | tf_op jit(solution)/shard_map/all_to_all | solution.py:211
  364.7 53.4 %all-to-all-start.1 = ((f32[2,2048,128]{2,0,1:T(2,128)}), f32[2,2048,128]{2,0,1:T(2,128)}, u32[]{:S(2)}, u32[]{:S(2)}) async-start(f32[2,2048,128]{2,0,1:T(2,128)} %copy.176), calls=%async_computation.1 | async-start | bytes 4194304 | tf_op jit(solution)/shard_map/all_to_all | solution.py:211
  418.1 53.6 %all-to-all-start = ((f32[2,2048,128]{2,0,1:T(2,128)}), f32[2,2048,128]{2,0,1:T(2,128)}, u32[]{:S(2)}, u32[]{:S(2)}) async-start(f32[2,2048,128]{2,0,1:T(2,128)} %copy.174), calls=%async_computation | async-start | bytes 4194304 | tf_op jit(solution)/shard_map/all_to_all | solution.py:211
  493.9 5.2 copy-start.14
  529.1 3.3 copy-start.7
  549.5 3.5 copy-start.19
  549.6 3.8 copy-start.18
  595.3 52.6 %all-to-all-start.4 = ((f32[2,256,1024]{1,0,2:T(2,128)}), f32[2,256,1024]{1,0,2:T(2,128)S(1)}, u32[]{:S(2)}, u32[]{:S(2)}) async-start(f32[2,256,1024]{1,0,2:T(2,128)} %copy.212), calls=%async_computation.4 | async-start | bytes 4194304 | tf_op jit(solution)/shard_map/all_to_all | solution.py:229
  649.2 52.6 %all-to-all-start.5 = ((f32[2,256,1024]{1,0,2:T(2,128)}), f32[2,256,1024]{1,0,2:T(2,128)S(1)}, u32[]{:S(2)}, u32[]{:S(2)}) async-start(f32[2,256,1024]{1,0,2:T(2,128)} %copy.216), calls=%async_computation.6 | async-start | bytes 4194304 | tf_op jit(solution)/shard_map/all_to_all | solution.py:229
  652.8 9.7 copy-start.11
  701.8 53.6 %all-to-all-start.6 = ((f32[2,256,1024]{1,0,2:T(2,128)}), f32[2,256,1024]{1,0,2:T(2,128)}, u32[]{:S(2)}, u32[]{:S(2)}) async-start(f32[2,256,1024]{1,0,2:T(2,128)} %copy.219), calls=%async_computation.8 | async-start | bytes 4194304 | tf_op jit(solution)/shard_map/all_to_all | solution.py:229
  707.9 3.1 copy-start.28
  755.4 53.4 %all-to-all-start.7 = ((f32[2,256,1024]{1,0,2:T(2,128)}), f32[2,256,1024]{1,0,2:T(2,128)}, u32[]{:S(2)}, u32[]{:S(2)}) async-start(f32[2,256,1024]{1,0,2:T(2,128)} %copy.222), calls=%async_computation.10 | async-start | bytes 4194304 | tf_op jit(solution)/shard_map/all_to_all | solution.py:229
  759.8 141.5 %reduce-scatter.11.cloned.1.call-start = ((), (), s32[]{:S(2)}) async-start(), calls=%async_computation.19 | async-start | bytes 5242880 | tf_op jit(solution)/shard_map/reduce_scatter | solution.py:243
  850.5 106.2 %reduce-scatter.9.cloned.1.call-start = ((), (), s32[]{:S(2)}) async-start(), calls=%async_computation.18 | async-start | bytes 5242880 | tf_op jit(solution)/shard_map/reduce_scatter | solution.py:243
  851.0 161.2 %reduce-scatter.7.cloned.1.call-start = ((), (), s32[]{:S(2)}) async-start(), calls=%async_computation.17 | async-start | bytes 5242880 | tf_op jit(solution)/shard_map/reduce_scatter | solution.py:243
  851.8 216.1 %reduce-scatter.5.cloned.1.call-start = ((), (), s32[]{:S(2)}) async-start(), calls=%async_computation.16 | async-start | bytes 5242880 | tf_op jit(solution)/shard_map/reduce_scatter | solution.py:243
  (25 other events, 54.7 us)
Sparse Core Ops, SparseCore 0:
  11.1 55.2 all-gather.4
  68.3 52.5 all-gather.6
  122.7 52.5 all-gather.8
  177.0 52.5 all-gather.10
  850.6 50.5 reduce-scatter.10
  904.0 52.5 reduce-scatter.8
  959.6 52.5 reduce-scatter.6
  1015.2 52.5 reduce-scatter.4

commit v5 on v2

--- a/solution.py
+++ b/solution.py
@@ -7,7 +7,7 @@
 
 
 SOFTENING = 0.1
-HIGHEST_PRECISION = lax.Precision.HIGH
+HIGHEST_PRECISION = lax.Precision.HIGHEST
 CHUNKS = 4
 
 
@@ -171,8 +171,15 @@
         stacked = jnp.stack([half_re, half_im])
         spread = lax.all_to_all(stacked, "row", split_axis=1, concat_axis=2, tiled=True)
         spreads.append(spread.reshape(2, block_rows, row_count, width))
-    spread_all = jnp.stack(spreads, axis=3).reshape(2, block_rows, row_count * size_cols)
-    window_part = lax.dynamic_slice_in_dim(spread_all, col_shift, window, 2)
+    folds = row_count * size_cols // window
+    per_fold = row_count // folds
+    folded = []
+    for spread in spreads:
+        total = spread[:, :, :per_fold]
+        for f in range(1, folds):
+            total = total + spread[:, :, f * per_fold:(f + 1) * per_fold]
+        folded.append(total)
+    window_part = jnp.stack(folded, axis=3).reshape(2, block_rows, window)
     field = transform(
         window_part.reshape(shape_cols), "ytr", "ykr", "yjk", outer_cols, row_count, 1.0
     )
@@ -187,14 +194,11 @@
         row_count,
         -1.0,
     )
-    padded = jnp.zeros((2, block_rows, row_count * size_cols), jnp.float32)
-    padded = lax.dynamic_update_slice_in_dim(
-        padded, back.reshape(2, block_rows, window), col_shift, 2
-    )
-    padded = padded.reshape(2, block_rows, row_count, chunks, width)
+    back = back.reshape(2, block_rows, per_fold, chunks, width)
     gathered_all = []
     for chunk in range(chunks):
-        piece = padded[:, :, :, chunk, :].reshape(2, block_rows, row_count * width)
+        piece = jnp.concatenate([back[:, :, :, chunk, :]] * folds, axis=2)
+        piece = piece.reshape(2, block_rows, row_count * width)
         gathered_all.append(lax.all_to_all(piece, "row", split_axis=2, concat_axis=1, tiled=True))
     results = []
     for chunk in range(chunks):

time: 1040 us -> 1030 us (level)
  matrix products: 70.5 us -> 112 us
  local copies, waits for them, and re-layouts: 214 us -> 175 us
  waiting for transfers between devices: 595 us -> 576 us
    dot_general x8, matrix products: 49.3 us -> 78.9 us  [row_transform(): middle = jnp.dot(table, stacked, precision=HIGHEST_PRECISION)]
    another operation x9 -> x6, local copies, waits for them, and re-layouts: 33 us -> 19.8 us  [the longest x4 15.1 us: on_device(): piece = padded[:, :, :, chunk, :].reshape(2, block_rows, row_count * width)]
    dynamic_update_slice x1 -> x0, local copies, waits for them, and re-layouts: 12.5 us -> none  [on_device(): lax.dynamic_update_slice_in_dim(padded, back.reshape(2, block_rows, windo...]
    all_to_all x4, waiting for transfers between devices: 96.2 us -> 85.3 us  [on_device(): lax.all_to_all(piece, 'row', split_axis=2, concat_axis=1, tiled=True)]
  transfers between devices with their start and end apart: 16 -> 16, of which waited for: 16 -> 16; matrix products, arithmetic and copies ran while one was open for 21% -> 24% of each run, Pallas kernels for 0% -> 0%
where the time goes in v5:
time: 1030 us; the launch traced here: 1020 us
  waiting for transfers between devices  576 us (56%)
  local copies, waits for them, and re-layouts  175 us (17%)
  matrix products  112 us (11%)
  other arithmetic  107 us (10%)
  starting transfers between devices  34.9 us (3%)
  between operations  17.8 us (2%)
    reduce_scatter x4, waiting for transfers between devices, on_device(): lax.psum_scatter(embedded, 'led', scatter_dimension=1, tiled=True)  215 us
    all_to_all x4, waiting for transfers between devices, on_device(): lax.all_to_all(stacked, 'row', split_axis=1, concat_axis=2, tiled=True)  151 us
    all_gather x4, waiting for transfers between devices, on_device(): regions.append(lax.all_gather(part, 'led', axis=1, tiled=True))  120 us
    all_to_all x4, waiting for transfers between devices, on_device(): lax.all_to_all(piece, 'row', split_axis=2, concat_axis=1, tiled=True)  85.3 us
    dot_general x8, matrix products, row_transform(): middle = jnp.dot(table, stacked, precision=HIGHEST_PRECISION)  78.9 us
    dynamic_update_slice x4, local copies, waits for them, and re-layouts, on_device(): lax.dynamic_update_slice_in_dim(embedded, jnp.stack([upd_re, upd_im]), ro...  28.1 us
    another operation x4, local copies, waits for them, and re-layouts, on_device(): stacked = jnp.stack([half_re, half_im])  28.1 us
    mul x1, other arithmetic, pupil_at(): return (weight * jnp.cos(phases), weight * jnp.sin(phases))  24.1 us
  transfers between devices with their start and end apart: 16, of which 16 were waited for; matrix products, arithmetic and copies ran while one was open for 24% of the time, Pallas kernels for 0%

profile of v5, /device:TPU:0, one launch (start us, length us, event | category | flops | bytes accessed | tf_op | source)
XLA Modules:
  0.0 1021.4 jit_solution(6043465723017257754)
XLA Ops:
  27.5 24.1 %select_multiply_fusion = (f32[2048,512]{1,0:T(8,128)}, f32[2048,512]{1,0:T(8,128)}) fusion(f32[]{:T(128)} %bitcast.6, f32[512]{0:T(512)S(1)} %get-tuple-element.199, f32[2048]{0:T(1024)S(1)} %get-tuple-element.202, f32[512]{0:T(512)S(1)} %get-tuple-element.200, f32[2048]{0:T(1024)S(1)} %convert_multiply_fusion.1, f32[]{:T(128)} %bitcast.3, f32[]{:T(128)} %bitcast.2, ...), kind=kLoop, calls=%fused_computation.5 | loop fusion | flops 27262976 | bytes 8429584 | tf_op jit(solution)/shard_map/mul | solution.py:29
  53.4 13.1 %all-gather.5.cloned.1.call-done = f32[2,4096,128]{2,1,0:T(8,128)} async-done(((f32[2,1024,128]{2,1,0:T(8,128)}), f32[2,4096,128]{2,1,0:T(8,128)}) %all-gather.5.cloned.1.call-update) | async-done | bytes 4194320 | tf_op jit(solution)/shard_map/all_gather | solution.py:160
  80.7 40.1 %all-gather.7.cloned.1.call-done = f32[2,4096,128]{2,1,0:T(8,128)} async-done(((f32[2,1024,128]{2,1,0:T(8,128)}), f32[2,4096,128]{2,1,0:T(8,128)}) %all-gather.7.cloned.1.call-update) | async-done | bytes 4194320 | tf_op jit(solution)/shard_map/all_gather | solution.py:160
  127.9 10.9 %fusion.36 = f32[1024,512]{1,0:T(8,128)S(1)} fusion(f32[512,512]{1,0:T(8,128)} %reshape.438, f32[512,512]{1,0:T(8,128)} %reshape.437, f32[512,512]{1,0:T(8,128)} %get-tuple-element.204, f32[512,512]{1,0:T(8,128)} %copy-done.18, f32[512,512]{1,0:T(8,128)} %fusion.81), kind=kOutput, calls=%fused_computation.45 | convolution fusion | flops 6446120960 | bytes 7340032 | tf_op jit(solution)/shard_map/dot_general | solution.py:96
  141.7 33.6 %all-gather.9.cloned.1.call-done = f32[2,4096,128]{2,1,0:T(8,128)} async-done(((f32[2,1024,128]{2,1,0:T(8,128)}), f32[2,4096,128]{2,1,0:T(8,128)}) %all-gather.9.cloned.1.call-update) | async-done | bytes 4194320 | tf_op jit(solution)/shard_map/all_gather | solution.py:160
  182.3 11.1 %fusion.40 = f32[1024,512]{1,0:T(8,128)S(1)} fusion(f32[512,512]{1,0:T(8,128)} %reshape.440, f32[512,512]{1,0:T(8,128)} %reshape.439, f32[512,512]{1,0:T(8,128)} %get-tuple-element.204, f32[512,512]{1,0:T(8,128)} %copy-done.18, f32[512,512]{1,0:T(8,128)} %fusion.81), kind=kOutput, calls=%fused_computation.50 | convolution fusion | flops 6446120960 | bytes 7340032 | tf_op jit(solution)/shard_map/dot_general | solution.py:96
  196.3 33.3 %all-gather.11.cloned.1.call-done = f32[2,4096,128]{2,1,0:T(8,128)} async-done(((f32[2,1024,128]{2,1,0:T(8,128)}), f32[2,4096,128]{2,1,0:T(8,128)}) %all-gather.11.cloned.1.call-update) | async-done | bytes 4194320 | tf_op jit(solution)/shard_map/all_gather | solution.py:160
  236.7 10.2 %fusion.44 = f32[1024,512]{1,0:T(8,128)S(1)} fusion(f32[512,512]{1,0:T(8,128)} %reshape.442, f32[512,512]{1,0:T(8,128)} %reshape.441, f32[512,512]{1,0:T(8,128)} %get-tuple-element.204, f32[512,512]{1,0:T(8,128)} %copy-done.18, f32[512,512]{1,0:T(8,128)} %fusion.81), kind=kOutput, calls=%fused_computation.55 | convolution fusion | flops 6446120960 | bytes 7340032 | tf_op jit(solution)/shard_map/dot_general | solution.py:96
  267.4 43.6 %all-to-all-done.3 = f32[2,2048,128]{2,0,1:T(2,128)} async-done(((f32[2,2048,128]{2,0,1:T(2,128)}), f32[2,2048,128]{2,0,1:T(2,128)}, u32[]{:S(2)}, u32[]{:S(2)}) %all-to-all-start.3) | async-done | bytes 2097184 | tf_op jit(solution)/shard_map/all_to_all | solution.py:172
  320.8 43.6 %all-to-all-done.2 = f32[2,2048,128]{2,0,1:T(2,128)} async-done(((f32[2,2048,128]{2,0,1:T(2,128)}), f32[2,2048,128]{2,0,1:T(2,128)}, u32[]{:S(2)}, u32[]{:S(2)}) %all-to-all-start.2) | async-done | bytes 2097184 | tf_op jit(solution)/shard_map/all_to_all | solution.py:172
  377.3 40.5 %all-to-all-done.1 = f32[2,2048,128]{2,0,1:T(2,128)} async-done(((f32[2,2048,128]{2,0,1:T(2,128)}), f32[2,2048,128]{2,0,1:T(2,128)}, u32[]{:S(2)}, u32[]{:S(2)}) %all-to-all-start.1) | async-done | bytes 2097184 | tf_op jit(solution)/shard_map/all_to_all | solution.py:172
  447.6 23.8 %all-to-all-done = f32[2,2048,128]{2,0,1:T(2,128)} async-done(((f32[2,2048,128]{2,0,1:T(2,128)}), f32[2,2048,128]{2,0,1:T(2,128)}, u32[]{:S(2)}, u32[]{:S(2)}) %all-to-all-start) | async-done | bytes 2097184 | tf_op jit(solution)/shard_map/all_to_all | solution.py:172
  486.4 9.5 fusion.27
  512.2 9.1 fusion.26
  544.4 44.3 %all-to-all-done.4 = f32[2,256,1024]{1,0,2:T(2,128)S(1)} async-done(((f32[2,256,1024]{1,0,2:T(2,128)}), f32[2,256,1024]{1,0,2:T(2,128)S(1)}, u32[]{:S(2)}, u32[]{:S(2)}) %all-to-all-start.4) | async-done | bytes 2097184 | tf_op jit(solution)/shard_map/all_to_all | solution.py:202
  618.6 24.1 %all-to-all-done.5 = f32[2,256,1024]{1,0,2:T(2,128)S(1)} async-done(((f32[2,256,1024]{1,0,2:T(2,128)}), f32[2,256,1024]{1,0,2:T(2,128)S(1)}, u32[]{:S(2)}, u32[]{:S(2)}) %all-to-all-start.5) | async-done | bytes 2097184 | tf_op jit(solution)/shard_map/all_to_all | solution.py:202
  677.7 10.0 fusion.52
  724.8 9.7 fusion.56
  739.7 10.0 all-to-all-done.7
  767.0 9.9 fusion.60
  792.8 48.6 %reduce-scatter.11.cloned.1.call-done = f32[2,1024,128]{2,1,0:T(8,128)} async-done(((f32[2,4096,128]{2,1,0:T(8,128)}), f32[2,1024,128]{2,1,0:T(8,128)}) %reduce-scatter.11.cloned.1.call-update) | async-done | bytes 1048592 | tf_op jit(solution)/shard_map/reduce_scatter | solution.py:216
  841.4 55.5 %reduce-scatter.9.cloned.1.call-done = f32[2,1024,128]{2,1,0:T(8,128)} async-done(((f32[2,4096,128]{2,1,0:T(8,128)}), f32[2,1024,128]{2,1,0:T(8,128)}) %reduce-scatter.9.cloned.1.call-update) | async-done | bytes 1048592 | tf_op jit(solution)/shard_map/reduce_scatter | solution.py:216
  896.9 55.6 %reduce-scatter.7.cloned.1.call-done = f32[2,1024,128]{2,1,0:T(8,128)} async-done(((f32[2,4096,128]{2,1,0:T(8,128)}), f32[2,1024,128]{2,1,0:T(8,128)}) %reduce-scatter.7.cloned.1.call-update) | async-done | bytes 1048592 | tf_op jit(solution)/shard_map/reduce_scatter | solution.py:216
  952.5 55.6 %reduce-scatter.5.cloned.1.call-done = f32[2,1024,128]{2,1,0:T(8,128)} async-done(((f32[2,4096,128]{2,1,0:T(8,128)}), f32[2,1024,128]{2,1,0:T(8,128)}) %reduce-scatter.5.cloned.1.call-update) | async-done | bytes 1048592 | tf_op jit(solution)/shard_map/reduce_scatter | solution.py:216
  (244 shorter events, 333.9 us)
Async XLA Ops:
  6.5 59.9 %all-gather.5.cloned.1.call-start = ((), (), s32[]{:S(2)}) async-start(), calls=%async_computation.12 | async-start | bytes 5242880 | tf_op jit(solution)/shard_map/all_gather | solution.py:160
  10.9 14.0 %copy-start.24 = (f32[6]{0:T(128)S(1)}, f32[6]{0:T(128)}, u32[]{:S(2)}) copy-start(f32[6]{0:T(128)} %param.7) | copy-start | bytes 76
  10.9 109.9 %all-gather.7.cloned.1.call-start = ((), (), s32[]{:S(2)}) async-start(), calls=%async_computation.13 | async-start | bytes 5242880 | tf_op jit(solution)/shard_map/all_gather | solution.py:160
  11.7 163.6 %all-gather.9.cloned.1.call-start = ((), (), s32[]{:S(2)}) async-start(), calls=%async_computation.14 | async-start | bytes 5242880 | tf_op jit(solution)/shard_map/all_gather | solution.py:160
  12.4 217.2 %all-gather.11.cloned.1.call-start = ((), (), s32[]{:S(2)}) async-start(), calls=%async_computation.15 | async-start | bytes 5242880 | tf_op jit(solution)/shard_map/all_gather | solution.py:160
  20.2 50.1 %copy-start.18 = (f32[512,512]{1,0:T(8,128)}, f32[512,512]{1,0:T(8,128)S(1)}, u32[]{:S(2)}) copy-start(f32[512,512]{1,0:T(8,128)S(1)} %get-tuple-element.203) | copy-start | bytes 3145732
  257.1 53.9 %all-to-all-start.3 = ((f32[2,2048,128]{2,0,1:T(2,128)}), f32[2,2048,128]{2,0,1:T(2,128)}, u32[]{:S(2)}, u32[]{:S(2)}) async-start(f32[2,2048,128]{2,0,1:T(2,128)} %copy.115), calls=%async_computation.3 | async-start | bytes 4194304 | tf_op jit(solution)/shard_map/all_to_all | solution.py:172
  311.0 53.4 %all-to-all-start.2 = ((f32[2,2048,128]{2,0,1:T(2,128)}), f32[2,2048,128]{2,0,1:T(2,128)}, u32[]{:S(2)}, u32[]{:S(2)}) async-start(f32[2,2048,128]{2,0,1:T(2,128)} %copy.113), calls=%async_computation.2 | async-start | bytes 4194304 | tf_op jit(solution)/shard_map/all_to_all | solution.py:172
  364.4 53.4 %all-to-all-start.1 = ((f32[2,2048,128]{2,0,1:T(2,128)}), f32[2,2048,128]{2,0,1:T(2,128)}, u32[]{:S(2)}, u32[]{:S(2)}) async-start(f32[2,2048,128]{2,0,1:T(2,128)} %copy.111), calls=%async_computation.1 | async-start | bytes 4194304 | tf_op jit(solution)/shard_map/all_to_all | solution.py:172
  417.8 53.6 %all-to-all-start = ((f32[2,2048,128]{2,0,1:T(2,128)}), f32[2,2048,128]{2,0,1:T(2,128)}, u32[]{:S(2)}, u32[]{:S(2)}) async-start(f32[2,2048,128]{2,0,1:T(2,128)} %copy.109), calls=%async_computation | async-start | bytes 4194304 | tf_op jit(solution)/shard_map/all_to_all | solution.py:172
  481.0 5.4 copy-start.16
  481.0 5.4 copy-start.17
  486.4 9.5 copy-start.8
  507.3 4.9 copy-start.14
  507.3 4.9 copy-start.15
  512.2 9.1 copy-start.7
  535.8 53.0 %all-to-all-start.4 = ((f32[2,256,1024]{1,0,2:T(2,128)}), f32[2,256,1024]{1,0,2:T(2,128)S(1)}, u32[]{:S(2)}, u32[]{:S(2)}) async-start(f32[2,256,1024]{1,0,2:T(2,128)} %copy.130), calls=%async_computation.4 | async-start | bytes 4194304 | tf_op jit(solution)/shard_map/all_to_all | solution.py:202
  590.1 52.6 %all-to-all-start.5 = ((f32[2,256,1024]{1,0,2:T(2,128)}), f32[2,256,1024]{1,0,2:T(2,128)S(1)}, u32[]{:S(2)}, u32[]{:S(2)}) async-start(f32[2,256,1024]{1,0,2:T(2,128)} %copy.134), calls=%async_computation.6 | async-start | bytes 4194304 | tf_op jit(solution)/shard_map/all_to_all | solution.py:202
  642.7 53.5 %all-to-all-start.6 = ((f32[2,256,1024]{1,0,2:T(2,128)}), f32[2,256,1024]{1,0,2:T(2,128)}, u32[]{:S(2)}, u32[]{:S(2)}) async-start(f32[2,256,1024]{1,0,2:T(2,128)} %copy.137), calls=%async_computation.8 | async-start | bytes 4194304 | tf_op jit(solution)/shard_map/all_to_all | solution.py:202
  696.2 53.4 %all-to-all-start.7 = ((f32[2,256,1024]{1,0,2:T(2,128)}), f32[2,256,1024]{1,0,2:T(2,128)}, u32[]{:S(2)}, u32[]{:S(2)}) async-start(f32[2,256,1024]{1,0,2:T(2,128)} %copy.140), calls=%async_computation.10 | async-start | bytes 4194304 | tf_op jit(solution)/shard_map/all_to_all | solution.py:202
  700.6 140.8 %reduce-scatter.11.cloned.1.call-start = ((), (), s32[]{:S(2)}) async-start(), calls=%async_computation.19 | async-start | bytes 5242880 | tf_op jit(solution)/shard_map/reduce_scatter | solution.py:216
  790.7 106.2 %reduce-scatter.9.cloned.1.call-start = ((), (), s32[]{:S(2)}) async-start(), calls=%async_computation.18 | async-start | bytes 5242880 | tf_op jit(solution)/shard_map/reduce_scatter | solution.py:216
  791.3 161.2 %reduce-scatter.7.cloned.1.call-start = ((), (), s32[]{:S(2)}) async-start(), calls=%async_computation.17 | async-start | bytes 5242880 | tf_op jit(solution)/shard_map/reduce_scatter | solution.py:216
  792.1 216.1 %reduce-scatter.5.cloned.1.call-start = ((), (), s32[]{:S(2)}) async-start(), calls=%async_computation.16 | async-start | bytes 5242880 | tf_op jit(solution)/shard_map/reduce_scatter | solution.py:216
  (18 other events, 49.0 us)
Sparse Core Ops, SparseCore 0:
  11.1 55.2 all-gather.4
  68.3 52.5 all-gather.6
  122.7 52.5 all-gather.8
  177.0 52.5 all-gather.10
  790.8 50.5 reduce-scatter.10
  844.3 52.5 reduce-scatter.8
  899.9 52.5 reduce-scatter.6
  955.5 52.5 reduce-scatter.4

commit v6 on v5

--- a/solution.py
+++ b/solution.py
@@ -168,18 +168,26 @@
         lit_re = pupil_re * band[0] - pupil_im * band[1]
         lit_im = pupil_re * band[1] + pupil_im * band[0]
         half_re, half_im = row_transform(lit_re, lit_im, 1.0)
-        stacked = jnp.stack([half_re, half_im])
-        spread = lax.all_to_all(stacked, "row", split_axis=1, concat_axis=2, tiled=True)
-        spreads.append(spread.reshape(2, block_rows, row_count, width))
+        stacked = jnp.stack(
+            [
+                half_re.reshape(row_count, block_rows, width),
+                half_im.reshape(row_count, block_rows, width),
+            ],
+            axis=1,
+        )
+        spread = lax.all_to_all(stacked, "row", split_axis=0, concat_axis=0, tiled=True)
+        spreads.append(spread)
     folds = row_count * size_cols // window
     per_fold = row_count // folds
     folded = []
     for spread in spreads:
-        total = spread[:, :, :per_fold]
+        total = spread[:per_fold]
         for f in range(1, folds):
-            total = total + spread[:, :, f * per_fold:(f + 1) * per_fold]
+            total = total + spread[f * per_fold:(f + 1) * per_fold]
         folded.append(total)
-    window_part = jnp.stack(folded, axis=3).reshape(2, block_rows, window)
+    window_part = (
+        jnp.stack(folded, axis=1).transpose(2, 3, 0, 1, 4).reshape(2, block_rows, window)
+    )
     field = transform(
         window_part.reshape(shape_cols), "ytr", "ykr", "yjk", outer_cols, row_count, 1.0
     )
@@ -197,15 +205,17 @@
     back = back.reshape(2, block_rows, per_fold, chunks, width)
     gathered_all = []
     for chunk in range(chunks):
-        piece = jnp.concatenate([back[:, :, :, chunk, :]] * folds, axis=2)
-        piece = piece.reshape(2, block_rows, row_count * width)
-        gathered_all.append(lax.all_to_all(piece, "row", split_axis=2, concat_axis=1, tiled=True))
+        piece = back[:, :, :, chunk, :].transpose(2, 0, 1, 3)
+        piece = jnp.concatenate([piece] * folds, axis=0)
+        gathered_all.append(lax.all_to_all(piece, "row", split_axis=0, concat_axis=0, tiled=True))
     results = []
     for chunk in range(chunks):
         gathered = gathered_all[chunk]
         if results:
             gathered, _ = lax.optimization_barrier((gathered, embedded))
-        spec_re, spec_im = row_transform(gathered[0], gathered[1], -1.0)
+        spec_re, spec_im = row_transform(
+            gathered[:, 0].reshape(window, width), gathered[:, 1].reshape(window, width), -1.0
+        )
         pupil_re, pupil_im = pupils[chunk]
         upd_re = pupil_re * spec_re + pupil_im * spec_im
         upd_im = pupil_re * spec_im - pupil_im * spec_re

time: 1030 us -> 896 us (0.87)
  waiting for transfers between devices: 576 us -> 450 us
  local copies, waits for them, and re-layouts: 175 us -> 115 us
  blocking collectives: 0 us -> 52.2 us
    all_to_all x8 -> x7, waiting for transfers between devices: 237 us -> 124 us  [the longest x4 90.6 us: on_device(): lax.all_to_all(piece, 'row', split_axis=0, concat_axis=0, tiled=True)]
    all_to_all x0 -> x1, blocking collectives: none -> 52.2 us  [on_device(): lax.all_to_all(stacked, 'row', split_axis=0, concat_axis=0, tiled=True)]
    another operation x9 -> x12, local copies, waits for them, and re-layouts: 42.5 us -> 14.9 us  [the longest x4 28.1 us: on_device(): stacked = jnp.stack([half_re, half_im])]
    all_to_all x11 -> x0, local copies, waits for them, and re-layouts: 21.5 us -> none  [the longest x7 14.5 us: on_device(): lax.all_to_all(piece, 'row', split_axis=2, concat_axis=1, tiled=True)]
    all_gather x4, waiting for transfers between devices: 120 us -> 106 us  [on_device(): regions.append(lax.all_gather(part, 'led', axis=1, tiled=True))]
    reshape x4 -> x0, local copies, waits for them, and re-layouts: 11.8 us -> none  [on_device(): piece = piece.reshape(2, block_rows, row_count * width)]
    all_to_all x8 -> x7, starting transfers between devices: 34.6 us -> 31.3 us  [the longest x4 17.2 us: on_device(): lax.all_to_all(piece, 'row', split_axis=0, concat_axis=0, tiled=True)]
  transfers between devices with their start and end apart: 16 -> 15, of which waited for: 16 -> 14; matrix products, arithmetic and copies ran while one was open for 24% -> 27% of each run, Pallas kernels for 0% -> 0%
where the time goes in v6:
time: 896 us; the launch traced here: 891 us
  waiting for transfers between devices  450 us (50%)
  local copies, waits for them, and re-layouts  115 us (13%)
  other arithmetic  115 us (13%)
  matrix products  110 us (12%)
  blocking collectives  52.2 us (6%)
  starting transfers between devices  31.5 us (4%)
  between operations  17.9 us (2%)
    reduce_scatter x4, waiting for transfers between devices, on_device(): lax.psum_scatter(embedded, 'led', scatter_dimension=1, tiled=True)  215 us
    all_gather x4, waiting for transfers between devices, on_device(): regions.append(lax.all_gather(part, 'led', axis=1, tiled=True))  106 us
    all_to_all x4, waiting for transfers between devices, on_device(): lax.all_to_all(piece, 'row', split_axis=0, concat_axis=0, tiled=True)  90.6 us
    dot_general x8, matrix products, row_transform(): middle = jnp.dot(table, stacked, precision=HIGHEST_PRECISION)  77.4 us
    all_to_all x1, blocking collectives, on_device(): lax.all_to_all(stacked, 'row', split_axis=0, concat_axis=0, tiled=True)  52.2 us
    all_to_all x3, waiting for transfers between devices, on_device(): lax.all_to_all(stacked, 'row', split_axis=0, concat_axis=0, tiled=True)  33.7 us
    dynamic_update_slice x4, local copies, waits for them, and re-layouts, on_device(): lax.dynamic_update_slice_in_dim(embedded, jnp.stack([upd_re, upd_im]), ro...  28.3 us
    mul x1, other arithmetic, pupil_at(): return (weight * jnp.cos(phases), weight * jnp.sin(phases))  24.6 us
  transfers between devices with their start and end apart: 15, of which 14 were waited for; matrix products, arithmetic and copies ran while one was open for 27% of the time, Pallas kernels for 0%

profile of v6, /device:TPU:0, one launch (start us, length us, event | category | flops | bytes accessed | tf_op | source)
XLA Modules:
  0.0 890.8 jit_solution(5621522869032283601)
XLA Ops:
  27.7 24.6 %select_multiply_fusion = (f32[2048,512]{1,0:T(8,128)}, f32[2048,512]{1,0:T(8,128)}) fusion(f32[]{:T(128)} %bitcast.6, f32[512]{0:T(512)S(1)} %get-tuple-element.207, f32[2048]{0:T(1024)S(1)} %get-tuple-element.210, f32[512]{0:T(512)S(1)} %get-tuple-element.208, f32[2048]{0:T(1024)S(1)} %convert_multiply_fusion.1, f32[]{:T(128)} %bitcast.3, f32[]{:T(128)} %bitcast.2, ...), kind=kLoop, calls=%fused_computation.5 | loop fusion | flops 27262976 | bytes 8429584 | tf_op jit(solution)/shard_map/mul | solution.py:29
  54.2 12.3 %all-gather.5.cloned.1.call-done = f32[2,4096,128]{2,1,0:T(8,128)} async-done(((f32[2,1024,128]{2,1,0:T(8,128)}), f32[2,4096,128]{2,1,0:T(8,128)}) %all-gather.5.cloned.1.call-update) | async-done | bytes 4194320 | tf_op jit(solution)/shard_map/all_gather | solution.py:160
  82.8 38.1 %all-gather.7.cloned.1.call-done = f32[2,4096,128]{2,1,0:T(8,128)} async-done(((f32[2,1024,128]{2,1,0:T(8,128)}), f32[2,4096,128]{2,1,0:T(8,128)}) %all-gather.7.cloned.1.call-update) | async-done | bytes 4194320 | tf_op jit(solution)/shard_map/all_gather | solution.py:160
  124.7 9.1 %fusion.36 = f32[1024,512]{1,0:T(8,128)S(1)} fusion(f32[512,512]{1,0:T(8,128)S(1)} %reshape.414, f32[512,512]{1,0:T(8,128)} %reshape.413, f32[512,512]{1,0:T(8,128)} %get-tuple-element.212, f32[512,512]{1,0:T(8,128)S(1)} %copy-done.19, f32[512,512]{1,0:T(8,128)} %fusion.81), kind=kOutput, calls=%fused_computation.45 | convolution fusion | flops 6446120960 | bytes 7340032 | tf_op jit(solution)/shard_map/dot_general | solution.py:96
  142.0 33.3 %all-gather.9.cloned.1.call-done = f32[2,4096,128]{2,1,0:T(8,128)} async-done(((f32[2,1024,128]{2,1,0:T(8,128)}), f32[2,4096,128]{2,1,0:T(8,128)}) %all-gather.9.cloned.1.call-update) | async-done | bytes 4194320 | tf_op jit(solution)/shard_map/all_gather | solution.py:160
  182.4 10.7 %fusion.40 = f32[1024,512]{1,0:T(8,128)S(1)} fusion(f32[512,512]{1,0:T(8,128)} %reshape.416, f32[512,512]{1,0:T(8,128)} %reshape.415, f32[512,512]{1,0:T(8,128)} %get-tuple-element.212, f32[512,512]{1,0:T(8,128)} %copy-done.18, f32[512,512]{1,0:T(8,128)} %fusion.81), kind=kOutput, calls=%fused_computation.50 | convolution fusion | flops 6446120960 | bytes 7340032 | tf_op jit(solution)/shard_map/dot_general | solution.py:96
  206.9 22.7 %all-gather.11.cloned.1.call-done = f32[2,4096,128]{2,1,0:T(8,128)} async-done(((f32[2,1024,128]{2,1,0:T(8,128)}), f32[2,4096,128]{2,1,0:T(8,128)}) %all-gather.11.cloned.1.call-update) | async-done | bytes 4194320 | tf_op jit(solution)/shard_map/all_gather | solution.py:160
  234.8 9.6 %fusion.44 = f32[1024,512]{1,0:T(8,128)S(1)} fusion(f32[512,512]{1,0:T(8,128)S(1)} %reshape.418, f32[512,512]{1,0:T(8,128)S(1)} %reshape.417, f32[512,512]{1,0:T(8,128)} %get-tuple-element.212, f32[512,512]{1,0:T(8,128)} %copy-done.18, f32[512,512]{1,0:T(8,128)} %fusion.81), kind=kOutput, calls=%fused_computation.55 | convolution fusion | flops 6446120960 | bytes 7340032 | tf_op jit(solution)/shard_map/dot_general | solution.py:96
  256.0 52.2 %all_to_all.40 = f32[8,2,256,128]{2,3,1,0:T(8,128)} all-to-all(f32[8,2,256,128]{2,3,1,0:T(8,128)S(1)} %pad_maximum_fusion.4), channel_id=1, replica_groups=mesh['led'=4,'row'=8] {'row'}, dimensions={0} | all-to-all | bytes 4194304 | tf_op jit(solution)/shard_map/all_to_all | solution.py:178
  335.3 26.7 %all-to-all-done = f32[8,2,256,128]{2,3,1,0:T(8,128)} async-done(((f32[8,2,256,128]{2,3,1,0:T(8,128)}), f32[8,2,256,128]{2,3,1,0:T(8,128)}, u32[]{:S(2)}, u32[]{:S(2)}) %all-to-all-start) | async-done | bytes 2097184 | tf_op jit(solution)/shard_map/all_to_all | solution.py:178
  371.9 9.2 %fusion.27 = f32[2,256,256,8,1]{1,2,3,0,4:T(8,128)S(1)} fusion(f32[2,256,256,8]{2,1,0,3:T(8,128)} %copy.89, f32[1,2,256,256]{2,3,0,1:T(8,128)S(1)} %copy-done.17, f32[1,2,256,256]{2,3,0,1:T(8,128)S(1)} %copy-done.16), kind=kOutput, calls=%fused_computation.37 | convolution fusion | flops 6442713088 | bytes 9437184 | tf_op jit(solution)/shard_map/pytr,pqtk->qykr/dot_general | solution.py:58
  397.4 9.2 %fusion.26 = f32[2,256,256,8,1]{1,2,3,0,4:T(8,128)S(1)} fusion(f32[1,256,256,8]{2,1,0,3:T(8,128)} %copy.96, f32[1,256,256,8]{2,1,0,3:T(8,128)} %copy.95, f32[1,2,256,256]{2,3,1,0:T(8,128)S(1)} %copy-done.15, f32[1,2,256,256]{2,3,1,0:T(8,128)S(1)} %copy-done.14), kind=kOutput, calls=%fused_computation.36 | convolution fusion | flops 6443761664 | bytes 9437184 | tf_op jit(solution)/shard_map/pytr,pqtk->qykr/dot_general | solution.py:58
  426.5 45.7 %all-to-all-done.4 = f32[8,2,256,128]{2,3,1,0:T(8,128)S(1)} async-done(((f32[8,2,256,128]{2,3,1,0:T(8,128)}), f32[8,2,256,128]{2,3,1,0:T(8,128)S(1)}, u32[]{:S(2)}, u32[]{:S(2)}) %all-to-all-start.4) | async-done | bytes 2097184 | tf_op jit(solution)/shard_map/all_to_all | solution.py:210
  496.3 9.9 %fusion.48 = f32[1024,512]{1,0:T(8,128)S(1)} fusion(f32[512,512]{1,0:T(8,128)S(1)} %reshape_reshape_squeeze.25, f32[512,512]{1,0:T(8,128)} %reshape_reshape_squeeze.24, f32[512,512]{1,0:T(8,128)} %get-tuple-element.218, f32[512,512]{1,0:T(8,128)} %get-tuple-element.217, f32[512,512]{1,0:T(8,128)} %fusion.80), kind=kOutput, calls=%fused_computation.61 | convolution fusion | flops 6446120960 | bytes 7340032 | tf_op jit(solution)/shard_map/dot_general | solution.py:96
  509.5 16.4 %all-to-all-done.5 = f32[8,2,256,128]{2,3,1,0:T(8,128)} async-done(((f32[8,2,256,128]{2,3,1,0:T(8,128)}), f32[8,2,256,128]{2,3,1,0:T(8,128)}, u32[]{:S(2)}, u32[]{:S(2)}) %all-to-all-start.5) | async-done | bytes 2097184 | tf_op jit(solution)/shard_map/all_to_all | solution.py:210
  548.7 9.7 %fusion.52 = f32[1024,512]{1,0:T(8,128)S(1)} fusion(f32[512,512]{1,0:T(8,128)S(1)} %reshape_reshape_squeeze.27, f32[512,512]{1,0:T(8,128)} %reshape_reshape_squeeze.26, f32[512,512]{1,0:T(8,128)} %get-tuple-element.218, f32[512,512]{1,0:T(8,128)} %get-tuple-element.217, f32[512,512]{1,0:T(8,128)S(1)} %copy-done.20), kind=kOutput, calls=%fused_computation.67 | convolution fusion | flops 6446120960 | bytes 7340032 | tf_op jit(solution)/shard_map/dot_general | solution.py:96
  561.4 18.2 %all-to-all-done.6 = f32[8,2,256,128]{2,3,1,0:T(8,128)} async-done(((f32[8,2,256,128]{2,3,1,0:T(8,128)}), f32[8,2,256,128]{2,3,1,0:T(8,128)}, u32[]{:S(2)}, u32[]{:S(2)}) %all-to-all-start.6) | async-done | bytes 2097184 | tf_op jit(solution)/shard_map/all_to_all | solution.py:210
  599.2 9.7 %fusion.56 = f32[1024,512]{1,0:T(8,128)S(1)} fusion(f32[512,512]{1,0:T(8,128)S(1)} %reshape_reshape_squeeze.29, f32[512,512]{1,0:T(8,128)} %reshape_reshape_squeeze.28, f32[512,512]{1,0:T(8,128)} %get-tuple-element.218, f32[512,512]{1,0:T(8,128)} %get-tuple-element.217, f32[512,512]{1,0:T(8,128)S(1)} %copy-done.21), kind=kOutput, calls=%fused_computation.73 | convolution fusion | flops 6446120960 | bytes 7340032 | tf_op jit(solution)/shard_map/dot_general | solution.py:96
  622.6 10.3 %all-to-all-done.7 = f32[8,2,256,128]{2,3,1,0:T(8,128)} async-done(((f32[8,2,256,128]{2,3,1,0:T(8,128)}), f32[8,2,256,128]{2,3,1,0:T(8,128)}, u32[]{:S(2)}, u32[]{:S(2)}) %all-to-all-start.7) | async-done | bytes 2097184 | tf_op jit(solution)/shard_map/all_to_all | solution.py:210
  636.7 9.9 %fusion.60 = f32[1024,512]{1,0:T(8,128)S(1)} fusion(f32[512,512]{1,0:T(8,128)S(1)} %reshape_reshape_squeeze.31, f32[512,512]{1,0:T(8,128)} %reshape_reshape_squeeze.30, f32[512,512]{1,0:T(8,128)} %get-tuple-element.218, f32[512,512]{1,0:T(8,128)} %get-tuple-element.217, f32[512,512]{1,0:T(8,128)S(1)} %copy-done.22), kind=kOutput, calls=%fused_computation.79 | convolution fusion | flops 6446120960 | bytes 7340032 | tf_op jit(solution)/shard_map/dot_general | solution.py:96
  662.4 48.6 %reduce-scatter.11.cloned.1.call-done = f32[2,1024,128]{2,1,0:T(8,128)} async-done(((f32[2,4096,128]{2,1,0:T(8,128)}), f32[2,1024,128]{2,1,0:T(8,128)}) %reduce-scatter.11.cloned.1.call-update) | async-done | bytes 1048592 | tf_op jit(solution)/shard_map/reduce_scatter | solution.py:226
  711.0 55.5 %reduce-scatter.9.cloned.1.call-done = f32[2,1024,128]{2,1,0:T(8,128)} async-done(((f32[2,4096,128]{2,1,0:T(8,128)}), f32[2,1024,128]{2,1,0:T(8,128)}) %reduce-scatter.9.cloned.1.call-update) | async-done | bytes 1048592 | tf_op jit(solution)/shard_map/reduce_scatter | solution.py:226
  766.5 55.6 %reduce-scatter.7.cloned.1.call-done = f32[2,1024,128]{2,1,0:T(8,128)} async-done(((f32[2,4096,128]{2,1,0:T(8,128)}), f32[2,1024,128]{2,1,0:T(8,128)}) %reduce-scatter.7.cloned.1.call-update) | async-done | bytes 1048592 | tf_op jit(solution)/shard_map/reduce_scatter | solution.py:226
  822.1 55.6 %reduce-scatter.5.cloned.1.call-done = f32[2,1024,128]{2,1,0:T(8,128)} async-done(((f32[2,4096,128]{2,1,0:T(8,128)}), f32[2,1024,128]{2,1,0:T(8,128)}) %reduce-scatter.5.cloned.1.call-update) | async-done | bytes 1048592 | tf_op jit(solution)/shard_map/reduce_scatter | solution.py:226
  (243 shorter events, 270.4 us)
Async XLA Ops:
  6.5 59.9 %all-gather.5.cloned.1.call-start = ((), (), s32[]{:S(2)}) async-start(), calls=%async_computation.12 | async-start | bytes 5242880 | tf_op jit(solution)/shard_map/all_gather | solution.py:160
  10.9 14.1 %copy-start.23 = (f32[6]{0:T(128)S(1)}, f32[6]{0:T(128)}, u32[]{:S(2)}) copy-start(f32[6]{0:T(128)} %param.7) | copy-start | bytes 76
  11.0 109.9 %all-gather.7.cloned.1.call-start = ((), (), s32[]{:S(2)}) async-start(), calls=%async_computation.13 | async-start | bytes 5242880 | tf_op jit(solution)/shard_map/all_gather | solution.py:160
  11.7 163.6 %all-gather.9.cloned.1.call-start = ((), (), s32[]{:S(2)}) async-start(), calls=%async_computation.14 | async-start | bytes 5242880 | tf_op jit(solution)/shard_map/all_gather | solution.py:160
  12.4 217.2 %all-gather.11.cloned.1.call-start = ((), (), s32[]{:S(2)}) async-start(), calls=%async_computation.15 | async-start | bytes 5242880 | tf_op jit(solution)/shard_map/all_gather | solution.py:160
  20.3 50.0 %copy-start.18 = (f32[512,512]{1,0:T(8,128)}, f32[512,512]{1,0:T(8,128)S(1)}, u32[]{:S(2)}) copy-start(f32[512,512]{1,0:T(8,128)S(1)} %get-tuple-element.211) | copy-start | bytes 3145732
  82.8 41.9 %copy-start.19 = (f32[512,512]{1,0:T(8,128)S(1)}, f32[512,512]{1,0:T(8,128)}, u32[]{:S(2)}) copy-start(f32[512,512]{1,0:T(8,128)} %copy-done.18) | copy-start | bytes 3145732
  137.4 64.8 %all-to-all-start.1 = ((f32[8,2,256,128]{2,3,1,0:T(8,128)}), f32[8,2,256,128]{2,3,1,0:T(8,128)S(1)}, u32[]{:S(2)}, u32[]{:S(2)}) async-start(f32[8,2,256,128]{2,3,1,0:T(8,128)} %pad_maximum_fusion.2), calls=%async_computation.1 | async-start | bytes 4194304 | tf_op jit(solution)/shard_map/all_to_all | solution.py:178
  202.2 31.0 %copy-start.7 = (f32[8,2,256,128]{2,3,1,0:T(8,128)}, f32[8,2,256,128]{2,3,1,0:T(8,128)S(1)}, u32[]{:S(2)}) copy-start(f32[8,2,256,128]{2,3,1,0:T(8,128)S(1)} %all-to-all-done.1) | copy-start | bytes 6291460
  202.2 53.8 %all-to-all-start.2 = ((f32[8,2,256,128]{2,3,1,0:T(8,128)}), f32[8,2,256,128]{2,3,1,0:T(8,128)}, u32[]{:S(2)}, u32[]{:S(2)}) async-start(f32[8,2,256,128]{2,3,1,0:T(8,128)} %pad_maximum_fusion.3), calls=%async_computation.2 | async-start | bytes 4194304 | tf_op jit(solution)/shard_map/all_to_all | solution.py:178
  308.2 53.8 %all-to-all-start = ((f32[8,2,256,128]{2,3,1,0:T(8,128)}), f32[8,2,256,128]{2,3,1,0:T(8,128)}, u32[]{:S(2)}, u32[]{:S(2)}) async-start(f32[8,2,256,128]{2,3,1,0:T(8,128)} %pad_maximum_fusion.1), calls=%async_computation | async-start | bytes 4194304 | tf_op jit(solution)/shard_map/all_to_all | solution.py:178
  324.4 6.3 copy-start.8
  366.5 5.4 copy-start.16
  366.5 5.4 copy-start.17
  371.9 9.2 %copy-start.5 = (f32[2,2,256,8,8]{3,4,0,1,2:T(8,128)S(1)}, f32[2,2,256,8,8]{3,4,0,1,2:T(8,128)}, u32[]{:S(2)}) copy-start(f32[2,2,256,8,8]{3,4,0,1,2:T(8,128)} %copy.90) | copy-start | bytes 786436
  397.4 9.2 %copy-start.4 = (f32[2,2,256,8,8]{3,4,0,1,2:T(8,128)S(1)}, f32[2,2,256,8,8]{3,4,0,1,2:T(8,128)}, u32[]{:S(2)}) copy-start(f32[2,2,256,8,8]{3,4,0,1,2:T(8,128)} %copy.98) | copy-start | bytes 786436
  419.6 52.6 %all-to-all-start.4 = ((f32[8,2,256,128]{2,3,1,0:T(8,128)}), f32[8,2,256,128]{2,3,1,0:T(8,128)S(1)}, u32[]{:S(2)}, u32[]{:S(2)}) async-start(f32[8,2,256,128]{2,3,1,0:T(8,128)} %copy.101), calls=%async_computation.4 | async-start | bytes 4194304 | tf_op jit(solution)/shard_map/all_to_all | solution.py:210
  472.2 53.8 %all-to-all-start.5 = ((f32[8,2,256,128]{2,3,1,0:T(8,128)}), f32[8,2,256,128]{2,3,1,0:T(8,128)}, u32[]{:S(2)}, u32[]{:S(2)}) async-start(f32[8,2,256,128]{2,3,1,0:T(8,128)} %copy.104), calls=%async_computation.6 | async-start | bytes 4194304 | tf_op jit(solution)/shard_map/all_to_all | solution.py:210
  526.0 53.6 %all-to-all-start.6 = ((f32[8,2,256,128]{2,3,1,0:T(8,128)}), f32[8,2,256,128]{2,3,1,0:T(8,128)}, u32[]{:S(2)}, u32[]{:S(2)}) async-start(f32[8,2,256,128]{2,3,1,0:T(8,128)} %copy.107), calls=%async_computation.8 | async-start | bytes 4194304 | tf_op jit(solution)/shard_map/all_to_all | solution.py:210
  579.5 53.4 %all-to-all-start.7 = ((f32[8,2,256,128]{2,3,1,0:T(8,128)}), f32[8,2,256,128]{2,3,1,0:T(8,128)}, u32[]{:S(2)}, u32[]{:S(2)}) async-start(f32[8,2,256,128]{2,3,1,0:T(8,128)} %copy.110), calls=%async_computation.10 | async-start | bytes 4194304 | tf_op jit(solution)/shard_map/all_to_all | solution.py:210
  583.9 127.1 %reduce-scatter.11.cloned.1.call-start = ((), (), s32[]{:S(2)}) async-start(), calls=%async_computation.19 | async-start | bytes 5242880 | tf_op jit(solution)/shard_map/reduce_scatter | solution.py:226
  660.3 106.1 %reduce-scatter.9.cloned.1.call-start = ((), (), s32[]{:S(2)}) async-start(), calls=%async_computation.18 | async-start | bytes 5242880 | tf_op jit(solution)/shard_map/reduce_scatter | solution.py:226
  660.9 161.2 %reduce-scatter.7.cloned.1.call-start = ((), (), s32[]{:S(2)}) async-start(), calls=%async_computation.17 | async-start | bytes 5242880 | tf_op jit(solution)/shard_map/reduce_scatter | solution.py:226
  661.7 216.0 %reduce-scatter.5.cloned.1.call-start = ((), (), s32[]{:S(2)}) async-start(), calls=%async_computation.16 | async-start | bytes 5242880 | tf_op jit(solution)/shard_map/reduce_scatter | solution.py:226
  (16 other events, 41.6 us)
Sparse Core Ops, SparseCore 0:
  11.1 55.3 all-gather.4
  68.3 52.5 all-gather.6
  122.7 52.5 all-gather.8
  177.0 52.5 all-gather.10
  660.5 50.5 reduce-scatter.10
  713.9 52.5 reduce-scatter.8
  769.5 52.5 reduce-scatter.6
  825.1 52.5 reduce-scatter.4

commit v7 on v6

--- a/solution.py
+++ b/solution.py
@@ -59,7 +59,7 @@
         "p" + inputs + ",pqtk->q" + middle, paired, first_table, precision=HIGHEST_PRECISION
     )
     return jnp.einsum(
-        "p" + middle + ",pqkrj->q" + output, middle_pair, second_table, precision=HIGHEST_PRECISION
+        "p" + middle + ",pqkrj->q" + output, middle_pair, second_table, precision=lax.Precision.HIGH
     )
 
 
@@ -224,8 +224,11 @@
             embedded, jnp.stack([upd_re, upd_im]), row_shift, 1
         )
         results.append(lax.psum_scatter(embedded, "led", scatter_dimension=1, tiled=True))
-    summed = jnp.concatenate(results, axis=2)
-    return spectrum + summed
+    out = spectrum
+    for chunk in range(chunks):
+        added = spectrum[:, :, chunk * width:(chunk + 1) * width] + results[chunk]
+        out = lax.dynamic_update_slice_in_dim(out, added, chunk * width, 2)
+    return out
 
 
 def solution(mesh):

time: 896 us -> 784 us (0.88)
  waiting for transfers between devices: 450 us -> 258 us
  blocking collectives: 52.2 us -> 155 us
  starting transfers between devices: 31.5 us -> 21.4 us
    reduce_scatter x4, waiting for transfers between devices: 215 us -> 38.1 us  [on_device(): lax.psum_scatter(embedded, 'led', scatter_dimension=1, tiled=True)]
    all_to_all x1 -> x3, blocking collectives: 52.2 us -> 155 us  [on_device(): lax.all_to_all(piece, 'row', split_axis=0, concat_axis=0, tiled=True)]
    all_to_all x3 -> x4, waiting for transfers between devices: 33.7 us -> 128 us  [on_device(): lax.all_to_all(stacked, 'row', split_axis=0, concat_axis=0, tiled=True)]
    all_gather x4, waiting for transfers between devices: 106 us -> 51.3 us  [on_device(): regions.append(lax.all_gather(part, 'led', axis=1, tiled=True))]
    all_to_all x4 -> x1, waiting for transfers between devices: 90.6 us -> 39 us  [on_device(): lax.all_to_all(piece, 'row', split_axis=0, concat_axis=0, tiled=True)]
    all_to_all x4 -> x1, starting transfers between devices: 17.2 us -> 3.6 us  [on_device(): lax.all_to_all(piece, 'row', split_axis=0, concat_axis=0, tiled=True)]
    dynamic_update_slice x0 -> x4, other arithmetic: none -> 10.6 us  [on_device(): out = lax.dynamic_update_slice_in_dim(out, added, chunk * width, 2)]
  transfers between devices with their start and end apart: 15 -> 13, of which waited for: 14 -> 8; matrix products, arithmetic and copies ran while one was open for 27% -> 30% of each run, Pallas kernels for 0% -> 0%
where the time goes in v7:
time: 784 us; the launch traced here: 779 us
  waiting for transfers between devices  258 us (33%)
  blocking collectives  155 us (20%)
  local copies, waits for them, and re-layouts  113 us (14%)
  other arithmetic  108 us (14%)
  matrix products  105 us (13%)
  starting transfers between devices  21.4 us (3%)
  between operations  18.4 us (2%)
    all_to_all x3, blocking collectives, on_device(): lax.all_to_all(piece, 'row', split_axis=0, concat_axis=0, tiled=True)  155 us
    all_to_all x4, waiting for transfers between devices, on_device(): lax.all_to_all(stacked, 'row', split_axis=0, concat_axis=0, tiled=True)  128 us
    dot_general x8, matrix products, row_transform(): middle = jnp.dot(table, stacked, precision=HIGHEST_PRECISION)  76.6 us
    all_gather x4, waiting for transfers between devices, on_device(): regions.append(lax.all_gather(part, 'led', axis=1, tiled=True))  51.3 us
    all_to_all x1, waiting for transfers between devices, on_device(): lax.all_to_all(piece, 'row', split_axis=0, concat_axis=0, tiled=True)  39 us
    reduce_scatter x4, waiting for transfers between devices, on_device(): lax.psum_scatter(embedded, 'led', scatter_dimension=1, tiled=True)  38.1 us
    dynamic_update_slice x4, local copies, waits for them, and re-layouts, on_device(): lax.dynamic_update_slice_in_dim(embedded, jnp.stack([upd_re, upd_im]), ro...  28.4 us
    mul x1, other arithmetic, pupil_at(): return (weight * jnp.cos(phases), weight * jnp.sin(phases))  24.3 us
  transfers between devices with their start and end apart: 13, of which 8 were waited for; matrix products, arithmetic and copies ran while one was open for 30% of the time, Pallas kernels for 0%

profile of v7, /device:TPU:0, one launch (start us, length us, event | category | flops | bytes accessed | tf_op | source)
XLA Modules:
  0.0 779.1 jit_solution(3550481159463387325)
XLA Ops:
  26.8 24.3 %select_multiply_fusion = (f32[2048,512]{1,0:T(8,128)}, f32[2048,512]{1,0:T(8,128)}) fusion(f32[]{:T(128)} %bitcast.6, f32[512]{0:T(512)S(1)} %get-tuple-element.207, f32[2048]{0:T(1024)S(1)} %get-tuple-element.210, f32[512]{0:T(512)S(1)} %get-tuple-element.208, f32[2048]{0:T(1024)S(1)} %convert_multiply_fusion.1, f32[]{:T(128)} %bitcast.3, f32[]{:T(128)} %bitcast.2, ...), kind=kLoop, calls=%fused_computation.5 | loop fusion | flops 27262976 | bytes 8429584 | tf_op jit(solution)/shard_map/mul | solution.py:29
  53.3 13.1 %all-gather.5.cloned.1.call-done = f32[2,4096,128]{2,1,0:T(8,128)} async-done(((f32[2,1024,128]{2,1,0:T(8,128)}), f32[2,4096,128]{2,1,0:T(8,128)}) %all-gather.5.cloned.1.call-update) | async-done | bytes 4194320 | tf_op jit(solution)/shard_map/all_gather | solution.py:160
  70.3 8.9 %fusion.32 = f32[1024,512]{1,0:T(8,128)S(1)} fusion(f32[512,512]{1,0:T(8,128)S(1)} %reshape.412, f32[512,512]{1,0:T(8,128)} %reshape.411, f32[512,512]{1,0:T(8,128)} %get-tuple-element.212, f32[512,512]{1,0:T(8,128)S(1)} %get-tuple-element.211, f32[512,512]{1,0:T(8,128)} %fusion.81), kind=kOutput, calls=%fused_computation.39 | convolution fusion | flops 6446120960 | bytes 7340032 | tf_op jit(solution)/shard_map/dot_general | solution.py:96
  82.7 38.1 %all-gather.7.cloned.1.call-done = f32[2,4096,128]{2,1,0:T(8,128)} async-done(((f32[2,1024,128]{2,1,0:T(8,128)}), f32[2,4096,128]{2,1,0:T(8,128)}) %all-gather.7.cloned.1.call-update) | async-done | bytes 4194320 | tf_op jit(solution)/shard_map/all_gather | solution.py:160
  124.7 9.1 %fusion.36 = f32[1024,512]{1,0:T(8,128)S(1)} fusion(f32[512,512]{1,0:T(8,128)S(1)} %reshape.414, f32[512,512]{1,0:T(8,128)} %reshape.413, f32[512,512]{1,0:T(8,128)} %get-tuple-element.212, f32[512,512]{1,0:T(8,128)S(1)} %copy-done.25, f32[512,512]{1,0:T(8,128)} %fusion.81), kind=kOutput, calls=%fused_computation.44 | convolution fusion | flops 6446120960 | bytes 7340032 | tf_op jit(solution)/shard_map/dot_general | solution.py:96
  142.6 48.5 %all-to-all-done.1 = f32[8,2,256,128]{2,3,1,0:T(8,128)S(1)} async-done(((f32[8,2,256,128]{2,3,1,0:T(8,128)}), f32[8,2,256,128]{2,3,1,0:T(8,128)S(1)}, u32[]{:S(2)}, u32[]{:S(2)}) %all-to-all-start.1) | async-done | bytes 2097184 | tf_op jit(solution)/shard_map/all_to_all | solution.py:178
  200.7 9.6 %fusion.40 = f32[1024,512]{1,0:T(8,128)S(1)} fusion(f32[512,512]{1,0:T(8,128)S(1)} %reshape.416, f32[512,512]{1,0:T(8,128)S(1)} %reshape.415, f32[512,512]{1,0:T(8,128)} %get-tuple-element.212, f32[512,512]{1,0:T(8,128)} %copy-done.24, f32[512,512]{1,0:T(8,128)} %fusion.81), kind=kOutput, calls=%fused_computation.49 | convolution fusion | flops 6446120960 | bytes 7340032 | tf_op jit(solution)/shard_map/dot_general | solution.py:96
  214.0 30.5 %all-to-all-done = f32[8,2,256,128]{2,3,1,0:T(8,128)} async-done(((f32[8,2,256,128]{2,3,1,0:T(8,128)}), f32[8,2,256,128]{2,3,1,0:T(8,128)}, u32[]{:S(2)}, u32[]{:S(2)}) %all-to-all-start) | async-done | bytes 2097184 | tf_op jit(solution)/shard_map/all_to_all | solution.py:178
  255.7 10.2 %fusion.44 = f32[1024,512]{1,0:T(8,128)S(1)} fusion(f32[512,512]{1,0:T(8,128)} %reshape.418, f32[512,512]{1,0:T(8,128)} %reshape.417, f32[512,512]{1,0:T(8,128)} %get-tuple-element.212, f32[512,512]{1,0:T(8,128)} %copy-done.24, f32[512,512]{1,0:T(8,128)} %fusion.81), kind=kOutput, calls=%fused_computation.54 | convolution fusion | flops 6446120960 | bytes 7340032 | tf_op jit(solution)/shard_map/dot_general | solution.py:96
  275.1 22.4 %all-to-all-done.2 = f32[8,2,256,128]{2,3,1,0:T(8,128)S(1)} async-done(((f32[8,2,256,128]{2,3,1,0:T(8,128)}), f32[8,2,256,128]{2,3,1,0:T(8,128)S(1)}, u32[]{:S(2)}, u32[]{:S(2)}) %all-to-all-start.2) | async-done | bytes 2097184 | tf_op jit(solution)/shard_map/all_to_all | solution.py:178
  324.4 26.7 %all-to-all-done.3 = f32[8,2,256,128]{2,3,1,0:T(8,128)} async-done(((f32[8,2,256,128]{2,3,1,0:T(8,128)}), f32[8,2,256,128]{2,3,1,0:T(8,128)}, u32[]{:S(2)}, u32[]{:S(2)}) %all-to-all-start.3) | async-done | bytes 2097184 | tf_op jit(solution)/shard_map/all_to_all | solution.py:178
  360.9 9.2 %fusion.27 = f32[2,256,256,8,1]{1,2,3,0,4:T(8,128)S(1)} fusion(f32[2,256,256,8]{2,1,0,3:T(8,128)} %copy.89, f32[1,2,256,256]{2,3,0,1:T(8,128)S(1)} %copy-done.23, f32[1,2,256,256]{2,3,0,1:T(8,128)S(1)} %copy-done.22), kind=kOutput, calls=%fused_computation.36 | convolution fusion | flops 6442713088 | bytes 9437184 | tf_op jit(solution)/shard_map/pytr,pqtk->qykr/dot_general | solution.py:58
  384.2 9.4 %fusion.26 = f32[2,256,256,8,1]{1,2,3,0,4:T(8,128)S(1)} fusion(f32[1,256,256,8]{2,1,0,3:T(8,128)} %copy.96, f32[1,256,256,8]{2,1,0,3:T(8,128)} %copy.95, f32[1,2,256,256]{2,3,1,0:T(8,128)S(1)} %copy-done.21, f32[1,2,256,256]{2,3,1,0:T(8,128)S(1)} %copy-done.20), kind=kOutput, calls=%fused_computation.35 | convolution fusion | flops 6443761664 | bytes 9437184 | tf_op jit(solution)/shard_map/pytr,pqtk->qykr/dot_general | solution.py:58
  417.9 39.0 %all-to-all-done.4 = f32[8,2,256,128]{2,3,1,0:T(8,128)S(1)} async-done(((f32[8,2,256,128]{2,3,1,0:T(8,128)}), f32[8,2,256,128]{2,3,1,0:T(8,128)S(1)}, u32[]{:S(2)}, u32[]{:S(2)}) %all-to-all-start.4) | async-done | bytes 2097184 | tf_op jit(solution)/shard_map/all_to_all | solution.py:210
  461.4 9.7 %fusion.48 = f32[1024,512]{1,0:T(8,128)S(1)} fusion(f32[512,512]{1,0:T(8,128)S(1)} %reshape_reshape_squeeze.25, f32[512,512]{1,0:T(8,128)} %reshape_reshape_squeeze.24, f32[512,512]{1,0:T(8,128)} %get-tuple-element.218, f32[512,512]{1,0:T(8,128)} %get-tuple-element.217, f32[512,512]{1,0:T(8,128)S(1)} %copy-done.26), kind=kOutput, calls=%fused_computation.60 | convolution fusion | flops 6446120960 | bytes 7340032 | tf_op jit(solution)/shard_map/dot_general | solution.py:96
  477.7 7.1 dynamic_update_slice.24
  485.4 51.7 %all_to_all.40 = f32[8,2,256,128]{2,3,1,0:T(8,128)S(1)} all-to-all(f32[8,2,256,128]{2,3,1,0:T(8,128)S(1)} %copy.104), channel_id=1, replica_groups=mesh['led'=4,'row'=8] {'row'}, dimensions={0} | all-to-all | bytes 4194304 | tf_op jit(solution)/shard_map/all_to_all | solution.py:210
  539.2 9.7 %fusion.52 = f32[1024,512]{1,0:T(8,128)S(1)} fusion(f32[512,512]{1,0:T(8,128)S(1)} %reshape_reshape_squeeze.27, f32[512,512]{1,0:T(8,128)} %reshape_reshape_squeeze.26, f32[512,512]{1,0:T(8,128)} %get-tuple-element.218, f32[512,512]{1,0:T(8,128)} %get-tuple-element.217, f32[512,512]{1,0:T(8,128)S(1)} %copy-done.27), kind=kOutput, calls=%fused_computation.66 | convolution fusion | flops 6446120960 | bytes 7340032 | tf_op jit(solution)/shard_map/dot_general | solution.py:96
  563.3 51.7 %all_to_all.41 = f32[8,2,256,128]{2,3,1,0:T(8,128)S(1)} all-to-all(f32[8,2,256,128]{2,3,1,0:T(8,128)S(1)} %copy.107), channel_id=1, replica_groups=mesh['led'=4,'row'=8] {'row'}, dimensions={0} | all-to-all | bytes 4194304 | tf_op jit(solution)/shard_map/all_to_all | solution.py:210
  617.1 9.7 %fusion.56 = f32[1024,512]{1,0:T(8,128)S(1)} fusion(f32[512,512]{1,0:T(8,128)S(1)} %reshape_reshape_squeeze.29, f32[512,512]{1,0:T(8,128)} %reshape_reshape_squeeze.28, f32[512,512]{1,0:T(8,128)} %get-tuple-element.218, f32[512,512]{1,0:T(8,128)} %get-tuple-element.217, f32[512,512]{1,0:T(8,128)S(1)} %copy-done.28), kind=kOutput, calls=%fused_computation.72 | convolution fusion | flops 6446120960 | bytes 7340032 | tf_op jit(solution)/shard_map/dot_general | solution.py:96
  633.4 7.1 dynamic_update_slice.28
  641.0 51.8 %all_to_all.42 = f32[8,2,256,128]{2,3,1,0:T(8,128)S(1)} all-to-all(f32[8,2,256,128]{2,3,1,0:T(8,128)S(1)} %copy.110), channel_id=1, replica_groups=mesh['led'=4,'row'=8] {'row'}, dimensions={0} | all-to-all | bytes 4194304 | tf_op jit(solution)/shard_map/all_to_all | solution.py:210
  694.9 9.7 %fusion.60 = f32[1024,512]{1,0:T(8,128)S(1)} fusion(f32[512,512]{1,0:T(8,128)S(1)} %reshape_reshape_squeeze.31, f32[512,512]{1,0:T(8,128)} %reshape_reshape_squeeze.30, f32[512,512]{1,0:T(8,128)} %get-tuple-element.218, f32[512,512]{1,0:T(8,128)} %get-tuple-element.217, f32[512,512]{1,0:T(8,128)S(1)} %copy-done.29), kind=kOutput, calls=%fused_computation.78 | convolution fusion | flops 6446120960 | bytes 7340032 | tf_op jit(solution)/shard_map/dot_general | solution.py:96
  731.0 38.1 %reduce-scatter.11.cloned.1.call-done = f32[2,1024,128]{2,1,0:T(8,128)} async-done(((f32[2,4096,128]{2,1,0:T(8,128)}), f32[2,1024,128]{2,1,0:T(8,128)}) %reduce-scatter.11.cloned.1.call-update) | async-done | bytes 1048592 | tf_op jit(solution)/shard_map/reduce_scatter | solution.py:226
  (259 shorter events, 215.3 us)
Async XLA Ops:
  6.5 5.9 copy-start.31
  6.5 59.8 %all-gather.5.cloned.1.call-start = ((), (), s32[]{:S(2)}) async-start(), calls=%async_computation.12 | async-start | bytes 5242880 | tf_op jit(solution)/shard_map/all_gather | solution.py:160
  10.9 13.4 %copy-start.30 = (f32[6]{0:T(128)S(1)}, f32[6]{0:T(128)}, u32[]{:S(2)}) copy-start(f32[6]{0:T(128)} %param.7) | copy-start | bytes 76
  10.9 109.9 %all-gather.7.cloned.1.call-start = ((), (), s32[]{:S(2)}) async-start(), calls=%async_computation.13 | async-start | bytes 5242880 | tf_op jit(solution)/shard_map/all_gather | solution.py:160
  11.7 183.8 %all-gather.9.cloned.1.call-start = ((), (), s32[]{:S(2)}) async-start(), calls=%async_computation.14 | async-start | bytes 5242880 | tf_op jit(solution)/shard_map/all_gather | solution.py:160
  19.5 50.7 %copy-start.24 = (f32[512,512]{1,0:T(8,128)}, f32[512,512]{1,0:T(8,128)S(1)}, u32[]{:S(2)}) copy-start(f32[512,512]{1,0:T(8,128)S(1)} %get-tuple-element.211) | copy-start | bytes 3145732
  82.7 41.9 %copy-start.25 = (f32[512,512]{1,0:T(8,128)S(1)}, f32[512,512]{1,0:T(8,128)}, u32[]{:S(2)}) copy-start(f32[512,512]{1,0:T(8,128)} %copy-done.24) | copy-start | bytes 3145732
  137.5 53.6 %all-to-all-start.1 = ((f32[8,2,256,128]{2,3,1,0:T(8,128)}), f32[8,2,256,128]{2,3,1,0:T(8,128)S(1)}, u32[]{:S(2)}, u32[]{:S(2)}) async-start(f32[8,2,256,128]{2,3,1,0:T(8,128)} %pad_maximum_fusion.2), calls=%async_computation.1 | async-start | bytes 4194304 | tf_op jit(solution)/shard_map/all_to_all | solution.py:178
  142.1 106.5 %all-gather.11.cloned.1.call-start = ((), (), s32[]{:S(2)}) async-start(), calls=%async_computation.15 | async-start | bytes 5242880 | tf_op jit(solution)/shard_map/all_gather | solution.py:160
  191.1 8.0 %copy-start.11 = (f32[8,2,256,128]{2,3,1,0:T(8,128)}, f32[8,2,256,128]{2,3,1,0:T(8,128)S(1)}, u32[]{:S(2)}) copy-start(f32[8,2,256,128]{2,3,1,0:T(8,128)S(1)} %all-to-all-done.1) | copy-start | bytes 6291460
  191.1 53.4 %all-to-all-start = ((f32[8,2,256,128]{2,3,1,0:T(8,128)}), f32[8,2,256,128]{2,3,1,0:T(8,128)}, u32[]{:S(2)}, u32[]{:S(2)}) async-start(f32[8,2,256,128]{2,3,1,0:T(8,128)} %pad_maximum_fusion.1), calls=%async_computation | async-start | bytes 4194304 | tf_op jit(solution)/shard_map/all_to_all | solution.py:178
  244.5 53.0 %all-to-all-start.2 = ((f32[8,2,256,128]{2,3,1,0:T(8,128)}), f32[8,2,256,128]{2,3,1,0:T(8,128)S(1)}, u32[]{:S(2)}, u32[]{:S(2)}) async-start(f32[8,2,256,128]{2,3,1,0:T(8,128)} %pad_maximum_fusion.3), calls=%async_computation.2 | async-start | bytes 4194304 | tf_op jit(solution)/shard_map/all_to_all | solution.py:178
  297.5 53.6 %all-to-all-start.3 = ((f32[8,2,256,128]{2,3,1,0:T(8,128)}), f32[8,2,256,128]{2,3,1,0:T(8,128)}, u32[]{:S(2)}, u32[]{:S(2)}) async-start(f32[8,2,256,128]{2,3,1,0:T(8,128)} %pad_maximum_fusion.4), calls=%async_computation.3 | async-start | bytes 4194304 | tf_op jit(solution)/shard_map/all_to_all | solution.py:178
  313.5 6.3 copy-start.12
  360.9 9.2 %copy-start.9 = (f32[2,2,256,8,8]{3,4,0,1,2:T(8,128)S(1)}, f32[2,2,256,8,8]{3,4,0,1,2:T(8,128)}, u32[]{:S(2)}) copy-start(f32[2,2,256,8,8]{3,4,0,1,2:T(8,128)} %copy.90) | copy-start | bytes 786436
  384.2 9.4 %copy-start.8 = (f32[2,2,256,8,8]{3,4,0,1,2:T(8,128)S(1)}, f32[2,2,256,8,8]{3,4,0,1,2:T(8,128)}, u32[]{:S(2)}) copy-start(f32[2,2,256,8,8]{3,4,0,1,2:T(8,128)} %copy.98) | copy-start | bytes 786436
  404.3 52.6 %all-to-all-start.4 = ((f32[8,2,256,128]{2,3,1,0:T(8,128)}), f32[8,2,256,128]{2,3,1,0:T(8,128)S(1)}, u32[]{:S(2)}, u32[]{:S(2)}) async-start(f32[8,2,256,128]{2,3,1,0:T(8,128)} %copy.101), calls=%async_computation.4 | async-start | bytes 4194304 | tf_op jit(solution)/shard_map/all_to_all | solution.py:210
  407.9 315.1 %reduce-scatter.5.cloned.1.call-start = ((), (), s32[]{:S(2)}) async-start(), calls=%async_computation.16 | async-start | bytes 5242880 | tf_op jit(solution)/shard_map/reduce_scatter | solution.py:226
  477.7 7.2 copy-start.17
  484.9 240.8 %reduce-scatter.7.cloned.1.call-start = ((), (), s32[]{:S(2)}) async-start(), calls=%async_computation.17 | async-start | bytes 5242880 | tf_op jit(solution)/shard_map/reduce_scatter | solution.py:226
  555.6 7.2 copy-start.16
  562.8 165.6 %reduce-scatter.9.cloned.1.call-start = ((), (), s32[]{:S(2)}) async-start(), calls=%async_computation.18 | async-start | bytes 5242880 | tf_op jit(solution)/shard_map/reduce_scatter | solution.py:226
  633.4 7.2 copy-start.15
  640.6 128.6 %reduce-scatter.11.cloned.1.call-start = ((), (), s32[]{:S(2)}) async-start(), calls=%async_computation.19 | async-start | bytes 5242880 | tf_op jit(solution)/shard_map/reduce_scatter | solution.py:226
  (21 other events, 65.1 us)
Sparse Core Ops, SparseCore 0:
  11.0 55.2 all-gather.4
  68.2 52.5 all-gather.6
  122.7 52.5 all-gather.8
  177.0 52.5 all-gather.10
  485.0 50.5 reduce-scatter.4
  562.9 50.5 reduce-scatter.6
  640.7 50.5 reduce-scatter.8
  718.5 50.6 reduce-scatter.10

commit v8 on v7

--- a/solution.py
+++ b/solution.py
@@ -78,7 +78,7 @@
     return value_re * c - value_im * s, value_re * s + value_im * c
 
 
-def row_transform(pair_re, pair_im, direction, inner=4):
+def row_transform(pair_re, pair_im, direction, inner=4, precision=HIGHEST_PRECISION):
     length, width = pair_re.shape
     outer = length // inner
     angle_step = direction * 2.0 * math.pi / outer
@@ -93,7 +93,7 @@
     stacked = jnp.concatenate(
         [pair_re.reshape(outer, inner * width), pair_im.reshape(outer, inner * width)], axis=0
     )
-    middle = jnp.dot(table, stacked, precision=HIGHEST_PRECISION)
+    middle = jnp.dot(table, stacked, precision=precision)
     mid_re = middle[:outer]
     mid_im = middle[outer:]
     scaling = 1.0 / math.sqrt(length)
@@ -167,7 +167,10 @@
         pupil_re, pupil_im = pupils[chunk]
         lit_re = pupil_re * band[0] - pupil_im * band[1]
         lit_im = pupil_re * band[1] + pupil_im * band[0]
-        half_re, half_im = row_transform(lit_re, lit_im, 1.0)
+        last = chunk == chunks - 1 and chunks > 1
+        half_re, half_im = row_transform(
+            lit_re, lit_im, 1.0, precision=lax.Precision.HIGH if last else HIGHEST_PRECISION
+        )
         stacked = jnp.stack(
             [
                 half_re.reshape(row_count, block_rows, width),

time: 784 us -> 783 us (level)
  transfers between devices with their start and end apart: 13 -> 13, of which waited for: 8 -> 8; matrix products, arithmetic and copies ran while one was open for 30% -> 29% of each run, Pallas kernels for 0% -> 0%
where the time goes in v8:
time: 783 us; the launch traced here: 778 us
  waiting for transfers between devices  262 us (33%)
  blocking collectives  155 us (20%)
  local copies, waits for them, and re-layouts  113 us (14%)
  other arithmetic  108 us (14%)
  matrix products  100 us (13%)
  starting transfers between devices  21.2 us (3%)
  between operations  18.1 us (2%)
    all_to_all x3, blocking collectives, on_device(): lax.all_to_all(piece, 'row', split_axis=0, concat_axis=0, tiled=True)  155 us
    all_to_all x4, waiting for transfers between devices, on_device(): lax.all_to_all(stacked, 'row', split_axis=0, concat_axis=0, tiled=True)  132 us
    dot_general x8, matrix products, row_transform(): middle = jnp.dot(table, stacked, precision=precision)  72.5 us
    all_gather x4, waiting for transfers between devices, on_device(): regions.append(lax.all_gather(part, 'led', axis=1, tiled=True))  50.9 us
    all_to_all x1, waiting for transfers between devices, on_device(): lax.all_to_all(piece, 'row', split_axis=0, concat_axis=0, tiled=True)  38.8 us
    reduce_scatter x4, waiting for transfers between devices, on_device(): lax.psum_scatter(embedded, 'led', scatter_dimension=1, tiled=True)  38.1 us
    dynamic_update_slice x4, local copies, waits for them, and re-layouts, on_device(): lax.dynamic_update_slice_in_dim(embedded, jnp.stack([upd_re, upd_im]), ro...  28.4 us
    mul x1, other arithmetic, pupil_at(): return (weight * jnp.cos(phases), weight * jnp.sin(phases))  24.7 us
  transfers between devices with their start and end apart: 13, of which 8 were waited for; matrix products, arithmetic and copies ran while one was open for 29% of the time, Pallas kernels for 0%

profile of v8, /device:TPU:0, one launch (start us, length us, event | category | flops | bytes accessed | tf_op | source)
XLA Modules:
  0.0 778.1 jit_solution(9775148555650598221)
XLA Ops:
  26.8 24.7 %select_multiply_fusion = (f32[2048,512]{1,0:T(8,128)}, f32[2048,512]{1,0:T(8,128)}) fusion(f32[]{:T(128)} %bitcast.6, f32[512]{0:T(512)S(1)} %get-tuple-element.207, f32[2048]{0:T(1024)S(1)} %get-tuple-element.210, f32[512]{0:T(512)S(1)} %get-tuple-element.208, f32[2048]{0:T(1024)S(1)} %convert_multiply_fusion.1, f32[]{:T(128)} %bitcast.3, f32[]{:T(128)} %bitcast.2, ...), kind=kLoop, calls=%fused_computation.5 | loop fusion | flops 27262976 | bytes 8429584 | tf_op jit(solution)/shard_map/mul | solution.py:29
  53.6 12.8 %all-gather.5.cloned.1.call-done = f32[2,4096,128]{2,1,0:T(8,128)} async-done(((f32[2,1024,128]{2,1,0:T(8,128)}), f32[2,4096,128]{2,1,0:T(8,128)}) %all-gather.5.cloned.1.call-update) | async-done | bytes 4194320 | tf_op jit(solution)/shard_map/all_gather | solution.py:160
  70.3 8.9 %fusion.32 = f32[1024,512]{1,0:T(8,128)S(1)} fusion(f32[512,512]{1,0:T(8,128)S(1)} %reshape.412, f32[512,512]{1,0:T(8,128)} %reshape.411, f32[512,512]{1,0:T(8,128)} %get-tuple-element.212, f32[512,512]{1,0:T(8,128)S(1)} %get-tuple-element.211, f32[512,512]{1,0:T(8,128)} %fusion.81), kind=kOutput, calls=%fused_computation.39 | convolution fusion | flops 6446120960 | bytes 7340032 | tf_op jit(solution)/shard_map/dot_general | solution.py:96
  82.7 38.1 %all-gather.7.cloned.1.call-done = f32[2,4096,128]{2,1,0:T(8,128)} async-done(((f32[2,1024,128]{2,1,0:T(8,128)}), f32[2,4096,128]{2,1,0:T(8,128)}) %all-gather.7.cloned.1.call-update) | async-done | bytes 4194320 | tf_op jit(solution)/shard_map/all_gather | solution.py:160
  124.7 9.1 %fusion.36 = f32[1024,512]{1,0:T(8,128)S(1)} fusion(f32[512,512]{1,0:T(8,128)S(1)} %reshape.414, f32[512,512]{1,0:T(8,128)} %reshape.413, f32[512,512]{1,0:T(8,128)} %get-tuple-element.212, f32[512,512]{1,0:T(8,128)S(1)} %copy-done.25, f32[512,512]{1,0:T(8,128)} %fusion.81), kind=kOutput, calls=%fused_computation.44 | convolution fusion | flops 6446120960 | bytes 7340032 | tf_op jit(solution)/shard_map/dot_general | solution.py:96
  142.6 48.5 %all-to-all-done.1 = f32[8,2,256,128]{2,3,1,0:T(8,128)S(1)} async-done(((f32[8,2,256,128]{2,3,1,0:T(8,128)}), f32[8,2,256,128]{2,3,1,0:T(8,128)S(1)}, u32[]{:S(2)}, u32[]{:S(2)}) %all-to-all-start.1) | async-done | bytes 2097184 | tf_op jit(solution)/shard_map/all_to_all | solution.py:181
  200.6 9.6 %fusion.40 = f32[1024,512]{1,0:T(8,128)S(1)} fusion(f32[512,512]{1,0:T(8,128)S(1)} %reshape.416, f32[512,512]{1,0:T(8,128)S(1)} %reshape.415, f32[512,512]{1,0:T(8,128)} %get-tuple-element.212, f32[512,512]{1,0:T(8,128)} %copy-done.24, f32[512,512]{1,0:T(8,128)} %fusion.81), kind=kOutput, calls=%fused_computation.49 | convolution fusion | flops 6446120960 | bytes 7340032 | tf_op jit(solution)/shard_map/dot_general | solution.py:96
  213.9 30.5 %all-to-all-done = f32[8,2,256,128]{2,3,1,0:T(8,128)} async-done(((f32[8,2,256,128]{2,3,1,0:T(8,128)}), f32[8,2,256,128]{2,3,1,0:T(8,128)}, u32[]{:S(2)}, u32[]{:S(2)}) %all-to-all-start) | async-done | bytes 2097184 | tf_op jit(solution)/shard_map/all_to_all | solution.py:181
  270.9 26.4 %all-to-all-done.2 = f32[8,2,256,128]{2,3,1,0:T(8,128)S(1)} async-done(((f32[8,2,256,128]{2,3,1,0:T(8,128)}), f32[8,2,256,128]{2,3,1,0:T(8,128)S(1)}, u32[]{:S(2)}, u32[]{:S(2)}) %all-to-all-start.2) | async-done | bytes 2097184 | tf_op jit(solution)/shard_map/all_to_all | solution.py:181
  324.1 26.7 %all-to-all-done.3 = f32[8,2,256,128]{2,3,1,0:T(8,128)} async-done(((f32[8,2,256,128]{2,3,1,0:T(8,128)}), f32[8,2,256,128]{2,3,1,0:T(8,128)}, u32[]{:S(2)}, u32[]{:S(2)}) %all-to-all-start.3) | async-done | bytes 2097184 | tf_op jit(solution)/shard_map/all_to_all | solution.py:181
  360.6 9.2 %fusion.27 = f32[2,256,256,8,1]{1,2,3,0,4:T(8,128)S(1)} fusion(f32[2,256,256,8]{2,1,0,3:T(8,128)} %copy.89, f32[1,2,256,256]{2,3,0,1:T(8,128)S(1)} %copy-done.23, f32[1,2,256,256]{2,3,0,1:T(8,128)S(1)} %copy-done.22), kind=kOutput, calls=%fused_computation.36 | convolution fusion | flops 6442713088 | bytes 9437184 | tf_op jit(solution)/shard_map/pytr,pqtk->qykr/dot_general | solution.py:58
  383.8 9.2 %fusion.26 = f32[2,256,256,8,1]{1,2,3,0,4:T(8,128)S(1)} fusion(f32[1,256,256,8]{2,1,0,3:T(8,128)} %copy.96, f32[1,256,256,8]{2,1,0,3:T(8,128)} %copy.95, f32[1,2,256,256]{2,3,1,0:T(8,128)S(1)} %copy-done.21, f32[1,2,256,256]{2,3,1,0:T(8,128)S(1)} %copy-done.20), kind=kOutput, calls=%fused_computation.35 | convolution fusion | flops 6443761664 | bytes 9437184 | tf_op jit(solution)/shard_map/pytr,pqtk->qykr/dot_general | solution.py:58
  417.5 38.8 %all-to-all-done.4 = f32[8,2,256,128]{2,3,1,0:T(8,128)S(1)} async-done(((f32[8,2,256,128]{2,3,1,0:T(8,128)}), f32[8,2,256,128]{2,3,1,0:T(8,128)S(1)}, u32[]{:S(2)}, u32[]{:S(2)}) %all-to-all-start.4) | async-done | bytes 2097184 | tf_op jit(solution)/shard_map/all_to_all | solution.py:213
  460.8 9.7 %fusion.48 = f32[1024,512]{1,0:T(8,128)S(1)} fusion(f32[512,512]{1,0:T(8,128)S(1)} %reshape_reshape_squeeze.25, f32[512,512]{1,0:T(8,128)} %reshape_reshape_squeeze.24, f32[512,512]{1,0:T(8,128)} %get-tuple-element.218, f32[512,512]{1,0:T(8,128)} %get-tuple-element.217, f32[512,512]{1,0:T(8,128)S(1)} %copy-done.26), kind=kOutput, calls=%fused_computation.60 | convolution fusion | flops 6446120960 | bytes 7340032 | tf_op jit(solution)/shard_map/dot_general | solution.py:96
  477.1 7.1 dynamic_update_slice.24
  484.8 51.6 %all_to_all.40 = f32[8,2,256,128]{2,3,1,0:T(8,128)S(1)} all-to-all(f32[8,2,256,128]{2,3,1,0:T(8,128)S(1)} %copy.104), channel_id=1, replica_groups=mesh['led'=4,'row'=8] {'row'}, dimensions={0} | all-to-all | bytes 4194304 | tf_op jit(solution)/shard_map/all_to_all | solution.py:213
  538.6 9.7 %fusion.52 = f32[1024,512]{1,0:T(8,128)S(1)} fusion(f32[512,512]{1,0:T(8,128)S(1)} %reshape_reshape_squeeze.27, f32[512,512]{1,0:T(8,128)} %reshape_reshape_squeeze.26, f32[512,512]{1,0:T(8,128)} %get-tuple-element.218, f32[512,512]{1,0:T(8,128)} %get-tuple-element.217, f32[512,512]{1,0:T(8,128)S(1)} %copy-done.27), kind=kOutput, calls=%fused_computation.66 | convolution fusion | flops 6446120960 | bytes 7340032 | tf_op jit(solution)/shard_map/dot_general | solution.py:96
  555.0 7.1 dynamic_update_slice.26
  562.6 51.7 %all_to_all.41 = f32[8,2,256,128]{2,3,1,0:T(8,128)S(1)} all-to-all(f32[8,2,256,128]{2,3,1,0:T(8,128)S(1)} %copy.107), channel_id=1, replica_groups=mesh['led'=4,'row'=8] {'row'}, dimensions={0} | all-to-all | bytes 4194304 | tf_op jit(solution)/shard_map/all_to_all | solution.py:213
  616.4 9.7 %fusion.56 = f32[1024,512]{1,0:T(8,128)S(1)} fusion(f32[512,512]{1,0:T(8,128)S(1)} %reshape_reshape_squeeze.29, f32[512,512]{1,0:T(8,128)} %reshape_reshape_squeeze.28, f32[512,512]{1,0:T(8,128)} %get-tuple-element.218, f32[512,512]{1,0:T(8,128)} %get-tuple-element.217, f32[512,512]{1,0:T(8,128)S(1)} %copy-done.28), kind=kOutput, calls=%fused_computation.72 | convolution fusion | flops 6446120960 | bytes 7340032 | tf_op jit(solution)/shard_map/dot_general | solution.py:96
  632.7 7.1 dynamic_update_slice.28
  640.4 51.7 %all_to_all.42 = f32[8,2,256,128]{2,3,1,0:T(8,128)S(1)} all-to-all(f32[8,2,256,128]{2,3,1,0:T(8,128)S(1)} %copy.110), channel_id=1, replica_groups=mesh['led'=4,'row'=8] {'row'}, dimensions={0} | all-to-all | bytes 4194304 | tf_op jit(solution)/shard_map/all_to_all | solution.py:213
  694.2 9.7 %fusion.60 = f32[1024,512]{1,0:T(8,128)S(1)} fusion(f32[512,512]{1,0:T(8,128)S(1)} %reshape_reshape_squeeze.31, f32[512,512]{1,0:T(8,128)} %reshape_reshape_squeeze.30, f32[512,512]{1,0:T(8,128)} %get-tuple-element.218, f32[512,512]{1,0:T(8,128)} %get-tuple-element.217, f32[512,512]{1,0:T(8,128)S(1)} %copy-done.29), kind=kOutput, calls=%fused_computation.78 | convolution fusion | flops 6446120960 | bytes 7340032 | tf_op jit(solution)/shard_map/dot_general | solution.py:96
  730.3 38.1 %reduce-scatter.11.cloned.1.call-done = f32[2,1024,128]{2,1,0:T(8,128)} async-done(((f32[2,4096,128]{2,1,0:T(8,128)}), f32[2,1024,128]{2,1,0:T(8,128)}) %reduce-scatter.11.cloned.1.call-update) | async-done | bytes 1048592 | tf_op jit(solution)/shard_map/reduce_scatter | solution.py:229
  (259 shorter events, 214.5 us)
Async XLA Ops:
  6.5 5.9 copy-start.31
  6.5 59.8 %all-gather.5.cloned.1.call-start = ((), (), s32[]{:S(2)}) async-start(), calls=%async_computation.12 | async-start | bytes 5242880 | tf_op jit(solution)/shard_map/all_gather | solution.py:160
  10.9 13.4 %copy-start.30 = (f32[6]{0:T(128)S(1)}, f32[6]{0:T(128)}, u32[]{:S(2)}) copy-start(f32[6]{0:T(128)} %param.7) | copy-start | bytes 76
  10.9 109.9 %all-gather.7.cloned.1.call-start = ((), (), s32[]{:S(2)}) async-start(), calls=%async_computation.13 | async-start | bytes 5242880 | tf_op jit(solution)/shard_map/all_gather | solution.py:160
  11.7 183.7 %all-gather.9.cloned.1.call-start = ((), (), s32[]{:S(2)}) async-start(), calls=%async_computation.14 | async-start | bytes 5242880 | tf_op jit(solution)/shard_map/all_gather | solution.py:160
  19.5 50.7 %copy-start.24 = (f32[512,512]{1,0:T(8,128)}, f32[512,512]{1,0:T(8,128)S(1)}, u32[]{:S(2)}) copy-start(f32[512,512]{1,0:T(8,128)S(1)} %get-tuple-element.211) | copy-start | bytes 3145732
  82.7 41.9 %copy-start.25 = (f32[512,512]{1,0:T(8,128)S(1)}, f32[512,512]{1,0:T(8,128)}, u32[]{:S(2)}) copy-start(f32[512,512]{1,0:T(8,128)} %copy-done.24) | copy-start | bytes 3145732
  137.4 53.6 %all-to-all-start.1 = ((f32[8,2,256,128]{2,3,1,0:T(8,128)}), f32[8,2,256,128]{2,3,1,0:T(8,128)S(1)}, u32[]{:S(2)}, u32[]{:S(2)}) async-start(f32[8,2,256,128]{2,3,1,0:T(8,128)} %pad_maximum_fusion.2), calls=%async_computation.1 | async-start | bytes 4194304 | tf_op jit(solution)/shard_map/all_to_all | solution.py:181
  142.0 106.4 %all-gather.11.cloned.1.call-start = ((), (), s32[]{:S(2)}) async-start(), calls=%async_computation.15 | async-start | bytes 5242880 | tf_op jit(solution)/shard_map/all_gather | solution.py:160
  191.0 8.0 %copy-start.11 = (f32[8,2,256,128]{2,3,1,0:T(8,128)}, f32[8,2,256,128]{2,3,1,0:T(8,128)S(1)}, u32[]{:S(2)}) copy-start(f32[8,2,256,128]{2,3,1,0:T(8,128)S(1)} %all-to-all-done.1) | copy-start | bytes 6291460
  191.0 53.4 %all-to-all-start = ((f32[8,2,256,128]{2,3,1,0:T(8,128)}), f32[8,2,256,128]{2,3,1,0:T(8,128)}, u32[]{:S(2)}, u32[]{:S(2)}) async-start(f32[8,2,256,128]{2,3,1,0:T(8,128)} %pad_maximum_fusion.1), calls=%async_computation | async-start | bytes 4194304 | tf_op jit(solution)/shard_map/all_to_all | solution.py:181
  244.4 53.0 %all-to-all-start.2 = ((f32[8,2,256,128]{2,3,1,0:T(8,128)}), f32[8,2,256,128]{2,3,1,0:T(8,128)S(1)}, u32[]{:S(2)}, u32[]{:S(2)}) async-start(f32[8,2,256,128]{2,3,1,0:T(8,128)} %pad_maximum_fusion.3), calls=%async_computation.2 | async-start | bytes 4194304 | tf_op jit(solution)/shard_map/all_to_all | solution.py:181
  297.4 53.4 %all-to-all-start.3 = ((f32[8,2,256,128]{2,3,1,0:T(8,128)}), f32[8,2,256,128]{2,3,1,0:T(8,128)}, u32[]{:S(2)}, u32[]{:S(2)}) async-start(f32[8,2,256,128]{2,3,1,0:T(8,128)} %pad_maximum_fusion.4), calls=%async_computation.3 | async-start | bytes 4194304 | tf_op jit(solution)/shard_map/all_to_all | solution.py:181
  313.2 6.3 copy-start.12
  360.6 9.2 %copy-start.9 = (f32[2,2,256,8,8]{3,4,0,1,2:T(8,128)S(1)}, f32[2,2,256,8,8]{3,4,0,1,2:T(8,128)}, u32[]{:S(2)}) copy-start(f32[2,2,256,8,8]{3,4,0,1,2:T(8,128)} %copy.90) | copy-start | bytes 786436
  383.8 9.2 %copy-start.8 = (f32[2,2,256,8,8]{3,4,0,1,2:T(8,128)S(1)}, f32[2,2,256,8,8]{3,4,0,1,2:T(8,128)}, u32[]{:S(2)}) copy-start(f32[2,2,256,8,8]{3,4,0,1,2:T(8,128)} %copy.98) | copy-start | bytes 786436
  403.7 52.6 %all-to-all-start.4 = ((f32[8,2,256,128]{2,3,1,0:T(8,128)}), f32[8,2,256,128]{2,3,1,0:T(8,128)S(1)}, u32[]{:S(2)}, u32[]{:S(2)}) async-start(f32[8,2,256,128]{2,3,1,0:T(8,128)} %copy.101), calls=%async_computation.4 | async-start | bytes 4194304 | tf_op jit(solution)/shard_map/all_to_all | solution.py:213
  407.3 315.0 %reduce-scatter.5.cloned.1.call-start = ((), (), s32[]{:S(2)}) async-start(), calls=%async_computation.16 | async-start | bytes 5242880 | tf_op jit(solution)/shard_map/reduce_scatter | solution.py:229
  477.1 7.2 copy-start.17
  484.3 240.7 %reduce-scatter.7.cloned.1.call-start = ((), (), s32[]{:S(2)}) async-start(), calls=%async_computation.17 | async-start | bytes 5242880 | tf_op jit(solution)/shard_map/reduce_scatter | solution.py:229
  555.0 7.2 copy-start.16
  562.1 165.5 %reduce-scatter.9.cloned.1.call-start = ((), (), s32[]{:S(2)}) async-start(), calls=%async_computation.18 | async-start | bytes 5242880 | tf_op jit(solution)/shard_map/reduce_scatter | solution.py:229
  632.7 7.2 copy-start.15
  639.9 128.5 %reduce-scatter.11.cloned.1.call-start = ((), (), s32[]{:S(2)}) async-start(), calls=%async_computation.19 | async-start | bytes 5242880 | tf_op jit(solution)/shard_map/reduce_scatter | solution.py:229
  (21 other events, 64.9 us)
Sparse Core Ops, SparseCore 0:
  11.0 55.2 all-gather.4
  68.2 52.5 all-gather.6
  122.7 52.5 all-gather.8
  177.0 52.5 all-gather.10
  484.4 50.5 reduce-scatter.4
  562.3 50.5 reduce-scatter.6
  640.0 50.5 reduce-scatter.8
  717.8 50.5 reduce-scatter.10

commit v9 on v8

--- a/solution.py
+++ b/solution.py
@@ -216,8 +216,12 @@
         gathered = gathered_all[chunk]
         if results:
             gathered, _ = lax.optimization_barrier((gathered, embedded))
+        first = chunk == 0 and chunks > 1
         spec_re, spec_im = row_transform(
-            gathered[:, 0].reshape(window, width), gathered[:, 1].reshape(window, width), -1.0
+            gathered[:, 0].reshape(window, width),
+            gathered[:, 1].reshape(window, width),
+            -1.0,
+            precision=lax.Precision.HIGH if first else HIGHEST_PRECISION,
         )
         pupil_re, pupil_im = pupils[chunk]
         upd_re = pupil_re * spec_re + pupil_im * spec_im

time: 783 us -> 780 us (level)
  no operation moved by 1% of the time
where the time goes in v9:
time: 780 us; the launch traced here: 775 us
  waiting for transfers between devices  262 us (34%)
  blocking collectives  155 us (20%)
  local copies, waits for them, and re-layouts  113 us (14%)
  other arithmetic  108 us (14%)
  matrix products  97.3 us (12%)
  starting transfers between devices  20.9 us (3%)
  between operations  18.1 us (2%)
    all_to_all x3, blocking collectives, on_device(): lax.all_to_all(piece, 'row', split_axis=0, concat_axis=0, tiled=True)  155 us
    all_to_all x4, waiting for transfers between devices, on_device(): lax.all_to_all(stacked, 'row', split_axis=0, concat_axis=0, tiled=True)  132 us
    dot_general x8, matrix products, row_transform(): middle = jnp.dot(table, stacked, precision=precision)  69.3 us
    all_gather x4, waiting for transfers between devices, on_device(): regions.append(lax.all_gather(part, 'led', axis=1, tiled=True))  51.2 us
    all_to_all x1, waiting for transfers between devices, on_device(): lax.all_to_all(piece, 'row', split_axis=0, concat_axis=0, tiled=True)  39 us
    reduce_scatter x4, waiting for transfers between devices, on_device(): lax.psum_scatter(embedded, 'led', scatter_dimension=1, tiled=True)  38.1 us
    dynamic_update_slice x4, local copies, waits for them, and re-layouts, on_device(): lax.dynamic_update_slice_in_dim(embedded, jnp.stack([upd_re, upd_im]), ro...  28.4 us
    mul x1, other arithmetic, pupil_at(): return (weight * jnp.cos(phases), weight * jnp.sin(phases))  24.4 us
  transfers between devices with their start and end apart: 13, of which 8 were waited for; matrix products, arithmetic and copies ran while one was open for 29% of the time, Pallas kernels for 0%

profile of v9, /device:TPU:0, one launch (start us, length us, event | category | flops | bytes accessed | tf_op | source)
XLA Modules:
  0.0 775.1 jit_solution(12132401188396209992)
XLA Ops:
  26.8 24.4 %select_multiply_fusion = (f32[2048,512]{1,0:T(8,128)}, f32[2048,512]{1,0:T(8,128)}) fusion(f32[]{:T(128)} %bitcast.6, f32[512]{0:T(512)S(1)} %get-tuple-element.207, f32[2048]{0:T(1024)S(1)} %get-tuple-element.210, f32[512]{0:T(512)S(1)} %get-tuple-element.208, f32[2048]{0:T(1024)S(1)} %convert_multiply_fusion.1, f32[]{:T(128)} %bitcast.3, f32[]{:T(128)} %bitcast.2, ...), kind=kLoop, calls=%fused_computation.5 | loop fusion | flops 27262976 | bytes 8429584 | tf_op jit(solution)/shard_map/mul | solution.py:29
  53.3 13.0 %all-gather.5.cloned.1.call-done = f32[2,4096,128]{2,1,0:T(8,128)} async-done(((f32[2,1024,128]{2,1,0:T(8,128)}), f32[2,4096,128]{2,1,0:T(8,128)}) %all-gather.5.cloned.1.call-update) | async-done | bytes 4194320 | tf_op jit(solution)/shard_map/all_gather | solution.py:160
  70.3 8.9 %fusion.32 = f32[1024,512]{1,0:T(8,128)S(1)} fusion(f32[512,512]{1,0:T(8,128)S(1)} %reshape.412, f32[512,512]{1,0:T(8,128)} %reshape.411, f32[512,512]{1,0:T(8,128)} %get-tuple-element.212, f32[512,512]{1,0:T(8,128)S(1)} %get-tuple-element.211, f32[512,512]{1,0:T(8,128)} %fusion.81), kind=kOutput, calls=%fused_computation.39 | convolution fusion | flops 6446120960 | bytes 7340032 | tf_op jit(solution)/shard_map/dot_general | solution.py:96
  82.7 38.1 %all-gather.7.cloned.1.call-done = f32[2,4096,128]{2,1,0:T(8,128)} async-done(((f32[2,1024,128]{2,1,0:T(8,128)}), f32[2,4096,128]{2,1,0:T(8,128)}) %all-gather.7.cloned.1.call-update) | async-done | bytes 4194320 | tf_op jit(solution)/shard_map/all_gather | solution.py:160
  124.7 9.5 %fusion.36 = f32[1024,512]{1,0:T(8,128)S(1)} fusion(f32[512,512]{1,0:T(8,128)S(1)} %reshape.414, f32[512,512]{1,0:T(8,128)} %reshape.413, f32[512,512]{1,0:T(8,128)} %get-tuple-element.212, f32[512,512]{1,0:T(8,128)S(1)} %copy-done.25, f32[512,512]{1,0:T(8,128)} %fusion.81), kind=kOutput, calls=%fused_computation.44 | convolution fusion | flops 6446120960 | bytes 7340032 | tf_op jit(solution)/shard_map/dot_general | solution.py:96
  143.0 48.5 %all-to-all-done.1 = f32[8,2,256,128]{2,3,1,0:T(8,128)S(1)} async-done(((f32[8,2,256,128]{2,3,1,0:T(8,128)}), f32[8,2,256,128]{2,3,1,0:T(8,128)S(1)}, u32[]{:S(2)}, u32[]{:S(2)}) %all-to-all-start.1) | async-done | bytes 2097184 | tf_op jit(solution)/shard_map/all_to_all | solution.py:181
  201.0 9.6 %fusion.40 = f32[1024,512]{1,0:T(8,128)S(1)} fusion(f32[512,512]{1,0:T(8,128)S(1)} %reshape.416, f32[512,512]{1,0:T(8,128)S(1)} %reshape.415, f32[512,512]{1,0:T(8,128)} %get-tuple-element.212, f32[512,512]{1,0:T(8,128)} %copy-done.24, f32[512,512]{1,0:T(8,128)} %fusion.81), kind=kOutput, calls=%fused_computation.49 | convolution fusion | flops 6446120960 | bytes 7340032 | tf_op jit(solution)/shard_map/dot_general | solution.py:96
  214.3 30.5 %all-to-all-done = f32[8,2,256,128]{2,3,1,0:T(8,128)} async-done(((f32[8,2,256,128]{2,3,1,0:T(8,128)}), f32[8,2,256,128]{2,3,1,0:T(8,128)}, u32[]{:S(2)}, u32[]{:S(2)}) %all-to-all-start) | async-done | bytes 2097184 | tf_op jit(solution)/shard_map/all_to_all | solution.py:181
  271.1 26.4 %all-to-all-done.2 = f32[8,2,256,128]{2,3,1,0:T(8,128)S(1)} async-done(((f32[8,2,256,128]{2,3,1,0:T(8,128)}), f32[8,2,256,128]{2,3,1,0:T(8,128)S(1)}, u32[]{:S(2)}, u32[]{:S(2)}) %all-to-all-start.2) | async-done | bytes 2097184 | tf_op jit(solution)/shard_map/all_to_all | solution.py:181
  324.3 26.7 %all-to-all-done.3 = f32[8,2,256,128]{2,3,1,0:T(8,128)} async-done(((f32[8,2,256,128]{2,3,1,0:T(8,128)}), f32[8,2,256,128]{2,3,1,0:T(8,128)}, u32[]{:S(2)}, u32[]{:S(2)}) %all-to-all-start.3) | async-done | bytes 2097184 | tf_op jit(solution)/shard_map/all_to_all | solution.py:181
  360.8 9.5 %fusion.27 = f32[2,256,256,8,1]{1,2,3,0,4:T(8,128)S(1)} fusion(f32[2,256,256,8]{2,1,0,3:T(8,128)} %copy.89, f32[1,2,256,256]{2,3,0,1:T(8,128)S(1)} %copy-done.23, f32[1,2,256,256]{2,3,0,1:T(8,128)S(1)} %copy-done.22), kind=kOutput, calls=%fused_computation.36 | convolution fusion | flops 6442713088 | bytes 9437184 | tf_op jit(solution)/shard_map/pytr,pqtk->qykr/dot_general | solution.py:58
  384.3 9.1 %fusion.26 = f32[2,256,256,8,1]{1,2,3,0,4:T(8,128)S(1)} fusion(f32[1,256,256,8]{2,1,0,3:T(8,128)} %copy.96, f32[1,256,256,8]{2,1,0,3:T(8,128)} %copy.95, f32[1,2,256,256]{2,3,1,0:T(8,128)S(1)} %copy-done.21, f32[1,2,256,256]{2,3,1,0:T(8,128)S(1)} %copy-done.20), kind=kOutput, calls=%fused_computation.35 | convolution fusion | flops 6443761664 | bytes 9437184 | tf_op jit(solution)/shard_map/pytr,pqtk->qykr/dot_general | solution.py:58
  417.8 39.0 %all-to-all-done.4 = f32[8,2,256,128]{2,3,1,0:T(8,128)S(1)} async-done(((f32[8,2,256,128]{2,3,1,0:T(8,128)}), f32[8,2,256,128]{2,3,1,0:T(8,128)S(1)}, u32[]{:S(2)}, u32[]{:S(2)}) %all-to-all-start.4) | async-done | bytes 2097184 | tf_op jit(solution)/shard_map/all_to_all | solution.py:213
  473.9 7.1 dynamic_update_slice.24
  481.6 51.7 %all_to_all.40 = f32[8,2,256,128]{2,3,1,0:T(8,128)S(1)} all-to-all(f32[8,2,256,128]{2,3,1,0:T(8,128)S(1)} %copy.104), channel_id=1, replica_groups=mesh['led'=4,'row'=8] {'row'}, dimensions={0} | all-to-all | bytes 4194304 | tf_op jit(solution)/shard_map/all_to_all | solution.py:213
  535.5 9.7 %fusion.52 = f32[1024,512]{1,0:T(8,128)S(1)} fusion(f32[512,512]{1,0:T(8,128)S(1)} %reshape_reshape_squeeze.27, f32[512,512]{1,0:T(8,128)} %reshape_reshape_squeeze.26, f32[512,512]{1,0:T(8,128)} %get-tuple-element.218, f32[512,512]{1,0:T(8,128)} %get-tuple-element.217, f32[512,512]{1,0:T(8,128)S(1)} %copy-done.27), kind=kOutput, calls=%fused_computation.66 | convolution fusion | flops 6446120960 | bytes 7340032 | tf_op jit(solution)/shard_map/dot_general | solution.py:96
  551.9 7.1 dynamic_update_slice.26
  559.5 51.9 %all_to_all.41 = f32[8,2,256,128]{2,3,1,0:T(8,128)S(1)} all-to-all(f32[8,2,256,128]{2,3,1,0:T(8,128)S(1)} %copy.107), channel_id=1, replica_groups=mesh['led'=4,'row'=8] {'row'}, dimensions={0} | all-to-all | bytes 4194304 | tf_op jit(solution)/shard_map/all_to_all | solution.py:213
  613.6 9.7 %fusion.56 = f32[1024,512]{1,0:T(8,128)S(1)} fusion(f32[512,512]{1,0:T(8,128)S(1)} %reshape_reshape_squeeze.29, f32[512,512]{1,0:T(8,128)} %reshape_reshape_squeeze.28, f32[512,512]{1,0:T(8,128)} %get-tuple-element.218, f32[512,512]{1,0:T(8,128)} %get-tuple-element.217, f32[512,512]{1,0:T(8,128)S(1)} %copy-done.28), kind=kOutput, calls=%fused_computation.72 | convolution fusion | flops 6446120960 | bytes 7340032 | tf_op jit(solution)/shard_map/dot_general | solution.py:96
  629.9 7.1 dynamic_update_slice.28
  637.5 51.6 %all_to_all.42 = f32[8,2,256,128]{2,3,1,0:T(8,128)S(1)} all-to-all(f32[8,2,256,128]{2,3,1,0:T(8,128)S(1)} %copy.110), channel_id=1, replica_groups=mesh['led'=4,'row'=8] {'row'}, dimensions={0} | all-to-all | bytes 4194304 | tf_op jit(solution)/shard_map/all_to_all | solution.py:213
  691.3 9.7 %fusion.60 = f32[1024,512]{1,0:T(8,128)S(1)} fusion(f32[512,512]{1,0:T(8,128)S(1)} %reshape_reshape_squeeze.31, f32[512,512]{1,0:T(8,128)} %reshape_reshape_squeeze.30, f32[512,512]{1,0:T(8,128)} %get-tuple-element.218, f32[512,512]{1,0:T(8,128)} %get-tuple-element.217, f32[512,512]{1,0:T(8,128)S(1)} %copy-done.29), kind=kOutput, calls=%fused_computation.78 | convolution fusion | flops 6446120960 | bytes 7340032 | tf_op jit(solution)/shard_map/dot_general | solution.py:96
  707.7 7.0 dynamic_update_slice.30
  727.4 38.1 %reduce-scatter.11.cloned.1.call-done = f32[2,1024,128]{2,1,0:T(8,128)} async-done(((f32[2,4096,128]{2,1,0:T(8,128)}), f32[2,1024,128]{2,1,0:T(8,128)}) %reduce-scatter.11.cloned.1.call-update) | async-done | bytes 1048592 | tf_op jit(solution)/shard_map/reduce_scatter | solution.py:233
  (259 shorter events, 213.1 us)
Async XLA Ops:
  6.5 5.9 copy-start.31
  6.5 59.8 %all-gather.5.cloned.1.call-start = ((), (), s32[]{:S(2)}) async-start(), calls=%async_computation.12 | async-start | bytes 5242880 | tf_op jit(solution)/shard_map/all_gather | solution.py:160
  10.9 13.4 %copy-start.30 = (f32[6]{0:T(128)S(1)}, f32[6]{0:T(128)}, u32[]{:S(2)}) copy-start(f32[6]{0:T(128)} %param.7) | copy-start | bytes 76
  10.9 109.9 %all-gather.7.cloned.1.call-start = ((), (), s32[]{:S(2)}) async-start(), calls=%async_computation.13 | async-start | bytes 5242880 | tf_op jit(solution)/shard_map/all_gather | solution.py:160
  11.7 184.1 %all-gather.9.cloned.1.call-start = ((), (), s32[]{:S(2)}) async-start(), calls=%async_computation.14 | async-start | bytes 5242880 | tf_op jit(solution)/shard_map/all_gather | solution.py:160
  19.5 50.7 %copy-start.24 = (f32[512,512]{1,0:T(8,128)}, f32[512,512]{1,0:T(8,128)S(1)}, u32[]{:S(2)}) copy-start(f32[512,512]{1,0:T(8,128)S(1)} %get-tuple-element.211) | copy-start | bytes 3145732
  82.7 41.9 %copy-start.25 = (f32[512,512]{1,0:T(8,128)S(1)}, f32[512,512]{1,0:T(8,128)}, u32[]{:S(2)}) copy-start(f32[512,512]{1,0:T(8,128)} %copy-done.24) | copy-start | bytes 3145732
  137.8 53.6 %all-to-all-start.1 = ((f32[8,2,256,128]{2,3,1,0:T(8,128)}), f32[8,2,256,128]{2,3,1,0:T(8,128)S(1)}, u32[]{:S(2)}, u32[]{:S(2)}) async-start(f32[8,2,256,128]{2,3,1,0:T(8,128)} %pad_maximum_fusion.2), calls=%async_computation.1 | async-start | bytes 4194304 | tf_op jit(solution)/shard_map/all_to_all | solution.py:181
  142.4 106.2 %all-gather.11.cloned.1.call-start = ((), (), s32[]{:S(2)}) async-start(), calls=%async_computation.15 | async-start | bytes 5242880 | tf_op jit(solution)/shard_map/all_gather | solution.py:160
  191.4 8.0 %copy-start.11 = (f32[8,2,256,128]{2,3,1,0:T(8,128)}, f32[8,2,256,128]{2,3,1,0:T(8,128)S(1)}, u32[]{:S(2)}) copy-start(f32[8,2,256,128]{2,3,1,0:T(8,128)S(1)} %all-to-all-done.1) | copy-start | bytes 6291460
  191.4 53.4 %all-to-all-start = ((f32[8,2,256,128]{2,3,1,0:T(8,128)}), f32[8,2,256,128]{2,3,1,0:T(8,128)}, u32[]{:S(2)}, u32[]{:S(2)}) async-start(f32[8,2,256,128]{2,3,1,0:T(8,128)} %pad_maximum_fusion.1), calls=%async_computation | async-start | bytes 4194304 | tf_op jit(solution)/shard_map/all_to_all | solution.py:181
  244.8 52.7 %all-to-all-start.2 = ((f32[8,2,256,128]{2,3,1,0:T(8,128)}), f32[8,2,256,128]{2,3,1,0:T(8,128)S(1)}, u32[]{:S(2)}, u32[]{:S(2)}) async-start(f32[8,2,256,128]{2,3,1,0:T(8,128)} %pad_maximum_fusion.3), calls=%async_computation.2 | async-start | bytes 4194304 | tf_op jit(solution)/shard_map/all_to_all | solution.py:181
  297.6 53.4 %all-to-all-start.3 = ((f32[8,2,256,128]{2,3,1,0:T(8,128)}), f32[8,2,256,128]{2,3,1,0:T(8,128)}, u32[]{:S(2)}, u32[]{:S(2)}) async-start(f32[8,2,256,128]{2,3,1,0:T(8,128)} %pad_maximum_fusion.4), calls=%async_computation.3 | async-start | bytes 4194304 | tf_op jit(solution)/shard_map/all_to_all | solution.py:181
  313.4 6.3 copy-start.12
  360.8 9.5 %copy-start.9 = (f32[2,2,256,8,8]{3,4,0,1,2:T(8,128)S(1)}, f32[2,2,256,8,8]{3,4,0,1,2:T(8,128)}, u32[]{:S(2)}) copy-start(f32[2,2,256,8,8]{3,4,0,1,2:T(8,128)} %copy.90) | copy-start | bytes 786436
  384.3 9.1 %copy-start.8 = (f32[2,2,256,8,8]{3,4,0,1,2:T(8,128)S(1)}, f32[2,2,256,8,8]{3,4,0,1,2:T(8,128)}, u32[]{:S(2)}) copy-start(f32[2,2,256,8,8]{3,4,0,1,2:T(8,128)} %copy.98) | copy-start | bytes 786436
  404.1 52.6 %all-to-all-start.4 = ((f32[8,2,256,128]{2,3,1,0:T(8,128)}), f32[8,2,256,128]{2,3,1,0:T(8,128)S(1)}, u32[]{:S(2)}, u32[]{:S(2)}) async-start(f32[8,2,256,128]{2,3,1,0:T(8,128)} %copy.101), calls=%async_computation.4 | async-start | bytes 4194304 | tf_op jit(solution)/shard_map/all_to_all | solution.py:213
  407.8 311.6 %reduce-scatter.5.cloned.1.call-start = ((), (), s32[]{:S(2)}) async-start(), calls=%async_computation.16 | async-start | bytes 5242880 | tf_op jit(solution)/shard_map/reduce_scatter | solution.py:233
  473.9 7.2 copy-start.17
  481.1 241.0 %reduce-scatter.7.cloned.1.call-start = ((), (), s32[]{:S(2)}) async-start(), calls=%async_computation.17 | async-start | bytes 5242880 | tf_op jit(solution)/shard_map/reduce_scatter | solution.py:233
  551.9 7.2 copy-start.16
  559.0 165.7 %reduce-scatter.9.cloned.1.call-start = ((), (), s32[]{:S(2)}) async-start(), calls=%async_computation.18 | async-start | bytes 5242880 | tf_op jit(solution)/shard_map/reduce_scatter | solution.py:233
  629.9 7.2 copy-start.15
  637.0 128.5 %reduce-scatter.11.cloned.1.call-start = ((), (), s32[]{:S(2)}) async-start(), calls=%async_computation.19 | async-start | bytes 5242880 | tf_op jit(solution)/shard_map/reduce_scatter | solution.py:233
  (21 other events, 64.9 us)
Sparse Core Ops, SparseCore 0:
  11.0 55.2 all-gather.4
  68.2 52.5 all-gather.6
  122.7 52.5 all-gather.8
  177.0 52.5 all-gather.10
  481.2 50.5 reduce-scatter.4
  559.1 50.5 reduce-scatter.6
  637.1 50.5 reduce-scatter.8
  714.8 50.6 reduce-scatter.10
